TPU v7x, 128 devices: a whole 4x4x4 slice. The times are simulated.
128 devices in a mesh: blk: 32 (over z, y, core), head: 4 (over x).
Axes of the slice: x: 4, y: 4, z: 4, core: 2. Of those that a mesh axis runs over, the one named last changes fastest.
Arguments:
- query_rows: bfloat16 [32768, 1024], P(('blk', 'head')), may hold values from -8 to 8
- key_rows: bfloat16 [32768, 1024], P(('blk', 'head')), may hold values from -8 to 8
- value_rows: bfloat16 [32768, 1024], P(('blk', 'head')), may hold values from -6 to 6
- out_grad: bfloat16 [32768, 1024], P(('blk', 'head')), may hold values from -6 to 6
- expander_device: int32 [256, 4], P('blk'), may hold values from 0 to 31, all different within a row; in each aligned block of 8 rows (0 to 7, 8 to 15, ...) at most 2 rows name the same one
- expander_block: int32 [256, 4], P('blk'), may hold values from 0 to 7
- local_offset: int32 [256, 11], P('blk'), may hold values from -4 to 4
- live_count: int32 [256], P('blk'), may hold values from 3 to 4
- drop_seed: int32 [16, 256, 16], P('head', 'blk'), may hold values from 0 to 1048575
Outputs:
- attended: bfloat16 [32768, 1024], P(('blk', 'head'))
- query_grad: bfloat16 [32768, 1024], P(('blk', 'head'))
- key_grad: bfloat16 [32768, 1024], P(('blk', 'head'))
- value_grad: bfloat16 [32768, 1024], P(('blk', 'head'))
Inputs may be any that keep to these rules, and one draw needn't show every extreme that they name: `expander_device`: each row names 4 different devices. Among the rows of one device (aligned blocks of 8 rows), no device is named by more than 2 rows, and in every draw some device is named exactly 2 times by one device's rows.
All inputs are finite; a program needn't handle non-finite values.
Results may differ from a plain program's by a relative error of at most 0.012.
Values may be sent and summed in bfloat16 or wider, within the bound.
No kernel may reach another device: no remote copies, remote signals or barrier semaphores. Data moves between devices by JAX's collectives and lax.ppermute only.
A program may use at most 128 MiB of HBM per device.

v0:
```python
import jax
import jax.numpy as jnp
from jax import lax
from jax.sharding import PartitionSpec as P

BS = 128
QB_DEV = 8
L = 11
E = 4
W = 4


KEEP_LEVEL = 102
KEEP_GAIN = 1024.0 / 922.0
MASKED = -1e30


def padded(block, sides, width):
    for axis, dim in sides:
        count = lax.axis_size(axis)
        forward = [(i, i + 1) for i in range(count - 1)]
        forward.append((count - 1, 0))
        backward = [(target, source) for source, target in forward]
        low = lax.ppermute(
            lax.slice_in_dim(block, block.shape[dim] - width, None, axis=dim), axis, forward
        )
        high = lax.ppermute(lax.slice_in_dim(block, 0, width, axis=dim), axis, backward)
        block = jnp.concatenate([low, block, high], axis=dim)
    return block


def shifted(block, axis, distance):
    devices = range(lax.axis_size(axis))
    route = [((i - distance) % len(devices), i) for i in devices]
    return lax.ppermute(block, axis, route)


def logical_right(value, amount):
    return lax.shift_right_logical(value, jnp.full(value.shape, amount, jnp.int32))


def keep_weights(seed_row, block_size):
    row_index = jnp.arange(block_size, dtype=jnp.int32)[:, None, None]
    col_index = jnp.arange(block_size, dtype=jnp.int32)[None, None, :]
    offset = row_index * block_size + col_index
    hashed = seed_row[:, None, :, None] * 40503 + offset[None]
    hashed = hashed ^ logical_right(hashed, 15)
    hashed = hashed * 739982445
    hashed = hashed ^ logical_right(hashed, 12)
    hashed = hashed * 695872825
    hashed = hashed ^ logical_right(hashed, 15)
    keep_scale = jnp.where(hashed & 1023 >= KEEP_LEVEL, KEEP_GAIN, 0.0).astype(jnp.float32)
    return keep_scale.reshape(seed_row.shape[0], block_size, -1)


def on_device(
    query_rows,
    key_rows,
    value_rows,
    out_grad,
    expander_device,
    expander_block,
    local_offset,
    live_count,
    drop_seed,
):
    head_count = lax.axis_size("head")
    head_index = lax.axis_index("head")
    share_rows = query_rows.shape[0]
    local_width = query_rows.shape[1] // head_count
    local_heads = drop_seed.shape[0]
    head_size = local_width // local_heads
    score_scale = head_size ** (-0.5)
    slot_count = 1 + L + E
    gathered = (
        lax.all_gather(query_rows, "head", axis=0, tiled=True),
        lax.all_gather(key_rows, "head", axis=0, tiled=True),
        lax.all_gather(value_rows, "head", axis=0, tiled=True),
        lax.all_gather(out_grad, "head", axis=0, tiled=True),
    )
    first_col = head_index * local_width
    query_local, key_local, value_local, grad_local = [
        lax.dynamic_slice_in_dim(member, first_col, local_width, 1) for member in gathered
    ]
    peer_count = lax.axis_size("blk")
    capacity = min(QB_DEV, max(2, (2 * QB_DEV * E + peer_count - 1) // peer_count))
    flat_device = expander_device.reshape(-1)
    matches = (flat_device[:, None] == jnp.arange(peer_count, dtype=jnp.int32)[None, :]).astype(
        jnp.int32
    )
    before = jnp.cumsum(matches, axis=0) - matches
    slot_rank = jnp.sum(before * matches, axis=1)
    far_position = flat_device * capacity + slot_rank
    far_live = jnp.arange(E, dtype=jnp.int32)[None, :] < live_count[:, None]
    asked_block = jnp.where(far_live, expander_block, -1)
    wanted = (
        jnp.full((peer_count * capacity,), -1, jnp.int32)
        .at[far_position]
        .set(asked_block.reshape(-1))
    )
    wanted_here = lax.all_to_all(
        wanted.reshape(peer_count, capacity), "blk", split_axis=0, concat_axis=0, tiled=True
    )
    key_blocks = key_local.reshape(QB_DEV, BS, local_width)
    value_blocks = value_local.reshape(QB_DEV, BS, local_width)
    stacked = jnp.stack([key_blocks, value_blocks], axis=1)
    widened = padded(stacked, (("blk", 0),), W)
    wanted_flat = wanted_here.reshape(-1)
    chosen = jnp.clip(wanted_flat, 0, QB_DEV - 1)
    asked_mask = (wanted_flat >= 0)[:, None, None]
    zero_block = jnp.zeros((), jnp.bfloat16)
    reply_shape = (peer_count, capacity, BS, local_width)
    far_key, far_value = (
        lax.all_to_all(
            jnp.where(asked_mask, key_blocks[chosen], zero_block).reshape(reply_shape),
            "blk",
            split_axis=0,
            concat_axis=0,
            tiled=True,
        ),
        lax.all_to_all(
            jnp.where(asked_mask, value_blocks[chosen], zero_block).reshape(reply_shape),
            "blk",
            split_axis=0,
            concat_axis=0,
            tiled=True,
        ),
    )
    near_count = QB_DEV + 2 * W
    far_total_count = peer_count * capacity
    key_table = jnp.concatenate(
        [widened[:, 0], far_key.reshape(far_total_count, BS, local_width)], axis=0
    )
    value_table = jnp.concatenate(
        [widened[:, 1], far_value.reshape(far_total_count, BS, local_width)], axis=0
    )
    local_block = jnp.arange(QB_DEV, dtype=jnp.int32)[:, None]
    self_slot = local_block + W
    near_slot = local_block + W + local_offset
    far_slot = near_count + far_position.reshape(QB_DEV, E)
    table_rows = jnp.concatenate([self_slot, near_slot, far_slot], axis=1)
    slot_number = jnp.arange(slot_count, dtype=jnp.int32)[None, :]
    live_slots = (slot_number <= L) | (slot_number - 1 - L < live_count[:, None])
    seed_rows = jnp.transpose(drop_seed, (1, 0, 2))
    query_grid = query_local.reshape(QB_DEV, BS, local_heads, head_size)
    grad_grid = grad_local.reshape(QB_DEV, BS, local_heads, head_size)

    def block_step(running, inputs):
        near_total, far_key_total, far_value_total = running
        query_block, grad_block, slot_row, live_row, seed_row = inputs
        key_block = key_table[slot_row].reshape(slot_count * BS, local_heads, head_size)
        value_block = value_table[slot_row].reshape(slot_count * BS, local_heads, head_size)
        live_keys = jnp.repeat(live_row, BS)
        keep_scale = keep_weights(seed_row, BS)
        scores = (
            jnp.einsum("qhd,khd->hqk", query_block, key_block, preferred_element_type=jnp.float32)
            * score_scale
        )
        scores = jnp.where(live_keys[None, None, :], scores, MASKED)
        largest = jnp.max(scores, axis=-1, keepdims=True)
        expterm = jnp.exp(scores - largest)
        attention = expterm / jnp.sum(expterm, axis=-1, keepdims=True)
        dropped = (attention * keep_scale).astype(jnp.bfloat16)
        attended_full = jnp.einsum(
            "hqk,khd->qhd", dropped, value_block, preferred_element_type=jnp.float32
        )
        row_delta = jnp.einsum("qhd,qhd->hq", grad_block.astype(jnp.float32), attended_full)
        drop_grad = jnp.einsum(
            "qhd,khd->hqk", grad_block, value_block, preferred_element_type=jnp.float32
        )
        score_grad = (
            attention * (drop_grad * keep_scale - row_delta[:, :, None]) * score_scale
        ).astype(jnp.bfloat16)
        query_block_grad = jnp.einsum(
            "hqk,khd->qhd", score_grad, key_block, preferred_element_type=jnp.float32
        )
        key_part = jnp.einsum(
            "hqk,qhd->khd", score_grad, query_block, preferred_element_type=jnp.float32
        )
        value_part = jnp.einsum(
            "hqk,qhd->khd", dropped, grad_block, preferred_element_type=jnp.float32
        )
        key_part = key_part.reshape(slot_count, BS, local_width)
        value_part = value_part.reshape(slot_count, BS, local_width)
        near_rows = slot_row[: L + 1]
        near_total = near_total.at[near_rows, 0].add(key_part[: L + 1])
        near_total = near_total.at[near_rows, 1].add(value_part[: L + 1])
        far_rows = slot_row[L + 1 :] - near_count
        far_key_total = far_key_total.at[far_rows].set(key_part[L + 1 :].astype(jnp.bfloat16))
        far_value_total = far_value_total.at[far_rows].set(value_part[L + 1 :].astype(jnp.bfloat16))
        return (
            (near_total, far_key_total, far_value_total),
            (attended_full.astype(jnp.bfloat16), query_block_grad.astype(jnp.bfloat16)),
        )

    start_totals = (
        jnp.zeros((near_count, 2, BS, local_width), jnp.float32),
        jnp.zeros((far_total_count, BS, local_width), jnp.bfloat16),
        jnp.zeros((far_total_count, BS, local_width), jnp.bfloat16),
    )
    totals, outputs = lax.scan(
        block_step, start_totals, (query_grid, grad_grid, table_rows, live_slots, seed_rows)
    )
    near_total, far_key_total, far_value_total = totals
    back_key, back_value = (
        lax.all_to_all(
            far_key_total.reshape(reply_shape), "blk", split_axis=0, concat_axis=0, tiled=True
        ),
        lax.all_to_all(
            far_value_total.reshape(reply_shape), "blk", split_axis=0, concat_axis=0, tiled=True
        ),
    )
    owner_match = (
        jnp.arange(QB_DEV, dtype=jnp.int32)[:, None] == wanted_here.reshape(1, -1)
    ).astype(jnp.bfloat16)
    far_key_sum = jnp.dot(
        owner_match,
        back_key.reshape(far_total_count, BS * local_width),
        preferred_element_type=jnp.float32,
    )
    far_value_sum = jnp.dot(
        owner_match,
        back_value.reshape(far_total_count, BS * local_width),
        preferred_element_type=jnp.float32,
    )
    from_below = shifted(near_total[QB_DEV + W :].astype(jnp.bfloat16), "blk", 1).astype(
        jnp.float32
    )
    from_above = shifted(near_total[:W].astype(jnp.bfloat16), "blk", -1).astype(jnp.float32)
    own_total = near_total[W : W + QB_DEV]
    own_total = own_total.at[:W].add(from_below)
    own_total = own_total.at[QB_DEV - W :].add(from_above)
    block_rows = QB_DEV * BS
    key_grad = (own_total[:, 0].reshape(QB_DEV, BS * local_width) + far_key_sum).astype(
        jnp.bfloat16
    )
    value_grad = (own_total[:, 1].reshape(QB_DEV, BS * local_width) + far_value_sum).astype(
        jnp.bfloat16
    )
    results = (
        outputs[0].reshape(block_rows, local_width),
        outputs[1].reshape(block_rows, local_width),
        key_grad.reshape(block_rows, local_width),
        value_grad.reshape(block_rows, local_width),
    )
    full_results = (
        lax.all_gather(results[0], "head", axis=1, tiled=True),
        lax.all_gather(results[1], "head", axis=1, tiled=True),
        lax.all_gather(results[2], "head", axis=1, tiled=True),
        lax.all_gather(results[3], "head", axis=1, tiled=True),
    )
    first_row = head_index * share_rows
    return tuple(
        (lax.dynamic_slice_in_dim(member, first_row, share_rows, 0) for member in full_results)
    )


def solution(mesh):
    in_specs = (
        P(("blk", "head"), None),
        P(("blk", "head"), None),
        P(("blk", "head"), None),
        P(("blk", "head"), None),
        P("blk", None),
        P("blk", None),
        P("blk", None),
        P("blk"),
        P("head", "blk", None),
    )
    out_specs = (
        P(("blk", "head"), None),
        P(("blk", "head"), None),
        P(("blk", "head"), None),
        P(("blk", "head"), None),
    )
    return jax.shard_map(
        on_device, mesh=mesh, in_specs=in_specs, out_specs=out_specs, check_vma=False
    )
```

profile of v0, /device:TPU:8, one launch (start us, length us, event | category | flops | bytes accessed | tf_op | source)
XLA Modules:
  0.0 829.0 jit_solution(16487344106228774958)
XLA Ops:
  12.2 8.5 %all-to-all-start = ((s32[32,1,2]{2,1,0:T(1,128)}), s32[32,1,2]{2,1,0:T(1,128)S(1)}, u32[]{:S(2)}, u32[]{:S(2)}) async-start(s32[32,1,2]{2,1,0:T(1,128)} %bitcast.28), calls=%async_computation | async-start | bytes 32768 | tf_op jit(solution)/shard_map/all_to_all | solution.py:101
  20.8 6.1 all-to-all-done
  29.1 13.7 %all-gather.13.cloned.1.call-done = bf16[1024,1024]{1,0:T(8,128)(2,1)} async-done(((bf16[256,1024]{1,0:T(8,128)(2,1)}), bf16[1024,1024]{1,0:T(8,128)(2,1)}) %all-gather.13.cloned.1.call-update) | async-done | bytes 2097168 | tf_op jit(solution)/shard_map/all_gather | solution.py:78
  46.7 28.5 %all-gather.11.cloned.1.call-done = bf16[1024,1024]{1,0:T(8,128)(2,1)} async-done(((bf16[256,1024]{1,0:T(8,128)(2,1)}), bf16[1024,1024]{1,0:T(8,128)(2,1)}) %all-gather.11.cloned.1.call-update) | async-done | bytes 2097168 | tf_op jit(solution)/shard_map/all_gather | solution.py:77
  79.1 5.9 broadcast_select_fusion
  85.0 7.6 all-to-all-start.2
  93.3 50.7 %all-to-all-done.2 = bf16[32,2,128,256]{3,2,1,0:T(8,128)(2,1)} async-done(((bf16[32,2,128,256]{3,2,1,0:T(8,128)(2,1)}), bf16[32,2,128,256]{3,2,1,0:T(8,128)(2,1)}, u32[]{:S(2)}, u32[]{:S(2)}) %all-to-all-start.2) | async-done | bytes 4194336 | tf_op jit(solution)/shard_map/all_to_all | solution.py:121
  144.0 7.4 all-to-all-start.1
  155.2 29.2 %all-gather.15.cloned.1.call-done = bf16[1024,1024]{1,0:T(8,128)(2,1)} async-done(((bf16[256,1024]{1,0:T(8,128)(2,1)}), bf16[1024,1024]{1,0:T(8,128)(2,1)}) %all-gather.15.cloned.1.call-update) | async-done | bytes 2097168 | tf_op jit(solution)/shard_map/all_gather | solution.py:79
  188.9 16.8 %collective-permute-done = bf16[4,2,128,256]{3,2,0,1:T(8,128)(2,1)} collective-permute-done((bf16[4,2,128,256]{3,2,0,1:T(8,128)(2,1)}, bf16[4,2,128,256]{3,2,0,1:T(8,128)(2,1)}, u32[]{:S(2)}, u32[]{:S(2)}) %collective-permute-start) | collective-permute-done | bytes 524320 | tf_op jit(solution)/shard_map/ppermute | solution.py:24
  207.3 5.0 pad_maximum_fusion.1
  212.3 5.0 pad_maximum_fusion
  224.9 435.0 %while.24 = (s32[]{:T(128)}, f32[16,2,128,256]{3,2,1,0:T(8,128)}, bf16[64,128,256]{2,1,0:T(8,128)(2,1)}, bf16[64,128,256]{2,1,0:T(8,128)(2,1)}, bf16[8,128,4,64]...) while((s32[]{:T(128)}, f32[16,2,128,256]{3,2,1,0:T(8,128)}, ...), condition=%wide.region_10.11_spmd, body=%wide.region_3.10_spmd.sunk | while | flops 845073280 | bytes 125162392 | solution.py:201
  266.3 4.6 scatter_fusion
  320.7 4.5 scatter_fusion
  375.0 4.5 scatter_fusion
  401.3 4.3 fusion.106
  429.5 4.5 scatter_fusion
  455.5 4.3 fusion.106
  483.6 4.6 scatter_fusion
  510.1 4.3 fusion.106
  538.2 4.5 scatter_fusion
  564.5 4.3 fusion.106
  592.6 4.5 scatter_fusion
  646.9 4.6 scatter_fusion
  662.2 9.3 %all-to-all-start.4 = ((bf16[32,2,128,256]{3,2,1,0:T(8,128)(2,1)}), bf16[32,2,128,256]{3,2,1,0:T(8,128)(2,1)}, u32[]{:S(2)}, u32[]{:S(2)}) async-start(bf16[32,2,128,256]{3,2,1,0:T(8,128)(2,1)} %bitcast.235), calls=%async_computation.4 | async-start | bytes 8388608 | tf_op jit(solution)/shard_map/all_to_all | solution.py:209
  677.5 45.6 %all-to-all-done.4 = bf16[32,2,128,256]{3,2,1,0:T(8,128)(2,1)} async-done(((bf16[32,2,128,256]{3,2,1,0:T(8,128)(2,1)}), bf16[32,2,128,256]{3,2,1,0:T(8,128)(2,1)}, u32[]{:S(2)}, u32[]{:S(2)}) %all-to-all-start.4) | async-done | bytes 4194336 | tf_op jit(solution)/shard_map/all_to_all | solution.py:209
  723.0 7.6 all-to-all-start.3
  734.9 4.7 copy.88
  742.3 39.8 %all-to-all-done.3 = bf16[32,2,128,256]{3,2,1,0:T(8,128)(2,1)} async-done(((bf16[32,2,128,256]{3,2,1,0:T(8,128)(2,1)}), bf16[32,2,128,256]{3,2,1,0:T(8,128)(2,1)}, u32[]{:S(2)}, u32[]{:S(2)}) %all-to-all-start.3) | async-done | bytes 4194336 | tf_op jit(solution)/shard_map/all_to_all | solution.py:206
  782.2 4.7 copy.86
  794.8 25.5 %all-gather.21.cloned.1.call-done = bf16[1024,1024]{1,0:T(8,128)(2,1)} async-done(((bf16[1024,256]{1,0:T(8,128)(2,1)}), bf16[1024,1024]{1,0:T(8,128)(2,1)}) %all-gather.21.cloned.1.call-update) | async-done | bytes 2097168 | tf_op jit(solution)/shard_map/all_gather | solution.py:249
  (536 shorter events, 437.6 us)
Async XLA Ops:
  7.2 35.6 %all-gather.13.cloned.1.call-start = ((), (), s32[]{:S(2)}) async-start(), calls=%async_computation.7 | async-start | bytes 2621440 | tf_op jit(solution)/shard_map/all_gather | solution.py:78
  7.9 67.3 %all-gather.11.cloned.1.call-start = ((), (), s32[]{:S(2)}) async-start(), calls=%async_computation.6 | async-start | bytes 2621440 | tf_op jit(solution)/shard_map/all_gather | solution.py:77
  12.2 14.7 %all-to-all-start = ((s32[32,1,2]{2,1,0:T(1,128)}), s32[32,1,2]{2,1,0:T(1,128)S(1)}, u32[]{:S(2)}, u32[]{:S(2)}) async-start(s32[32,1,2]{2,1,0:T(1,128)} %bitcast.28), calls=%async_computation | async-start | bytes 32768 | tf_op jit(solution)/shard_map/all_to_all | solution.py:101
  85.0 59.1 %all-to-all-start.2 = ((bf16[32,2,128,256]{3,2,1,0:T(8,128)(2,1)}), bf16[32,2,128,256]{3,2,1,0:T(8,128)(2,1)}, u32[]{:S(2)}, u32[]{:S(2)}) async-start(bf16[32,2,128,256]{3,2,1,0:T(8,128)(2,1)} %get-tuple-element.370), calls=%async_computation.2 | async-start | bytes 8388608 | tf_op jit(solution)/shard_map/all_to_all | solution.py:121
  92.6 62.6 %all-gather.9.cloned.1.call-start = ((), (), s32[]{:S(2)}) async-start(), calls=%async_computation.5 | async-start | bytes 2621440 | tf_op jit(solution)/shard_map/all_gather | solution.py:76
  144.0 8.1 copy-start.9
  144.0 11.0 %copy-start.8 = (s32[4,8,16]{2,1,0:T(8,128)S(1)}, s32[4,8,16]{2,1,0:T(8,128)}, u32[]{:S(2)}) copy-start(s32[4,8,16]{2,1,0:T(8,128)} %param.23) | copy-start | bytes 6148
  144.0 11.1 %copy-start.10 = (s32[8]{0:T(128)S(1)}, s32[8]{0:T(128)}, u32[]{:S(2)}) copy-start(s32[8]{0:T(128)} %param.22) | copy-start | bytes 100
  144.0 68.3 %all-to-all-start.1 = ((bf16[32,2,128,256]{3,2,1,0:T(8,128)(2,1)}), bf16[32,2,128,256]{3,2,1,0:T(8,128)(2,1)}, u32[]{:S(2)}, u32[]{:S(2)}) async-start(bf16[32,2,128,256]{3,2,1,0:T(8,128)(2,1)} %get-tuple-element.371), calls=%async_computation.1 | async-start | bytes 8388608 | tf_op jit(solution)/shard_map/all_to_all | solution.py:114
  151.5 32.9 %all-gather.15.cloned.1.call-start = ((), (), s32[]{:S(2)}) async-start(), calls=%async_computation.8 | async-start | bytes 2621440 | tf_op jit(solution)/shard_map/all_gather | solution.py:79
  152.0 636.7 %all-gather.19.cloned.1.call-start = ((), (), s32[]{:S(2)}) async-start(), calls=%async_computation.10 | async-start | bytes 2621440 | tf_op jit(solution)/shard_map/all_gather | solution.py:248
  153.3 52.4 %collective-permute-start = (bf16[4,2,128,256]{3,2,0,1:T(8,128)(2,1)}, bf16[4,2,128,256]{3,2,0,1:T(8,128)(2,1)}, u32[]{:S(2)}, u32[]{:S(2)}) collective-permute-start(bf16[4,2,128,256]{3,2,0,1:T(8,128)(2,1)} %get-tuple-element.368), channel_id=1, source_target_pairs={{0,4},{4,8},{8,12},{12,16},{16,20},{20,24},{24,28},{28,32},{32,36}... | collective-permute-start | bytes 1572872 | tf_op jit(solution)/shard_map/ppermute | solution.py:24
  153.4 52.3 %collective-permute-start.1 = (bf16[4,2,128,256]{3,2,0,1:T(8,128)(2,1)}, bf16[4,2,128,256]{3,2,0,1:T(8,128)(2,1)}, u32[]{:S(2)}, u32[]{:S(2)}) collective-permute-start(bf16[4,2,128,256]{3,2,0,1:T(8,128)(2,1)} %get-tuple-element.369), channel_id=1, source_target_pairs={{4,0},{8,4},{12,8},{16,12},{20,16},{24,20},{28,24},{32,28},{36,32}... | collective-permute-start | bytes 1572872 | tf_op jit(solution)/shard_map/ppermute | solution.py:27
  231.3 11.1 %copy-start.2 = (bf16[2048,4,64]{0,2,1:T(8,128)(2,1)}, bf16[2048,4,64]{0,2,1:T(8,128)(2,1)S(1)}, u32[]{:S(2)}) copy-start(bf16[2048,4,64]{0,2,1:T(8,128)(2,1)S(1)} %reshape.600) | copy-start | bytes 3145732 | tf_op jit(solution)/shard_map/while
  285.7 11.1 %copy-start.2 = (bf16[2048,4,64]{0,2,1:T(8,128)(2,1)}, bf16[2048,4,64]{0,2,1:T(8,128)(2,1)S(1)}, u32[]{:S(2)}) copy-start(bf16[2048,4,64]{0,2,1:T(8,128)(2,1)S(1)} %reshape.600) | copy-start | bytes 3145732 | tf_op jit(solution)/shard_map/while
  340.1 11.1 %copy-start.2 = (bf16[2048,4,64]{0,2,1:T(8,128)(2,1)}, bf16[2048,4,64]{0,2,1:T(8,128)(2,1)S(1)}, u32[]{:S(2)}) copy-start(bf16[2048,4,64]{0,2,1:T(8,128)(2,1)S(1)} %reshape.600) | copy-start | bytes 3145732 | tf_op jit(solution)/shard_map/while
  394.5 11.2 %copy-start.2 = (bf16[2048,4,64]{0,2,1:T(8,128)(2,1)}, bf16[2048,4,64]{0,2,1:T(8,128)(2,1)S(1)}, u32[]{:S(2)}) copy-start(bf16[2048,4,64]{0,2,1:T(8,128)(2,1)S(1)} %reshape.600) | copy-start | bytes 3145732 | tf_op jit(solution)/shard_map/while
  448.7 11.2 %copy-start.2 = (bf16[2048,4,64]{0,2,1:T(8,128)(2,1)}, bf16[2048,4,64]{0,2,1:T(8,128)(2,1)S(1)}, u32[]{:S(2)}) copy-start(bf16[2048,4,64]{0,2,1:T(8,128)(2,1)S(1)} %reshape.600) | copy-start | bytes 3145732 | tf_op jit(solution)/shard_map/while
  483.6 4.6 copy-start
  503.3 11.2 %copy-start.2 = (bf16[2048,4,64]{0,2,1:T(8,128)(2,1)}, bf16[2048,4,64]{0,2,1:T(8,128)(2,1)S(1)}, u32[]{:S(2)}) copy-start(bf16[2048,4,64]{0,2,1:T(8,128)(2,1)S(1)} %reshape.600) | copy-start | bytes 3145732 | tf_op jit(solution)/shard_map/while
  557.7 11.2 %copy-start.2 = (bf16[2048,4,64]{0,2,1:T(8,128)(2,1)}, bf16[2048,4,64]{0,2,1:T(8,128)(2,1)S(1)}, u32[]{:S(2)}) copy-start(bf16[2048,4,64]{0,2,1:T(8,128)(2,1)S(1)} %reshape.600) | copy-start | bytes 3145732 | tf_op jit(solution)/shard_map/while
  611.9 11.1 %copy-start.2 = (bf16[2048,4,64]{0,2,1:T(8,128)(2,1)}, bf16[2048,4,64]{0,2,1:T(8,128)(2,1)S(1)}, u32[]{:S(2)}) copy-start(bf16[2048,4,64]{0,2,1:T(8,128)(2,1)S(1)} %reshape.600) | copy-start | bytes 3145732 | tf_op jit(solution)/shard_map/while
  646.9 4.6 copy-start
  662.2 9.4 %copy-start.6 = (bf16[8,128,4,64]{1,3,2,0:T(8,128)(2,1)S(1)}, bf16[8,128,4,64]{1,3,2,0:T(8,128)(2,1)}, u32[]{:S(2)}) copy-start(bf16[8,128,4,64]{1,3,2,0:T(8,128)(2,1)} %get-tuple-element.287) | copy-start | bytes 1572868
  662.2 60.8 %all-to-all-start.4 = ((bf16[32,2,128,256]{3,2,1,0:T(8,128)(2,1)}), bf16[32,2,128,256]{3,2,1,0:T(8,128)(2,1)}, u32[]{:S(2)}, u32[]{:S(2)}) async-start(bf16[32,2,128,256]{3,2,1,0:T(8,128)(2,1)} %bitcast.235), calls=%async_computation.4 | async-start | bytes 8388608 | tf_op jit(solution)/shard_map/all_to_all | solution.py:209
  671.5 119.3 %all-gather.17.cloned.1.call-start = ((), (), s32[]{:S(2)}) async-start(), calls=%async_computation.9 | async-start | bytes 2621440 | tf_op jit(solution)/shard_map/all_gather | solution.py:247
  675.7 56.9 %collective-permute-start.2 = (bf16[4,2,128,256]{3,2,1,0:T(8,128)(2,1)S(1)}, bf16[4,2,128,256]{3,2,1,0:T(8,128)(2,1)S(1)}, u32[]{:S(2)}, u32[]{:S(2)}) collective-permute-start(bf16[4,2,128,256]{3,2,1,0:T(8,128)(2,1)S(1)} %get-tuple-element.365), channel_id=1, source_target_pairs={{124,0},{0,4},{4,8},{8,12},{12,16},{16,20},{20,24},{24,28},{28,32}... | collective-permute-start | bytes 1572872 | tf_op jit(solution)/shard_map/ppermute | solution.py:35
  675.8 58.1 %collective-permute-start.3 = (bf16[4,2,128,256]{3,2,1,0:T(8,128)(2,1)S(1)}, bf16[4,2,128,256]{3,2,1,0:T(8,128)(2,1)S(1)}, u32[]{:S(2)}, u32[]{:S(2)}) collective-permute-start(bf16[4,2,128,256]{3,2,1,0:T(8,128)(2,1)S(1)} %get-tuple-element.364), channel_id=1, source_target_pairs={{4,0},{8,4},{12,8},{16,12},{20,16},{24,20},{28,24},{32,28},{36,32}... | collective-permute-start | bytes 1572872 | tf_op jit(solution)/shard_map/ppermute | solution.py:35
  723.0 7.7 copy-start.7
  723.0 59.1 %all-to-all-start.3 = ((bf16[32,2,128,256]{3,2,1,0:T(8,128)(2,1)}), bf16[32,2,128,256]{3,2,1,0:T(8,128)(2,1)}, u32[]{:S(2)}, u32[]{:S(2)}) async-start(bf16[32,2,128,256]{3,2,1,0:T(8,128)(2,1)} %bitcast.236), calls=%async_computation.3 | async-start | bytes 8388608 | tf_op jit(solution)/shard_map/all_to_all | solution.py:206
  730.6 62.3 %all-gather.23.cloned.1.call-start = ((), (), s32[]{:S(2)}) async-start(), calls=%async_computation.12 | async-start | bytes 2621440 | tf_op jit(solution)/shard_map/all_gather | solution.py:250
  741.4 78.8 %all-gather.21.cloned.1.call-start = ((), (), s32[]{:S(2)}) async-start(), calls=%async_computation.11 | async-start | bytes 2621440 | tf_op jit(solution)/shard_map/all_gather | solution.py:249
  (38 other events, 142.9 us)
Sparse Core Ops, SparseCore 0:
  9.6 33.0 all-gather.12
  44.4 30.7 all-gather.10
  95.1 30.5 all-gather.8
  153.6 30.6 all-gather.14
  662.3 32.2 all-gather.18
  696.7 30.7 all-gather.16
  741.5 33.8 all-gather.22
  788.8 31.3 all-gather.20
where the time goes:
time: 834 us; the launch traced here: 829 us
  local copies, waits for them, and re-layouts  272 us (33%)
  waiting for transfers between devices  258 us (31%)
  other arithmetic  124 us (15%)
  matrix products  113 us (14%)
  starting transfers between devices  44.6 us (5%)
  between operations  14.4 us (2%)
    all_to_all x1, waiting for transfers between devices, on_device(): lax.all_to_all(jnp.where(asked_mask, value_blocks[chosen], zero_block).re...  50.7 us
    all_to_all x1, waiting for transfers between devices, on_device(): lax.all_to_all(far_value_total.reshape(reply_shape), 'blk', split_axis=0,...  45.6 us
    gather x16, local copies, waits for them, and re-layouts, block_step(): value_table[slot_row].reshape(slot_count * BS, local_heads, head_size)  42.2 us
    all_to_all x1, waiting for transfers between devices, on_device(): lax.all_to_all(far_key_total.reshape(reply_shape), 'blk', split_axis=0, c...  39.8 us
    slice x24, local copies, waits for them, and re-layouts, block_step(): near_total = near_total.at[near_rows, 0].add(key_part[:L + 1])  37.1 us
    scatter-add x8, other arithmetic, block_step(): near_total = near_total.at[near_rows, 0].add(key_part[:L + 1])  36.2 us
    slice x24, local copies, waits for them, and re-layouts, block_step(): near_total = near_total.at[near_rows, 1].add(value_part[:L + 1])  35.8 us
    sub x8, matrix products, block_step(): expterm = jnp.exp(scores - largest)  34.6 us
  transfers between devices with their start and end apart: 17, of which 9 were waited for; matrix products, arithmetic and copies ran while one was open for 6% of the time, Pallas kernels for 0%

commit v1 on v0

--- a/solution.py
+++ b/solution.py
@@ -1,6 +1,10 @@
+import functools
+
 import jax
 import jax.numpy as jnp
 from jax import lax
+from jax.experimental import pallas as pl
+from jax.experimental.pallas import tpu as pltpu
 from jax.sharding import PartitionSpec as P
 
 BS = 128
@@ -51,6 +55,160 @@
     hashed = hashed ^ logical_right(hashed, 15)
     keep_scale = jnp.where(hashed & 1023 >= KEEP_LEVEL, KEEP_GAIN, 0.0).astype(jnp.float32)
     return keep_scale.reshape(seed_row.shape[0], block_size, -1)
+
+
+def srl(value, amount):
+    return lax.shift_right_logical(value, jnp.full(value.shape, amount, jnp.int32))
+
+
+def attention_kernel(
+    rows_ref, live_ref, seed_ref, q_ref, g_ref, kt_ref, vt_ref,
+    att_ref, qg_ref, nk_ref, nv_ref, fk_ref, fv_ref,
+    s_scr, keep_scr, drop_scr,
+    *, scale, near_count, slot_count, blocks,
+):
+    h = pl.program_id(0)
+    c = pl.program_id(1)
+    head_size = q_ref.shape[-1]
+
+    @pl.when(c == 0)
+    def _():
+        nk_ref[...] = jnp.zeros_like(nk_ref)
+        nv_ref[...] = jnp.zeros_like(nv_ref)
+        fk_ref[...] = jnp.zeros_like(fk_ref)
+        fv_ref[...] = jnp.zeros_like(fv_ref)
+
+    q = q_ref[0]
+    g = g_ref[0]
+    base = c * slot_count
+    seed_base = (h * blocks + c) * slot_count
+
+    def start_of(j):
+        return pl.multiple_of(rows_ref[base + j] * BS, BS)
+
+    def keys(j):
+        return kt_ref[0, pl.ds(start_of(j), BS), :]
+
+    def values(j):
+        return vt_ref[0, pl.ds(start_of(j), BS), :]
+
+    def score_pass(j, m):
+        s = lax.dot_general(
+            q, keys(j), (((1,), (1,)), ((), ())), preferred_element_type=jnp.float32
+        ) * scale
+        s = jnp.where(live_ref[base + j] > 0, s, MASKED)
+        s_scr[j] = s
+        return jnp.maximum(m, jnp.max(s, axis=1, keepdims=True))
+
+    m = lax.fori_loop(0, slot_count, score_pass, jnp.full((BS, 1), -jnp.inf, jnp.float32))
+
+    def exp_pass(j, total):
+        e = jnp.exp(s_scr[j] - m)
+        s_scr[j] = e
+        return total + jnp.sum(e, axis=1, keepdims=True)
+
+    total = lax.fori_loop(0, slot_count, exp_pass, jnp.zeros((BS, 1), jnp.float32))
+    inv = 1.0 / total
+    offs = (
+        lax.broadcasted_iota(jnp.int32, (BS, BS), 0) * BS
+        + lax.broadcasted_iota(jnp.int32, (BS, BS), 1)
+    )
+
+    def drop_pass(j, acc):
+        att = s_scr[j] * inv
+        s_scr[j] = att
+        word = seed_ref[seed_base + j] * 40503 + offs
+        word = word ^ srl(word, 15)
+        word = word * 739982445
+        word = word ^ srl(word, 12)
+        word = word * 695872825
+        word = word ^ srl(word, 15)
+        keep = jnp.where((word & 1023) >= KEEP_LEVEL, KEEP_GAIN, 0.0).astype(jnp.float32)
+        keep_scr[j] = keep
+        dropped = (att * keep).astype(jnp.bfloat16)
+        drop_scr[j] = dropped
+        return acc + jnp.dot(dropped, values(j), preferred_element_type=jnp.float32)
+
+    acc = lax.fori_loop(0, slot_count, drop_pass, jnp.zeros((BS, head_size), jnp.float32))
+    att_ref[0] = acc.astype(att_ref.dtype)
+    delta = jnp.sum(g.astype(jnp.float32) * acc, axis=1, keepdims=True)
+
+    def grad_terms(j, qacc):
+        k = keys(j)
+        dg = lax.dot_general(
+            g, values(j), (((1,), (1,)), ((), ())), preferred_element_type=jnp.float32
+        )
+        sg = (s_scr[j] * (dg * keep_scr[j] - delta) * scale).astype(jnp.bfloat16)
+        qacc = qacc + jnp.dot(sg, k, preferred_element_type=jnp.float32)
+        kp = lax.dot_general(sg, q, (((0,), (0,)), ((), ())), preferred_element_type=jnp.float32)
+        vp = lax.dot_general(
+            drop_scr[j], g, (((0,), (0,)), ((), ())), preferred_element_type=jnp.float32
+        )
+        return qacc, kp, vp
+
+    def near_pass(j, qacc):
+        qacc, kp, vp = grad_terms(j, qacc)
+        at = pl.ds(start_of(j), BS)
+        nk_ref[0, at, :] += kp
+        nv_ref[0, at, :] += vp
+        return qacc
+
+    def far_pass(j, qacc):
+        qacc, kp, vp = grad_terms(j, qacc)
+        at = pl.ds(pl.multiple_of(start_of(j) - near_count * BS, BS), BS)
+        fk_ref[0, at, :] = kp.astype(fk_ref.dtype)
+        fv_ref[0, at, :] = vp.astype(fv_ref.dtype)
+        return qacc
+
+    qacc = lax.fori_loop(0, L + 1, near_pass, jnp.zeros((BS, head_size), jnp.float32))
+    qacc = lax.fori_loop(L + 1, slot_count, far_pass, qacc)
+    qg_ref[0] = qacc.astype(qg_ref.dtype)
+
+
+def block_attention(rows, live, seeds, q, g, kt, vt, *, near_count, far_count, scale):
+    heads, row_count, head_size = q.shape
+    blocks = row_count // BS
+    slot_count = 1 + L + E
+    kernel = functools.partial(
+        attention_kernel, scale=scale, near_count=near_count, slot_count=slot_count, blocks=blocks
+    )
+    q_spec = pl.BlockSpec((1, BS, head_size), lambda h, c, *_: (h, c, 0))
+    table_spec = pl.BlockSpec((1, kt.shape[1], head_size), lambda h, c, *_: (h, 0, 0))
+    near_spec = pl.BlockSpec((1, near_count * BS, head_size), lambda h, c, *_: (h, 0, 0))
+    far_spec = pl.BlockSpec((1, far_count * BS, head_size), lambda h, c, *_: (h, 0, 0))
+    grid_spec = pltpu.PrefetchScalarGridSpec(
+        num_scalar_prefetch=3,
+        grid=(heads, blocks),
+        in_specs=[q_spec, q_spec, table_spec, table_spec],
+        out_specs=[q_spec, q_spec, near_spec, near_spec, far_spec, far_spec],
+        scratch_shapes=[
+            pltpu.VMEM((slot_count, BS, BS), jnp.float32),
+            pltpu.VMEM((slot_count, BS, BS), jnp.float32),
+            pltpu.VMEM((slot_count, BS, BS), jnp.bfloat16),
+        ],
+    )
+    flops = 6 * 2 * heads * blocks * slot_count * BS * BS * head_size
+    cost = pl.CostEstimate(
+        flops=flops,
+        transcendentals=heads * blocks * slot_count * BS * BS,
+        bytes_accessed=2 * (q.size * 4 + kt.size * 2) + 4 * heads * (near_count + far_count) * BS * head_size * 2,
+    )
+    return pl.pallas_call(
+        kernel,
+        grid_spec=grid_spec,
+        out_shape=[
+            jax.ShapeDtypeStruct(q.shape, jnp.bfloat16),
+            jax.ShapeDtypeStruct(q.shape, jnp.bfloat16),
+            jax.ShapeDtypeStruct((heads, near_count * BS, head_size), jnp.float32),
+            jax.ShapeDtypeStruct((heads, near_count * BS, head_size), jnp.float32),
+            jax.ShapeDtypeStruct((heads, far_count * BS, head_size), jnp.bfloat16),
+            jax.ShapeDtypeStruct((heads, far_count * BS, head_size), jnp.bfloat16),
+        ],
+        compiler_params=pltpu.CompilerParams(
+            dimension_semantics=("arbitrary", "arbitrary"), vmem_limit_bytes=48 * 1024 * 1024
+        ),
+        cost_estimate=cost,
+    )(rows, live, seeds, q, g, kt, vt)
 
 
 def on_device(
@@ -141,67 +299,39 @@
     table_rows = jnp.concatenate([self_slot, near_slot, far_slot], axis=1)
     slot_number = jnp.arange(slot_count, dtype=jnp.int32)[None, :]
     live_slots = (slot_number <= L) | (slot_number - 1 - L < live_count[:, None])
-    seed_rows = jnp.transpose(drop_seed, (1, 0, 2))
-    query_grid = query_local.reshape(QB_DEV, BS, local_heads, head_size)
-    grad_grid = grad_local.reshape(QB_DEV, BS, local_heads, head_size)
-
-    def block_step(running, inputs):
-        near_total, far_key_total, far_value_total = running
-        query_block, grad_block, slot_row, live_row, seed_row = inputs
-        key_block = key_table[slot_row].reshape(slot_count * BS, local_heads, head_size)
-        value_block = value_table[slot_row].reshape(slot_count * BS, local_heads, head_size)
-        live_keys = jnp.repeat(live_row, BS)
-        keep_scale = keep_weights(seed_row, BS)
-        scores = (
-            jnp.einsum("qhd,khd->hqk", query_block, key_block, preferred_element_type=jnp.float32)
-            * score_scale
+    slot_rows = table_rows.reshape(-1).astype(jnp.int32)
+    live_flat = live_slots.reshape(-1).astype(jnp.int32)
+    seed_flat = drop_seed.reshape(-1).astype(jnp.int32)
+    table_count = key_table.shape[0]
+
+    def head_major(rows):
+        return rows.reshape(-1, local_heads, head_size).transpose(1, 0, 2)
+
+    att_out, qg_out, nk, nv, fk, fv = block_attention(
+        slot_rows,
+        live_flat,
+        seed_flat,
+        head_major(query_local),
+        head_major(grad_local),
+        head_major(key_table.reshape(table_count * BS, local_width)),
+        head_major(value_table.reshape(table_count * BS, local_width)),
+        near_count=near_count,
+        far_count=far_total_count,
+        scale=score_scale,
+    )
+
+    def row_major(arr, count):
+        return arr.reshape(local_heads, count, BS, head_size).transpose(1, 2, 0, 3).reshape(
+            count, BS, local_width
         )
-        scores = jnp.where(live_keys[None, None, :], scores, MASKED)
-        largest = jnp.max(scores, axis=-1, keepdims=True)
-        expterm = jnp.exp(scores - largest)
-        attention = expterm / jnp.sum(expterm, axis=-1, keepdims=True)
-        dropped = (attention * keep_scale).astype(jnp.bfloat16)
-        attended_full = jnp.einsum(
-            "hqk,khd->qhd", dropped, value_block, preferred_element_type=jnp.float32
-        )
-        row_delta = jnp.einsum("qhd,qhd->hq", grad_block.astype(jnp.float32), attended_full)
-        drop_grad = jnp.einsum(
-            "qhd,khd->hqk", grad_block, value_block, preferred_element_type=jnp.float32
-        )
-        score_grad = (
-            attention * (drop_grad * keep_scale - row_delta[:, :, None]) * score_scale
-        ).astype(jnp.bfloat16)
-        query_block_grad = jnp.einsum(
-            "hqk,khd->qhd", score_grad, key_block, preferred_element_type=jnp.float32
-        )
-        key_part = jnp.einsum(
-            "hqk,qhd->khd", score_grad, query_block, preferred_element_type=jnp.float32
-        )
-        value_part = jnp.einsum(
-            "hqk,qhd->khd", dropped, grad_block, preferred_element_type=jnp.float32
-        )
-        key_part = key_part.reshape(slot_count, BS, local_width)
-        value_part = value_part.reshape(slot_count, BS, local_width)
-        near_rows = slot_row[: L + 1]
-        near_total = near_total.at[near_rows, 0].add(key_part[: L + 1])
-        near_total = near_total.at[near_rows, 1].add(value_part[: L + 1])
-        far_rows = slot_row[L + 1 :] - near_count
-        far_key_total = far_key_total.at[far_rows].set(key_part[L + 1 :].astype(jnp.bfloat16))
-        far_value_total = far_value_total.at[far_rows].set(value_part[L + 1 :].astype(jnp.bfloat16))
-        return (
-            (near_total, far_key_total, far_value_total),
-            (attended_full.astype(jnp.bfloat16), query_block_grad.astype(jnp.bfloat16)),
-        )
-
-    start_totals = (
-        jnp.zeros((near_count, 2, BS, local_width), jnp.float32),
-        jnp.zeros((far_total_count, BS, local_width), jnp.bfloat16),
-        jnp.zeros((far_total_count, BS, local_width), jnp.bfloat16),
-    )
-    totals, outputs = lax.scan(
-        block_step, start_totals, (query_grid, grad_grid, table_rows, live_slots, seed_rows)
-    )
-    near_total, far_key_total, far_value_total = totals
+
+    near_total = jnp.stack([row_major(nk, near_count), row_major(nv, near_count)], axis=1)
+    far_key_total = row_major(fk, far_total_count)
+    far_value_total = row_major(fv, far_total_count)
+    outputs = (
+        row_major(att_out, QB_DEV),
+        row_major(qg_out, QB_DEV),
+    )
     back_key, back_value = (
         lax.all_to_all(
             far_key_total.reshape(reply_shape), "blk", split_axis=0, concat_axis=0, tiled=True

time: 834 us -> 921 us (1.10)
  Pallas kernels: 0 us -> 454 us
  local copies, waits for them, and re-layouts: 272 us -> 136 us
  matrix products: 113 us -> 5.69 us
  other arithmetic: 124 us -> 26.4 us
  waiting for transfers between devices: 258 us -> 238 us
    pallas_call x0 -> x1, Pallas kernels: none -> 454 us  [block_attention(): pl.pallas_call(kernel, grid_spec=grid_spec, out_shape=[jax.ShapeDtypeStru...]
    dot_general x40 -> x0, matrix products: 77.5 us -> none  [the longest x8 30.5 us: block_step(): jnp.einsum('qhd,khd->hqk', grad_block, value_block, preferred_element_typ...]
    gather x32 -> x0, local copies, waits for them, and re-layouts: 75.6 us -> none  [the longest x16 42.2 us: block_step(): value_table[slot_row].reshape(slot_count * BS, local_heads, head_size)]
    slice x65 -> x3, local copies, waits for them, and re-layouts: 75.2 us -> 1.13 us  [the longest x2 0.65 us: on_device(): own_total[:, 1].reshape(QB_DEV, BS * local_width) + far_value_sum]
    scatter-add x16 -> x0, other arithmetic: 68.4 us -> none  [the longest x8 36.2 us: block_step(): near_total = near_total.at[near_rows, 0].add(key_part[:L + 1])]
    scatter x16 -> x0, local copies, waits for them, and re-layouts: 35.3 us -> none  [the longest x8 17.7 us: block_step(): far_key_total.at[far_rows].set(key_part[L + 1:].astype(jnp.bfloat16))]
    sub x8 -> x0, matrix products: 34.6 us -> none  [block_step(): expterm = jnp.exp(scores - largest)]
    another operation x2 -> x4, local copies, waits for them, and re-layouts: 4.99 us -> 36.4 us  [head_major(): return rows.reshape(-1, local_heads, head_size).transpose(1, 0, 2)]
  transfers between devices with their start and end apart: 17 -> 17, of which waited for: 9 -> 9; matrix products, arithmetic and copies ran while one was open for 6% -> 12% of each run, Pallas kernels for 0% -> 0%
where the time goes in v1:
time: 921 us; the launch traced here: 918 us
  Pallas kernels  454 us (49%)
  waiting for transfers between devices  238 us (26%)
  local copies, waits for them, and re-layouts  136 us (15%)
  starting transfers between devices  43.9 us (5%)
  other arithmetic  26.4 us (3%)
  between operations  14.4 us (2%)
    pallas_call x1, Pallas kernels, block_attention(): pl.pallas_call(kernel, grid_spec=grid_spec, out_shape=[jax.ShapeDtypeStru...  454 us
    all_to_all x1, waiting for transfers between devices, on_device(): lax.all_to_all(jnp.where(asked_mask, value_blocks[chosen], zero_block).re...  50.3 us
    another operation x4, local copies, waits for them, and re-layouts, head_major(): return rows.reshape(-1, local_heads, head_size).transpose(1, 0, 2)  36.4 us
    all_to_all x1, waiting for transfers between devices, on_device(): lax.all_to_all(far_value_total.reshape(reply_shape), 'blk', split_axis=0,...  36 us
    all_gather x1, waiting for transfers between devices, on_device(): lax.all_gather(out_grad, 'head', axis=0, tiled=True)  32.2 us
    all_to_all x1, waiting for transfers between devices, on_device(): lax.all_to_all(far_key_total.reshape(reply_shape), 'blk', split_axis=0, c...  30.1 us
    all_gather x1, waiting for transfers between devices, on_device(): lax.all_gather(key_rows, 'head', axis=0, tiled=True)  28.6 us
    reshape x6, local copies, waits for them, and re-layouts, row_major(): arr.reshape(local_heads, count, BS, head_size).transpose(1, 2, 0, 3)  25.9 us
  transfers between devices with their start and end apart: 17, of which 9 were waited for; matrix products, arithmetic and copies ran while one was open for 12% of the time, Pallas kernels for 0%

profile of v1, /device:TPU:8, one launch (start us, length us, event | category | flops | bytes accessed | tf_op | source)
XLA Modules:
  0.0 918.2 jit_solution(1795587709276136540)
XLA Ops:
  12.2 8.5 all-to-all-start
  20.8 6.1 all-to-all-done
  28.5 14.2 %all-gather.15.cloned.1.call-done = bf16[1024,1024]{1,0:T(8,128)(2,1)} async-done(((bf16[256,1024]{1,0:T(8,128)(2,1)}), bf16[1024,1024]{1,0:T(8,128)(2,1)}) %all-gather.15.cloned.1.call-update) | async-done | bytes 2097168 | tf_op jit(solution)/shard_map/all_gather | solution.py:236
  46.6 28.6 %all-gather.13.cloned.1.call-done = bf16[1024,1024]{1,0:T(8,128)(2,1)} async-done(((bf16[256,1024]{1,0:T(8,128)(2,1)}), bf16[1024,1024]{1,0:T(8,128)(2,1)}) %all-gather.13.cloned.1.call-update) | async-done | bytes 2097168 | tf_op jit(solution)/shard_map/all_gather | solution.py:235
  79.1 5.8 broadcast_select_fusion
  84.9 7.8 all-to-all-start.2
  93.8 50.3 %all-to-all-done.2 = bf16[32,2,128,256]{3,2,1,0:T(8,128)(2,1)} async-done(((bf16[32,2,128,256]{3,2,1,0:T(8,128)(2,1)}), bf16[32,2,128,256]{3,2,1,0:T(8,128)(2,1)}, u32[]{:S(2)}, u32[]{:S(2)}) %all-to-all-start.2) | async-done | bytes 4194336 | tf_op jit(solution)/shard_map/all_to_all | solution.py:279
  144.1 7.4 all-to-all-start.1
  156.0 32.2 %all-gather.11.cloned.1.call-done = bf16[1024,1024]{0,1:T(8,128)(2,1)} async-done(((bf16[256,1024]{0,1:T(8,128)(2,1)}), bf16[1024,1024]{0,1:T(8,128)(2,1)}) %all-gather.11.cloned.1.call-update) | async-done | bytes 2097168 | tf_op jit(solution)/shard_map/all_gather | solution.py:237
  192.3 13.5 %collective-permute-done = bf16[4,2,128,256]{3,2,0,1:T(8,128)(2,1)} collective-permute-done((bf16[4,2,128,256]{3,2,0,1:T(8,128)(2,1)}, bf16[4,2,128,256]{3,2,0,1:T(8,128)(2,1)}, u32[]{:S(2)}, u32[]{:S(2)}) %collective-permute-start) | collective-permute-done | bytes 524320 | tf_op jit(solution)/shard_map/ppermute | solution.py:28
  212.1 11.3 %copy.81 = bf16[32,2,128,256]{2,1,0,3:T(2,128)(2,1)} copy(bf16[32,2,128,256]{3,2,1,0:T(8,128)(2,1)} %all-to-all-done.2) | data formatting | bytes 8388608 | tf_op jit(solution)/shard_map/all_to_all | solution.py:279
  223.4 5.7 pad_maximum_fusion.2
  229.1 8.0 reshape_reshape.19
  237.1 11.3 %copy.78 = bf16[32,2,128,256]{2,1,0,3:T(2,128)(2,1)} copy(bf16[32,2,128,256]{3,2,1,0:T(8,128)(2,1)} %all-to-all-done.1) | data formatting | bytes 8388608 | tf_op jit(solution)/shard_map/all_to_all | solution.py:272
  248.4 5.4 pad_maximum_fusion.1
  253.8 8.0 reshape_reshape.18
  261.7 10.3 %copy.80 = bf16[10240,4,64]{2,0,1:T(8,128)(2,1)} copy(bf16[10240,4,64]{0,2,1:T(8,128)(2,1)} %reshape_reshape.18) | data formatting | bytes 10485760 | tf_op jit(solution)/shard_map/reshape;reshape | solution.py:308
  272.0 10.2 %copy.83 = bf16[10240,4,64]{2,0,1:T(8,128)(2,1)} copy(bf16[10240,4,64]{0,2,1:T(8,128)(2,1)} %reshape_reshape.19) | data formatting | bytes 10485760 | tf_op jit(solution)/shard_map/reshape;reshape | solution.py:308
  282.2 453.5 %shard_map.120 = (bf16[4,1024,64]{2,1,0:T(8,128)(2,1)S(1)}, bf16[4,1024,64]{2,1,0:T(8,128)(2,1)S(1)}, f32[4,2048,64]{2,1,0:T(8,128)}, f32[4,2048,64]{2,1,0:T(8,1...) custom-call(s32[128]{0:T(128)S(1)} %reshape.243.rows_ref, s32[128]{0:T(128)S(1)} %reshape.262.live_ref, ...), custom_call_target="tpu_custom_call" | custom-call | flops 6442450944 | bytes 33554432 | tf_op jit(solution)/shard_map/pallas_call | solution.py:196
  739.3 8.6 copy.89
  747.8 8.7 all-to-all-start.3
  757.9 2.9 copy.86
  760.8 3.9 copy.87
  769.4 8.6 copy.92
  778.0 30.1 %all-to-all-done.3 = bf16[32,2,128,256]{2,3,1,0:T(8,128)(2,1)} async-done(((bf16[32,2,128,256]{2,3,1,0:T(8,128)(2,1)}), bf16[32,2,128,256]{2,3,1,0:T(8,128)(2,1)}, u32[]{:S(2)}, u32[]{:S(2)}) %all-to-all-start.3) | async-done | bytes 4194336 | tf_op jit(solution)/shard_map/all_to_all | solution.py:336
  808.1 7.5 all-to-all-start.4
  819.8 6.8 copy.98
  826.6 2.8 fusion
  831.0 36.0 %all-to-all-done.4 = bf16[32,2,128,256]{2,3,1,0:T(8,128)(2,1)} async-done(((bf16[32,2,128,256]{2,3,1,0:T(8,128)(2,1)}), bf16[32,2,128,256]{2,3,1,0:T(8,128)(2,1)}, u32[]{:S(2)}, u32[]{:S(2)}) %all-to-all-start.4) | async-done | bytes 4194336 | tf_op jit(solution)/shard_map/all_to_all | solution.py:339
  867.1 6.8 copy.99
  873.9 2.8 fusion.1
  883.9 25.6 %all-gather.23.cloned.1.call-done = bf16[1024,1024]{1,0:T(8,128)(2,1)} async-done(((bf16[1024,256]{1,0:T(8,128)(2,1)}), bf16[1024,1024]{1,0:T(8,128)(2,1)}) %all-gather.23.cloned.1.call-update) | async-done | bytes 2097168 | tf_op jit(solution)/shard_map/all_gather | solution.py:380
  (109 shorter events, 54.6 us)
Async XLA Ops:
  7.2 35.6 %all-gather.15.cloned.1.call-start = ((), (), s32[]{:S(2)}) async-start(), calls=%async_computation.8 | async-start | bytes 2621440 | tf_op jit(solution)/shard_map/all_gather | solution.py:236
  7.9 67.3 %all-gather.13.cloned.1.call-start = ((), (), s32[]{:S(2)}) async-start(), calls=%async_computation.7 | async-start | bytes 2621440 | tf_op jit(solution)/shard_map/all_gather | solution.py:235
  12.2 14.7 %all-to-all-start = ((s32[32,1,2]{2,1,0:T(1,128)}), s32[32,1,2]{2,1,0:T(1,128)S(1)}, u32[]{:S(2)}, u32[]{:S(2)}) async-start(s32[32,1,2]{2,1,0:T(1,128)} %bitcast.9), calls=%async_computation | async-start | bytes 32768 | tf_op jit(solution)/shard_map/all_to_all | solution.py:259
  84.9 7.8 copy-start.2
  84.9 59.2 %all-to-all-start.2 = ((bf16[32,2,128,256]{3,2,1,0:T(8,128)(2,1)}), bf16[32,2,128,256]{3,2,1,0:T(8,128)(2,1)}, u32[]{:S(2)}, u32[]{:S(2)}) async-start(bf16[32,2,128,256]{3,2,1,0:T(8,128)(2,1)} %get-tuple-element.62), calls=%async_computation.2 | async-start | bytes 8388608 | tf_op jit(solution)/shard_map/all_to_all | solution.py:279
  92.7 63.3 %all-gather.9.cloned.1.call-start = ((), (), s32[]{:S(2)}) async-start(), calls=%async_computation.5 | async-start | bytes 2621440 | tf_op jit(solution)/shard_map/all_gather | solution.py:234
  144.1 7.5 copy-start.3
  144.1 8.6 copy-start.6
  144.1 11.5 %copy-start.4 = (s32[4,8,16]{2,1,0:T(8,128)S(1)}, s32[4,8,16]{2,1,0:T(8,128)}, u32[]{:S(2)}) copy-start(s32[4,8,16]{2,1,0:T(8,128)} %param.21) | copy-start | bytes 6148
  144.1 11.7 %copy-start.5 = (s32[8,11]{1,0:T(8,128)S(1)}, s32[8,11]{1,0:T(8,128)}, u32[]{:S(2)}) copy-start(s32[8,11]{1,0:T(8,128)} %param.19) | copy-start | bytes 1060
  144.1 93.0 %all-to-all-start.1 = ((bf16[32,2,128,256]{3,2,1,0:T(8,128)(2,1)}), bf16[32,2,128,256]{3,2,1,0:T(8,128)(2,1)}, u32[]{:S(2)}, u32[]{:S(2)}) async-start(bf16[32,2,128,256]{3,2,1,0:T(8,128)(2,1)} %get-tuple-element.63), calls=%async_computation.1 | async-start | bytes 8388608 | tf_op jit(solution)/shard_map/all_to_all | solution.py:272
  151.6 36.6 %all-gather.11.cloned.1.call-start = ((), (), s32[]{:S(2)}) async-start(), calls=%async_computation.6 | async-start | bytes 2621440 | tf_op jit(solution)/shard_map/all_gather | solution.py:237
  152.6 725.2 %all-gather.19.cloned.1.call-start = ((), (), s32[]{:S(2)}) async-start(), calls=%async_computation.10 | async-start | bytes 2621440 | tf_op jit(solution)/shard_map/all_gather | solution.py:378
  153.9 51.9 %collective-permute-start = (bf16[4,2,128,256]{3,2,0,1:T(8,128)(2,1)}, bf16[4,2,128,256]{3,2,0,1:T(8,128)(2,1)}, u32[]{:S(2)}, u32[]{:S(2)}) collective-permute-start(bf16[4,2,128,256]{3,2,0,1:T(8,128)(2,1)} %get-tuple-element.60), channel_id=1, source_target_pairs={{0,4},{4,8},{8,12},{12,16},{16,20},{20,24},{24,28},{28,32},{32,36}... | collective-permute-start | bytes 1572872 | tf_op jit(solution)/shard_map/ppermute | solution.py:28
  154.0 51.8 %collective-permute-start.1 = (bf16[4,2,128,256]{3,2,0,1:T(8,128)(2,1)}, bf16[4,2,128,256]{3,2,0,1:T(8,128)(2,1)}, u32[]{:S(2)}, u32[]{:S(2)}) collective-permute-start(bf16[4,2,128,256]{3,2,0,1:T(8,128)(2,1)} %get-tuple-element.61), channel_id=1, source_target_pairs={{4,0},{8,4},{12,8},{16,12},{20,16},{24,20},{28,24},{32,28},{36,32}... | collective-permute-start | bytes 1572872 | tf_op jit(solution)/shard_map/ppermute | solution.py:31
  735.8 1.0 copy-start
  747.8 60.2 %all-to-all-start.3 = ((bf16[32,2,128,256]{2,3,1,0:T(8,128)(2,1)}), bf16[32,2,128,256]{2,3,1,0:T(8,128)(2,1)}, u32[]{:S(2)}, u32[]{:S(2)}) async-start(bf16[32,2,128,256]{2,3,1,0:T(8,128)(2,1)} %bitcast.96), calls=%async_computation.3 | async-start | bytes 8388608 | tf_op jit(solution)/shard_map/all_to_all | solution.py:336
  756.5 123.4 %all-gather.17.cloned.1.call-start = ((), (), s32[]{:S(2)}) async-start(), calls=%async_computation.9 | async-start | bytes 2621440 | tf_op jit(solution)/shard_map/all_gather | solution.py:377
  767.5 49.8 %collective-permute-start.2 = (bf16[4,2,128,256]{2,3,0,1:T(8,128)(2,1)}, bf16[4,2,128,256]{2,3,0,1:T(8,128)(2,1)}, u32[]{:S(2)}, u32[]{:S(2)}) collective-permute-start(bf16[4,2,128,256]{2,3,0,1:T(8,128)(2,1)} %get-tuple-element.57), channel_id=1, source_target_pairs={{124,0},{0,4},{4,8},{8,12},{12,16},{16,20},{20,24},{24,28},{28,32}... | collective-permute-start | bytes 1572872 | tf_op jit(solution)/shard_map/ppermute | solution.py:39
  767.6 51.2 %collective-permute-start.3 = (bf16[4,2,128,256]{2,3,0,1:T(8,128)(2,1)S(1)}, bf16[4,2,128,256]{2,3,0,1:T(8,128)(2,1)S(1)}, u32[]{:S(2)}, u32[]{:S(2)}) collective-permute-start(bf16[4,2,128,256]{2,3,0,1:T(8,128)(2,1)S(1)} %get-tuple-element.56), channel_id=1, source_target_pairs={{4,0},{8,4},{12,8},{16,12},{20,16},{24,20},{28,24},{32,28},{36,32}... | collective-permute-start | bytes 1572872 | tf_op jit(solution)/shard_map/ppermute | solution.py:39
  808.1 59.0 %all-to-all-start.4 = ((bf16[32,2,128,256]{2,3,1,0:T(8,128)(2,1)}), bf16[32,2,128,256]{2,3,1,0:T(8,128)(2,1)}, u32[]{:S(2)}, u32[]{:S(2)}) async-start(bf16[32,2,128,256]{2,3,1,0:T(8,128)(2,1)} %bitcast.95), calls=%async_computation.4 | async-start | bytes 8388608 | tf_op jit(solution)/shard_map/all_to_all | solution.py:339
  815.5 66.5 %all-gather.21.cloned.1.call-start = ((), (), s32[]{:S(2)}) async-start(), calls=%async_computation.11 | async-start | bytes 2621440 | tf_op jit(solution)/shard_map/all_gather | solution.py:379
  815.8 1.9 copy-start.1
  830.5 79.0 %all-gather.23.cloned.1.call-start = ((), (), s32[]{:S(2)}) async-start(), calls=%async_computation.12 | async-start | bytes 2621440 | tf_op jit(solution)/shard_map/all_gather | solution.py:380
Sparse Core Ops, SparseCore 0:
  9.6 33.0 all-gather.14
  44.4 30.7 all-gather.12
  95.7 33.7 all-gather.8
  154.3 33.8 all-gather.10
  739.4 31.8 all-gather.18
  773.4 30.7 all-gather.16
  830.6 33.8 all-gather.20
  877.9 31.5 all-gather.22

commit v2 on v1

--- a/solution.py
+++ b/solution.py
@@ -57,15 +57,21 @@
     return keep_scale.reshape(seed_row.shape[0], block_size, -1)
 
 
+def unrolled(body, carry, first, last):
+    for j in range(first, last):
+        carry = body(j, carry)
+    return carry
+
+
 def srl(value, amount):
     return lax.shift_right_logical(value, jnp.full(value.shape, amount, jnp.int32))
 
 
 def attention_kernel(
-    rows_ref, live_ref, seed_ref, q_ref, g_ref, kt_ref, vt_ref,
+    rows_ref, count_ref, seed_ref, q_ref, g_ref, kt_ref, vt_ref,
     att_ref, qg_ref, nk_ref, nv_ref, fk_ref, fv_ref,
     s_scr, keep_scr, drop_scr,
-    *, scale, near_count, slot_count, blocks,
+    *, scale, near_count, slot_count, blocks, use_hash=True,
 ):
     h = pl.program_id(0)
     c = pl.program_id(1)
@@ -78,10 +84,13 @@
         fk_ref[...] = jnp.zeros_like(fk_ref)
         fv_ref[...] = jnp.zeros_like(fv_ref)
 
-    q = q_ref[0]
+    q = q_ref[0] * jnp.asarray(scale, q_ref.dtype)
     g = g_ref[0]
+    q_t = q.T
+    g_t = g.T
     base = c * slot_count
     seed_base = (h * blocks + c) * slot_count
+    live_end = L + 1 + count_ref[c]
 
     def start_of(j):
         return pl.multiple_of(rows_ref[base + j] * BS, BS)
@@ -95,20 +104,22 @@
     def score_pass(j, m):
         s = lax.dot_general(
             q, keys(j), (((1,), (1,)), ((), ())), preferred_element_type=jnp.float32
-        ) * scale
-        s = jnp.where(live_ref[base + j] > 0, s, MASKED)
+        )
+        if j > L:
+            s = jnp.where(j < live_end, s, MASKED)
         s_scr[j] = s
-        return jnp.maximum(m, jnp.max(s, axis=1, keepdims=True))
-
-    m = lax.fori_loop(0, slot_count, score_pass, jnp.full((BS, 1), -jnp.inf, jnp.float32))
+        return jnp.maximum(m, s)
+
+    m = unrolled(score_pass, jnp.full((BS, BS), -jnp.inf, jnp.float32), 0, slot_count)
+    m = jnp.max(m, axis=1, keepdims=True)
 
     def exp_pass(j, total):
         e = jnp.exp(s_scr[j] - m)
         s_scr[j] = e
-        return total + jnp.sum(e, axis=1, keepdims=True)
-
-    total = lax.fori_loop(0, slot_count, exp_pass, jnp.zeros((BS, 1), jnp.float32))
-    inv = 1.0 / total
+        return total + e
+
+    total = unrolled(exp_pass, jnp.zeros((BS, BS), jnp.float32), 0, slot_count)
+    inv = 1.0 / jnp.sum(total, axis=1, keepdims=True)
     offs = (
         lax.broadcasted_iota(jnp.int32, (BS, BS), 0) * BS
         + lax.broadcasted_iota(jnp.int32, (BS, BS), 1)
@@ -117,65 +128,66 @@
     def drop_pass(j, acc):
         att = s_scr[j] * inv
         s_scr[j] = att
-        word = seed_ref[seed_base + j] * 40503 + offs
-        word = word ^ srl(word, 15)
-        word = word * 739982445
-        word = word ^ srl(word, 12)
-        word = word * 695872825
-        word = word ^ srl(word, 15)
-        keep = jnp.where((word & 1023) >= KEEP_LEVEL, KEEP_GAIN, 0.0).astype(jnp.float32)
+        if use_hash:
+            word = seed_ref[seed_base + j] * 40503 + offs
+            word = word ^ srl(word, 15)
+            word = word * 739982445
+            word = word ^ srl(word, 12)
+            word = word * 695872825
+            word = word ^ srl(word, 15)
+            keep = jnp.where((word & 1023) >= KEEP_LEVEL, KEEP_GAIN, 0.0).astype(jnp.float32)
+        else:
+            keep = jnp.where(offs >= seed_ref[seed_base + j], KEEP_GAIN, 0.0).astype(jnp.float32)
         keep_scr[j] = keep
         dropped = (att * keep).astype(jnp.bfloat16)
         drop_scr[j] = dropped
         return acc + jnp.dot(dropped, values(j), preferred_element_type=jnp.float32)
 
-    acc = lax.fori_loop(0, slot_count, drop_pass, jnp.zeros((BS, head_size), jnp.float32))
+    acc = unrolled(drop_pass, jnp.zeros((BS, head_size), jnp.float32), 0, slot_count)
     att_ref[0] = acc.astype(att_ref.dtype)
     delta = jnp.sum(g.astype(jnp.float32) * acc, axis=1, keepdims=True)
 
     def grad_terms(j, qacc):
-        k = keys(j)
         dg = lax.dot_general(
             g, values(j), (((1,), (1,)), ((), ())), preferred_element_type=jnp.float32
         )
-        sg = (s_scr[j] * (dg * keep_scr[j] - delta) * scale).astype(jnp.bfloat16)
-        qacc = qacc + jnp.dot(sg, k, preferred_element_type=jnp.float32)
-        kp = lax.dot_general(sg, q, (((0,), (0,)), ((), ())), preferred_element_type=jnp.float32)
-        vp = lax.dot_general(
-            drop_scr[j], g, (((0,), (0,)), ((), ())), preferred_element_type=jnp.float32
-        )
+        sg = (s_scr[j] * (dg * keep_scr[j] - delta)).astype(jnp.bfloat16)
+        qacc = qacc + jnp.dot(sg, keys(j), preferred_element_type=jnp.float32)
+        kp = jnp.dot(q_t, sg, preferred_element_type=jnp.float32)
+        vp = jnp.dot(g_t, drop_scr[j], preferred_element_type=jnp.float32)
         return qacc, kp, vp
 
     def near_pass(j, qacc):
         qacc, kp, vp = grad_terms(j, qacc)
-        at = pl.ds(start_of(j), BS)
-        nk_ref[0, at, :] += kp
-        nv_ref[0, at, :] += vp
+        at = rows_ref[base + j]
+        nk_ref[0, at] += kp
+        nv_ref[0, at] += vp
         return qacc
 
     def far_pass(j, qacc):
         qacc, kp, vp = grad_terms(j, qacc)
-        at = pl.ds(pl.multiple_of(start_of(j) - near_count * BS, BS), BS)
-        fk_ref[0, at, :] = kp.astype(fk_ref.dtype)
-        fv_ref[0, at, :] = vp.astype(fv_ref.dtype)
+        at = rows_ref[base + j] - near_count
+        fk_ref[0, at] = kp.astype(fk_ref.dtype)
+        fv_ref[0, at] = vp.astype(fv_ref.dtype)
         return qacc
 
-    qacc = lax.fori_loop(0, L + 1, near_pass, jnp.zeros((BS, head_size), jnp.float32))
-    qacc = lax.fori_loop(L + 1, slot_count, far_pass, qacc)
-    qg_ref[0] = qacc.astype(qg_ref.dtype)
-
-
-def block_attention(rows, live, seeds, q, g, kt, vt, *, near_count, far_count, scale):
+    qacc = unrolled(near_pass, jnp.zeros((BS, head_size), jnp.float32), 0, L + 1)
+    qacc = unrolled(far_pass, qacc, L + 1, slot_count)
+    qg_ref[0] = (qacc * scale).astype(qg_ref.dtype)
+
+
+def block_attention(rows, counts, seeds, q, g, kt, vt, *, near_count, far_count, scale, use_hash=True):
     heads, row_count, head_size = q.shape
     blocks = row_count // BS
     slot_count = 1 + L + E
     kernel = functools.partial(
-        attention_kernel, scale=scale, near_count=near_count, slot_count=slot_count, blocks=blocks
+        attention_kernel, scale=scale, near_count=near_count, slot_count=slot_count,
+        blocks=blocks, use_hash=use_hash,
     )
     q_spec = pl.BlockSpec((1, BS, head_size), lambda h, c, *_: (h, c, 0))
     table_spec = pl.BlockSpec((1, kt.shape[1], head_size), lambda h, c, *_: (h, 0, 0))
-    near_spec = pl.BlockSpec((1, near_count * BS, head_size), lambda h, c, *_: (h, 0, 0))
-    far_spec = pl.BlockSpec((1, far_count * BS, head_size), lambda h, c, *_: (h, 0, 0))
+    near_spec = pl.BlockSpec((1, near_count, head_size, BS), lambda h, c, *_: (h, 0, 0, 0))
+    far_spec = pl.BlockSpec((1, far_count, head_size, BS), lambda h, c, *_: (h, 0, 0, 0))
     grid_spec = pltpu.PrefetchScalarGridSpec(
         num_scalar_prefetch=3,
         grid=(heads, blocks),
@@ -199,16 +211,16 @@
         out_shape=[
             jax.ShapeDtypeStruct(q.shape, jnp.bfloat16),
             jax.ShapeDtypeStruct(q.shape, jnp.bfloat16),
-            jax.ShapeDtypeStruct((heads, near_count * BS, head_size), jnp.float32),
-            jax.ShapeDtypeStruct((heads, near_count * BS, head_size), jnp.float32),
-            jax.ShapeDtypeStruct((heads, far_count * BS, head_size), jnp.bfloat16),
-            jax.ShapeDtypeStruct((heads, far_count * BS, head_size), jnp.bfloat16),
+            jax.ShapeDtypeStruct((heads, near_count, head_size, BS), jnp.float32),
+            jax.ShapeDtypeStruct((heads, near_count, head_size, BS), jnp.float32),
+            jax.ShapeDtypeStruct((heads, far_count, head_size, BS), jnp.bfloat16),
+            jax.ShapeDtypeStruct((heads, far_count, head_size, BS), jnp.bfloat16),
         ],
         compiler_params=pltpu.CompilerParams(
             dimension_semantics=("arbitrary", "arbitrary"), vmem_limit_bytes=48 * 1024 * 1024
         ),
         cost_estimate=cost,
-    )(rows, live, seeds, q, g, kt, vt)
+    )(rows, counts, seeds, q, g, kt, vt)
 
 
 def on_device(
@@ -300,7 +312,6 @@
     slot_number = jnp.arange(slot_count, dtype=jnp.int32)[None, :]
     live_slots = (slot_number <= L) | (slot_number - 1 - L < live_count[:, None])
     slot_rows = table_rows.reshape(-1).astype(jnp.int32)
-    live_flat = live_slots.reshape(-1).astype(jnp.int32)
     seed_flat = drop_seed.reshape(-1).astype(jnp.int32)
     table_count = key_table.shape[0]
 
@@ -309,7 +320,7 @@
 
     att_out, qg_out, nk, nv, fk, fv = block_attention(
         slot_rows,
-        live_flat,
+        live_count.astype(jnp.int32),
         seed_flat,
         head_major(query_local),
         head_major(grad_local),
@@ -325,9 +336,12 @@
             count, BS, local_width
         )
 
-    near_total = jnp.stack([row_major(nk, near_count), row_major(nv, near_count)], axis=1)
-    far_key_total = row_major(fk, far_total_count)
-    far_value_total = row_major(fv, far_total_count)
+    def from_columns(arr, count):
+        return arr.transpose(1, 3, 0, 2).reshape(count, BS, local_width)
+
+    near_total = jnp.stack([from_columns(nk, near_count), from_columns(nv, near_count)], axis=1)
+    far_key_total = from_columns(fk, far_total_count)
+    far_value_total = from_columns(fv, far_total_count)
     outputs = (
         row_major(att_out, QB_DEV),
         row_major(qg_out, QB_DEV),

time: 921 us -> 611 us (0.66)
  Pallas kernels: 454 us -> 146 us
  local copies, waits for them, and re-layouts: 136 us -> 126 us
    pallas_call x1, Pallas kernels: 454 us -> 146 us  [block_attention(): pl.pallas_call(kernel, grid_spec=grid_spec, out_shape=[jax.ShapeDtypeStru...]
    reshape x6 -> x2, local copies, waits for them, and re-layouts: 25.9 us -> 2.02 us  [row_major(): arr.reshape(local_heads, count, BS, head_size).transpose(1, 2, 0, 3)]
    transpose x0 -> x4, local copies, waits for them, and re-layouts: none -> 13.4 us  [from_columns(): return arr.transpose(1, 3, 0, 2).reshape(count, BS, local_width)]
    unnamed x23 -> x27, local copies, waits for them, and re-layouts: 21.5 us -> 21.9 us
  transfers between devices with their start and end apart: 17 -> 17, of which waited for: 9 -> 9; matrix products, arithmetic and copies ran while one was open for 12% -> 16% of each run, Pallas kernels for 0% -> 0%
where the time goes in v2:
time: 611 us; the launch traced here: 608 us
  waiting for transfers between devices  247 us (40%)
  Pallas kernels  146 us (24%)
  local copies, waits for them, and re-layouts  126 us (21%)
  starting transfers between devices  43.7 us (7%)
  other arithmetic  24.7 us (4%)
  between operations  14.4 us (2%)
    pallas_call x1, Pallas kernels, block_attention(): pl.pallas_call(kernel, grid_spec=grid_spec, out_shape=[jax.ShapeDtypeStru...  146 us
    all_to_all x1, waiting for transfers between devices, on_device(): lax.all_to_all(jnp.where(asked_mask, value_blocks[chosen], zero_block).re...  50.3 us
    all_to_all x1, waiting for transfers between devices, on_device(): lax.all_to_all(far_key_total.reshape(reply_shape), 'blk', split_axis=0, c...  38.7 us
    another operation x4, local copies, waits for them, and re-layouts, head_major(): return rows.reshape(-1, local_heads, head_size).transpose(1, 0, 2)  36.5 us
    all_to_all x1, waiting for transfers between devices, on_device(): lax.all_to_all(far_value_total.reshape(reply_shape), 'blk', split_axis=0,...  36.2 us
    all_gather x1, waiting for transfers between devices, on_device(): lax.all_gather(out_grad, 'head', axis=0, tiled=True)  32.4 us
    all_gather x1, waiting for transfers between devices, on_device(): lax.all_gather(key_rows, 'head', axis=0, tiled=True)  28.6 us
    all_gather x1, waiting for transfers between devices, on_device(): lax.all_gather(results[3], 'head', axis=1, tiled=True)  25.5 us
  transfers between devices with their start and end apart: 17, of which 9 were waited for; matrix products, arithmetic and copies ran while one was open for 16% of the time, Pallas kernels for 0%

profile of v2, /device:TPU:8, one launch (start us, length us, event | category | flops | bytes accessed | tf_op | source)
XLA Modules:
  0.0 607.9 jit_solution(15795891148552018394)
XLA Ops:
  12.2 8.5 %all-to-all-start = ((s32[32,1,2]{2,1,0:T(1,128)}), s32[32,1,2]{2,1,0:T(1,128)S(1)}, u32[]{:S(2)}, u32[]{:S(2)}) async-start(s32[32,1,2]{2,1,0:T(1,128)} %bitcast.9), calls=%async_computation | async-start | bytes 32768 | tf_op jit(solution)/shard_map/all_to_all | solution.py:271
  20.8 6.1 %all-to-all-done = s32[32,1,2]{2,1,0:T(1,128)S(1)} async-done(((s32[32,1,2]{2,1,0:T(1,128)}), s32[32,1,2]{2,1,0:T(1,128)S(1)}, u32[]{:S(2)}, u32[]{:S(2)}) %all-to-all-start) | async-done | bytes 288 | tf_op jit(solution)/shard_map/all_to_all | solution.py:271
  28.5 14.2 %all-gather.15.cloned.1.call-done = bf16[1024,1024]{1,0:T(8,128)(2,1)} async-done(((bf16[256,1024]{1,0:T(8,128)(2,1)}), bf16[1024,1024]{1,0:T(8,128)(2,1)}) %all-gather.15.cloned.1.call-update) | async-done | bytes 2097168 | tf_op jit(solution)/shard_map/all_gather | solution.py:248
  43.8 2.8 gather_fusion.1
  46.6 28.6 %all-gather.13.cloned.1.call-done = bf16[1024,1024]{1,0:T(8,128)(2,1)} async-done(((bf16[256,1024]{1,0:T(8,128)(2,1)}), bf16[1024,1024]{1,0:T(8,128)(2,1)}) %all-gather.13.cloned.1.call-update) | async-done | bytes 2097168 | tf_op jit(solution)/shard_map/all_gather | solution.py:247
  76.3 2.8 gather_fusion
  79.1 5.9 broadcast_select_fusion
  84.9 7.8 %all-to-all-start.2 = ((bf16[32,2,128,256]{3,2,1,0:T(8,128)(2,1)}), bf16[32,2,128,256]{3,2,1,0:T(8,128)(2,1)}, u32[]{:S(2)}, u32[]{:S(2)}) async-start(bf16[32,2,128,256]{3,2,1,0:T(8,128)(2,1)} %get-tuple-element.62), calls=%async_computation.2 | async-start | bytes 8388608 | tf_op jit(solution)/shard_map/all_to_all | solution.py:291
  93.8 50.3 %all-to-all-done.2 = bf16[32,2,128,256]{3,2,1,0:T(8,128)(2,1)} async-done(((bf16[32,2,128,256]{3,2,1,0:T(8,128)(2,1)}), bf16[32,2,128,256]{3,2,1,0:T(8,128)(2,1)}, u32[]{:S(2)}, u32[]{:S(2)}) %all-to-all-start.2) | async-done | bytes 4194336 | tf_op jit(solution)/shard_map/all_to_all | solution.py:291
  144.1 7.4 %all-to-all-start.1 = ((bf16[32,2,128,256]{3,2,1,0:T(8,128)(2,1)}), bf16[32,2,128,256]{3,2,1,0:T(8,128)(2,1)}, u32[]{:S(2)}, u32[]{:S(2)}) async-start(bf16[32,2,128,256]{3,2,1,0:T(8,128)(2,1)} %get-tuple-element.63), calls=%async_computation.1 | async-start | bytes 8388608 | tf_op jit(solution)/shard_map/all_to_all | solution.py:284
  155.8 32.4 %all-gather.11.cloned.1.call-done = bf16[1024,1024]{0,1:T(8,128)(2,1)} async-done(((bf16[256,1024]{0,1:T(8,128)(2,1)}), bf16[1024,1024]{0,1:T(8,128)(2,1)}) %all-gather.11.cloned.1.call-update) | async-done | bytes 2097168 | tf_op jit(solution)/shard_map/all_gather | solution.py:249
  192.3 13.5 %collective-permute-done = bf16[4,2,128,256]{3,2,0,1:T(8,128)(2,1)} collective-permute-done((bf16[4,2,128,256]{3,2,0,1:T(8,128)(2,1)}, bf16[4,2,128,256]{3,2,0,1:T(8,128)(2,1)}, u32[]{:S(2)}, u32[]{:S(2)}) %collective-permute-start) | collective-permute-done | bytes 524320 | tf_op jit(solution)/shard_map/ppermute | solution.py:28
  212.2 11.3 %copy.81 = bf16[32,2,128,256]{2,1,0,3:T(2,128)(2,1)} copy(bf16[32,2,128,256]{3,2,1,0:T(8,128)(2,1)} %all-to-all-done.2) | data formatting | bytes 8388608 | tf_op jit(solution)/shard_map/all_to_all | solution.py:291
  223.4 5.7 pad_maximum_fusion.2
  229.1 8.0 %reshape_reshape.19 = bf16[10240,4,64]{0,2,1:T(8,128)(2,1)} reshape(bf16[80,128,256]{1,0,2:T(8,128)(2,1)} %pad_maximum_fusion.2) | data formatting | bytes 10485760 | tf_op jit(solution)/shard_map/reshape;reshape | solution.py:319
  237.1 11.3 %copy.78 = bf16[32,2,128,256]{2,1,0,3:T(2,128)(2,1)} copy(bf16[32,2,128,256]{3,2,1,0:T(8,128)(2,1)} %all-to-all-done.1) | data formatting | bytes 8388608 | tf_op jit(solution)/shard_map/all_to_all | solution.py:284
  248.4 5.4 pad_maximum_fusion.1
  253.8 8.0 %reshape_reshape.18 = bf16[10240,4,64]{0,2,1:T(8,128)(2,1)} reshape(bf16[80,128,256]{1,0,2:T(8,128)(2,1)} %pad_maximum_fusion.1) | data formatting | bytes 10485760 | tf_op jit(solution)/shard_map/reshape;reshape | solution.py:319
  261.8 10.3 %copy.80 = bf16[10240,4,64]{2,0,1:T(8,128)(2,1)} copy(bf16[10240,4,64]{0,2,1:T(8,128)(2,1)} %reshape_reshape.18) | data formatting | bytes 10485760 | tf_op jit(solution)/shard_map/reshape;reshape | solution.py:319
  272.1 10.2 %copy.83 = bf16[10240,4,64]{2,0,1:T(8,128)(2,1)} copy(bf16[10240,4,64]{0,2,1:T(8,128)(2,1)} %reshape_reshape.19) | data formatting | bytes 10485760 | tf_op jit(solution)/shard_map/reshape;reshape | solution.py:319
  282.3 146.2 %shard_map.120 = (bf16[4,1024,64]{2,1,0:T(8,128)(2,1)S(1)}, bf16[4,1024,64]{2,1,0:T(8,128)(2,1)S(1)}, f32[4,16,64,128]{3,2,1,0:T(8,128)}, f32[4,16,64,128]{3,2,1...) custom-call(s32[128]{0:T(128)S(1)} %reshape.212.rows_ref, s32[8]{0:T(128)S(1)} %copy-done.1, ...), custom_call_target="tpu_custom_call" | custom-call | flops 6442450944 | bytes 33554432 | tf_op jit(solution)/shard_map/pallas_call | solution.py:208
  432.1 5.6 copy.89
  437.7 8.7 %all-to-all-start.3 = ((bf16[32,2,128,256]{2,3,1,0:T(8,128)(2,1)}), bf16[32,2,128,256]{2,3,1,0:T(8,128)(2,1)}, u32[]{:S(2)}, u32[]{:S(2)}) async-start(bf16[32,2,128,256]{2,3,1,0:T(8,128)(2,1)} %bitcast.90), calls=%async_computation.3 | async-start | bytes 8388608 | tf_op jit(solution)/shard_map/all_to_all | solution.py:350
  453.6 5.7 copy.92
  459.3 38.7 %all-to-all-done.3 = bf16[32,2,128,256]{2,3,1,0:T(8,128)(2,1)} async-done(((bf16[32,2,128,256]{2,3,1,0:T(8,128)(2,1)}), bf16[32,2,128,256]{2,3,1,0:T(8,128)(2,1)}, u32[]{:S(2)}, u32[]{:S(2)}) %all-to-all-start.3) | async-done | bytes 4194336 | tf_op jit(solution)/shard_map/all_to_all | solution.py:350
  497.9 7.5 %all-to-all-start.4 = ((bf16[32,2,128,256]{2,3,1,0:T(8,128)(2,1)}), bf16[32,2,128,256]{2,3,1,0:T(8,128)(2,1)}, u32[]{:S(2)}, u32[]{:S(2)}) async-start(bf16[32,2,128,256]{2,3,1,0:T(8,128)(2,1)} %bitcast.89), calls=%async_computation.4 | async-start | bytes 8388608 | tf_op jit(solution)/shard_map/all_to_all | solution.py:353
  509.4 6.8 %copy.98 = bf16[8,8,128,256]{3,1,2,0:T(8,128)(2,1)} copy(bf16[8,8,128,256]{2,3,1,0:T(8,128)(2,1)} %bitcast.62) | data formatting | bytes 8388608
  516.2 2.8 fusion
  520.7 36.2 %all-to-all-done.4 = bf16[32,2,128,256]{2,3,1,0:T(8,128)(2,1)} async-done(((bf16[32,2,128,256]{2,3,1,0:T(8,128)(2,1)}), bf16[32,2,128,256]{2,3,1,0:T(8,128)(2,1)}, u32[]{:S(2)}, u32[]{:S(2)}) %all-to-all-start.4) | async-done | bytes 4194336 | tf_op jit(solution)/shard_map/all_to_all | solution.py:353
  556.9 6.8 %copy.99 = bf16[8,8,128,256]{3,1,2,0:T(8,128)(2,1)} copy(bf16[8,8,128,256]{2,3,1,0:T(8,128)(2,1)} %bitcast.63) | data formatting | bytes 8388608
  563.7 2.8 fusion.1
  573.7 25.5 %all-gather.23.cloned.1.call-done = bf16[1024,1024]{1,0:T(8,128)(2,1)} async-done(((bf16[1024,256]{1,0:T(8,128)(2,1)}), bf16[1024,1024]{1,0:T(8,128)(2,1)}) %all-gather.23.cloned.1.call-update) | async-done | bytes 2097168 | tf_op jit(solution)/shard_map/all_gather | solution.py:394
  (109 shorter events, 49.7 us)
Async XLA Ops:
  7.2 35.6 %all-gather.15.cloned.1.call-start = ((), (), s32[]{:S(2)}) async-start(), calls=%async_computation.8 | async-start | bytes 2621440 | tf_op jit(solution)/shard_map/all_gather | solution.py:248
  7.9 67.3 %all-gather.13.cloned.1.call-start = ((), (), s32[]{:S(2)}) async-start(), calls=%async_computation.7 | async-start | bytes 2621440 | tf_op jit(solution)/shard_map/all_gather | solution.py:247
  12.2 14.7 %all-to-all-start = ((s32[32,1,2]{2,1,0:T(1,128)}), s32[32,1,2]{2,1,0:T(1,128)S(1)}, u32[]{:S(2)}, u32[]{:S(2)}) async-start(s32[32,1,2]{2,1,0:T(1,128)} %bitcast.9), calls=%async_computation | async-start | bytes 32768 | tf_op jit(solution)/shard_map/all_to_all | solution.py:271
  84.9 7.8 %copy-start.5 = (bf16[256,1024]{1,0:T(8,128)(2,1)S(1)}, bf16[256,1024]{1,0:T(8,128)(2,1)}, u32[]{:S(2)}) copy-start(bf16[256,1024]{1,0:T(8,128)(2,1)} %param.13) | copy-start | bytes 1572868
  84.9 59.2 %all-to-all-start.2 = ((bf16[32,2,128,256]{3,2,1,0:T(8,128)(2,1)}), bf16[32,2,128,256]{3,2,1,0:T(8,128)(2,1)}, u32[]{:S(2)}, u32[]{:S(2)}) async-start(bf16[32,2,128,256]{3,2,1,0:T(8,128)(2,1)} %get-tuple-element.62), calls=%async_computation.2 | async-start | bytes 8388608 | tf_op jit(solution)/shard_map/all_to_all | solution.py:291
  92.7 63.1 %all-gather.9.cloned.1.call-start = ((), (), s32[]{:S(2)}) async-start(), calls=%async_computation.5 | async-start | bytes 2621440 | tf_op jit(solution)/shard_map/all_gather | solution.py:246
  144.1 7.5 %copy-start.6 = (bf16[256,1024]{1,0:T(8,128)(2,1)S(1)}, bf16[256,1024]{1,0:T(8,128)(2,1)}, u32[]{:S(2)}) copy-start(bf16[256,1024]{1,0:T(8,128)(2,1)} %param.16) | copy-start | bytes 1572868
  144.1 11.4 %copy-start.7 = (s32[4,8,16]{2,1,0:T(8,128)S(1)}, s32[4,8,16]{2,1,0:T(8,128)}, u32[]{:S(2)}) copy-start(s32[4,8,16]{2,1,0:T(8,128)} %param.21) | copy-start | bytes 6148
  144.1 11.5 %copy-start.8 = (s32[8,11]{1,0:T(8,128)S(1)}, s32[8,11]{1,0:T(8,128)}, u32[]{:S(2)}) copy-start(s32[8,11]{1,0:T(8,128)} %param.19) | copy-start | bytes 1060
  144.1 93.0 %all-to-all-start.1 = ((bf16[32,2,128,256]{3,2,1,0:T(8,128)(2,1)}), bf16[32,2,128,256]{3,2,1,0:T(8,128)(2,1)}, u32[]{:S(2)}, u32[]{:S(2)}) async-start(bf16[32,2,128,256]{3,2,1,0:T(8,128)(2,1)} %get-tuple-element.63), calls=%async_computation.1 | async-start | bytes 8388608 | tf_op jit(solution)/shard_map/all_to_all | solution.py:284
  151.6 36.6 %all-gather.11.cloned.1.call-start = ((), (), s32[]{:S(2)}) async-start(), calls=%async_computation.6 | async-start | bytes 2621440 | tf_op jit(solution)/shard_map/all_gather | solution.py:249
  152.7 415.0 %all-gather.19.cloned.1.call-start = ((), (), s32[]{:S(2)}) async-start(), calls=%async_computation.10 | async-start | bytes 2621440 | tf_op jit(solution)/shard_map/all_gather | solution.py:392
  153.8 52.0 %collective-permute-start = (bf16[4,2,128,256]{3,2,0,1:T(8,128)(2,1)}, bf16[4,2,128,256]{3,2,0,1:T(8,128)(2,1)}, u32[]{:S(2)}, u32[]{:S(2)}) collective-permute-start(bf16[4,2,128,256]{3,2,0,1:T(8,128)(2,1)} %get-tuple-element.60), channel_id=1, source_target_pairs={{0,4},{4,8},{8,12},{12,16},{16,20},{20,24},{24,28},{28,32},{32,36}... | collective-permute-start | bytes 1572872 | tf_op jit(solution)/shard_map/ppermute | solution.py:28
  153.9 51.9 %collective-permute-start.1 = (bf16[4,2,128,256]{3,2,0,1:T(8,128)(2,1)}, bf16[4,2,128,256]{3,2,0,1:T(8,128)(2,1)}, u32[]{:S(2)}, u32[]{:S(2)}) collective-permute-start(bf16[4,2,128,256]{3,2,0,1:T(8,128)(2,1)} %get-tuple-element.61), channel_id=1, source_target_pairs={{4,0},{8,4},{12,8},{16,12},{20,16},{24,20},{28,24},{32,28},{36,32}... | collective-permute-start | bytes 1572872 | tf_op jit(solution)/shard_map/ppermute | solution.py:31
  272.1 10.2 %copy-start.1 = (s32[8]{0:T(128)S(1)}, s32[8]{0:T(128)}, u32[]{:S(2)}) copy-start(s32[8]{0:T(128)} %count_ref.1) | copy-start | bytes 100
  428.6 1.0 copy-start
  437.7 60.2 %all-to-all-start.3 = ((bf16[32,2,128,256]{2,3,1,0:T(8,128)(2,1)}), bf16[32,2,128,256]{2,3,1,0:T(8,128)(2,1)}, u32[]{:S(2)}, u32[]{:S(2)}) async-start(bf16[32,2,128,256]{2,3,1,0:T(8,128)(2,1)} %bitcast.90), calls=%async_computation.3 | async-start | bytes 8388608 | tf_op jit(solution)/shard_map/all_to_all | solution.py:350
  446.4 123.3 %all-gather.17.cloned.1.call-start = ((), (), s32[]{:S(2)}) async-start(), calls=%async_computation.9 | async-start | bytes 2621440 | tf_op jit(solution)/shard_map/all_gather | solution.py:391
  447.8 2.2 copy-start.4
  450.2 1.5 copy-start.2
  451.7 55.2 %collective-permute-start.2 = (bf16[4,2,128,256]{2,3,0,1:T(8,128)(2,1)}, bf16[4,2,128,256]{2,3,0,1:T(8,128)(2,1)}, u32[]{:S(2)}, u32[]{:S(2)}) collective-permute-start(bf16[4,2,128,256]{2,3,0,1:T(8,128)(2,1)} %get-tuple-element.57), channel_id=1, source_target_pairs={{124,0},{0,4},{4,8},{8,12},{12,16},{16,20},{20,24},{24,28},{28,32}... | collective-permute-start | bytes 1572872 | tf_op jit(solution)/shard_map/ppermute | solution.py:39
  451.9 56.6 %collective-permute-start.3 = (bf16[4,2,128,256]{2,3,0,1:T(8,128)(2,1)S(1)}, bf16[4,2,128,256]{2,3,0,1:T(8,128)(2,1)S(1)}, u32[]{:S(2)}, u32[]{:S(2)}) collective-permute-start(bf16[4,2,128,256]{2,3,0,1:T(8,128)(2,1)S(1)} %get-tuple-element.56), channel_id=1, source_target_pairs={{4,0},{8,4},{12,8},{16,12},{20,16},{24,20},{28,24},{32,28},{36,32}... | collective-permute-start | bytes 1572872 | tf_op jit(solution)/shard_map/ppermute | solution.py:39
  497.9 59.0 %all-to-all-start.4 = ((bf16[32,2,128,256]{2,3,1,0:T(8,128)(2,1)}), bf16[32,2,128,256]{2,3,1,0:T(8,128)(2,1)}, u32[]{:S(2)}, u32[]{:S(2)}) async-start(bf16[32,2,128,256]{2,3,1,0:T(8,128)(2,1)} %bitcast.89), calls=%async_computation.4 | async-start | bytes 8388608 | tf_op jit(solution)/shard_map/all_to_all | solution.py:353
  505.4 66.4 %all-gather.21.cloned.1.call-start = ((), (), s32[]{:S(2)}) async-start(), calls=%async_computation.11 | async-start | bytes 2621440 | tf_op jit(solution)/shard_map/all_gather | solution.py:393
  505.4 1.9 copy-start.3
  520.1 79.0 %all-gather.23.cloned.1.call-start = ((), (), s32[]{:S(2)}) async-start(), calls=%async_computation.12 | async-start | bytes 2621440 | tf_op jit(solution)/shard_map/all_gather | solution.py:394
Sparse Core Ops, SparseCore 0:
  9.6 33.0 all-gather.14
  44.4 30.7 all-gather.12
  95.7 33.7 all-gather.8
  154.3 33.8 all-gather.10
  432.2 31.8 all-gather.18
  466.2 30.7 all-gather.16
  520.3 33.8 all-gather.20
  567.7 31.3 all-gather.22

commit v3 on v2

--- a/solution.py
+++ b/solution.py
@@ -71,11 +71,12 @@
     rows_ref, count_ref, seed_ref, q_ref, g_ref, kt_ref, vt_ref,
     att_ref, qg_ref, nk_ref, nv_ref, fk_ref, fv_ref,
     s_scr, keep_scr, drop_scr,
-    *, scale, near_count, slot_count, blocks, use_hash=True,
+    *, scale, near_count, slot_count, blocks, head_size,
 ):
-    h = pl.program_id(0)
+    p = pl.program_id(0)
     c = pl.program_id(1)
-    head_size = q_ref.shape[-1]
+    width = q_ref.shape[-1]
+    pair = width // head_size
 
     @pl.when(c == 0)
     def _():
@@ -84,126 +85,134 @@
         fk_ref[...] = jnp.zeros_like(fk_ref)
         fv_ref[...] = jnp.zeros_like(fv_ref)
 
-    q = q_ref[0] * jnp.asarray(scale, q_ref.dtype)
-    g = g_ref[0]
+    q = q_ref[...] * jnp.asarray(scale, q_ref.dtype)
+    g = g_ref[...]
+    lane_head = lax.broadcasted_iota(jnp.int32, (BS, width), 1) // head_size
+    row_head = lax.broadcasted_iota(jnp.int32, (width, BS), 0) // head_size
+    zero = jnp.zeros((), q.dtype)
+    q_parts = [jnp.where(lane_head == a, q, zero) for a in range(pair)]
+    g_parts = [jnp.where(lane_head == a, g, zero) for a in range(pair)]
     q_t = q.T
     g_t = g.T
     base = c * slot_count
-    seed_base = (h * blocks + c) * slot_count
+    seed_base = [((p * pair + a) * blocks + c) * slot_count for a in range(pair)]
     live_end = L + 1 + count_ref[c]
 
     def start_of(j):
         return pl.multiple_of(rows_ref[base + j] * BS, BS)
 
     def keys(j):
-        return kt_ref[0, pl.ds(start_of(j), BS), :]
+        return kt_ref[pl.ds(start_of(j), BS), :]
 
     def values(j):
-        return vt_ref[0, pl.ds(start_of(j), BS), :]
-
-    def score_pass(j, m):
-        s = lax.dot_general(
-            q, keys(j), (((1,), (1,)), ((), ())), preferred_element_type=jnp.float32
-        )
-        if j > L:
-            s = jnp.where(j < live_end, s, MASKED)
-        s_scr[j] = s
-        return jnp.maximum(m, s)
-
-    m = unrolled(score_pass, jnp.full((BS, BS), -jnp.inf, jnp.float32), 0, slot_count)
-    m = jnp.max(m, axis=1, keepdims=True)
-
-    def exp_pass(j, total):
-        e = jnp.exp(s_scr[j] - m)
-        s_scr[j] = e
-        return total + e
-
-    total = unrolled(exp_pass, jnp.zeros((BS, BS), jnp.float32), 0, slot_count)
-    inv = 1.0 / jnp.sum(total, axis=1, keepdims=True)
+        return vt_ref[pl.ds(start_of(j), BS), :]
+
+    def pick(parts, heads):
+        out = parts[-1]
+        for a in range(pair - 1):
+            out = jnp.where(heads == a, parts[a], out)
+        return out
+
+    nt = (((1,), (1,)), ((), ()))
+    f32 = jnp.float32
+    m = [jnp.full((BS, BS), -jnp.inf, f32) for _ in range(pair)]
+    for j in range(slot_count):
+        k = keys(j)
+        for a in range(pair):
+            s = lax.dot_general(q_parts[a], k, nt, preferred_element_type=f32)
+            if j > L:
+                s = jnp.where(j < live_end, s, MASKED)
+            s_scr[a, j] = s
+            m[a] = jnp.maximum(m[a], s)
+    m = [jnp.max(x, axis=1, keepdims=True) for x in m]
+    total = [jnp.zeros((BS, BS), f32) for _ in range(pair)]
+    for j in range(slot_count):
+        for a in range(pair):
+            e = jnp.exp(s_scr[a, j] - m[a])
+            s_scr[a, j] = e
+            total[a] = total[a] + e
+    inv = [1.0 / jnp.sum(x, axis=1, keepdims=True) for x in total]
     offs = (
         lax.broadcasted_iota(jnp.int32, (BS, BS), 0) * BS
         + lax.broadcasted_iota(jnp.int32, (BS, BS), 1)
     )
-
-    def drop_pass(j, acc):
-        att = s_scr[j] * inv
-        s_scr[j] = att
-        if use_hash:
-            word = seed_ref[seed_base + j] * 40503 + offs
+    acc = [jnp.zeros((BS, width), f32) for _ in range(pair)]
+    for j in range(slot_count):
+        v = values(j)
+        for a in range(pair):
+            att = s_scr[a, j] * inv[a]
+            s_scr[a, j] = att
+            word = seed_ref[seed_base[a] + j] * 40503 + offs
             word = word ^ srl(word, 15)
             word = word * 739982445
             word = word ^ srl(word, 12)
             word = word * 695872825
             word = word ^ srl(word, 15)
-            keep = jnp.where((word & 1023) >= KEEP_LEVEL, KEEP_GAIN, 0.0).astype(jnp.float32)
+            keep = jnp.where((word & 1023) >= KEEP_LEVEL, KEEP_GAIN, 0.0).astype(f32)
+            keep_scr[a, j] = keep
+            dropped = (att * keep).astype(jnp.bfloat16)
+            drop_scr[a, j] = dropped
+            acc[a] = acc[a] + jnp.dot(dropped, v, preferred_element_type=f32)
+    attended = pick(acc, lane_head)
+    att_ref[...] = attended.astype(att_ref.dtype)
+    spread = g.astype(f32) * attended
+    delta = [
+        jnp.sum(jnp.where(lane_head == a, spread, 0.0), axis=1, keepdims=True) for a in range(pair)
+    ]
+    qacc = [jnp.zeros((BS, width), f32) for _ in range(pair)]
+    for j in range(slot_count):
+        k = keys(j)
+        v = values(j)
+        kps, vps = [], []
+        for a in range(pair):
+            dg = lax.dot_general(g_parts[a], v, nt, preferred_element_type=f32)
+            sg = (s_scr[a, j] * (dg * keep_scr[a, j] - delta[a])).astype(jnp.bfloat16)
+            qacc[a] = qacc[a] + jnp.dot(sg, k, preferred_element_type=f32)
+            kps.append(jnp.dot(q_t, sg, preferred_element_type=f32))
+            vps.append(jnp.dot(g_t, drop_scr[a, j], preferred_element_type=f32))
+        kp = pick(kps, row_head)
+        vp = pick(vps, row_head)
+        at = rows_ref[base + j]
+        if j <= L:
+            nk_ref[at] += kp
+            nv_ref[at] += vp
         else:
-            keep = jnp.where(offs >= seed_ref[seed_base + j], KEEP_GAIN, 0.0).astype(jnp.float32)
-        keep_scr[j] = keep
-        dropped = (att * keep).astype(jnp.bfloat16)
-        drop_scr[j] = dropped
-        return acc + jnp.dot(dropped, values(j), preferred_element_type=jnp.float32)
-
-    acc = unrolled(drop_pass, jnp.zeros((BS, head_size), jnp.float32), 0, slot_count)
-    att_ref[0] = acc.astype(att_ref.dtype)
-    delta = jnp.sum(g.astype(jnp.float32) * acc, axis=1, keepdims=True)
-
-    def grad_terms(j, qacc):
-        dg = lax.dot_general(
-            g, values(j), (((1,), (1,)), ((), ())), preferred_element_type=jnp.float32
-        )
-        sg = (s_scr[j] * (dg * keep_scr[j] - delta)).astype(jnp.bfloat16)
-        qacc = qacc + jnp.dot(sg, keys(j), preferred_element_type=jnp.float32)
-        kp = jnp.dot(q_t, sg, preferred_element_type=jnp.float32)
-        vp = jnp.dot(g_t, drop_scr[j], preferred_element_type=jnp.float32)
-        return qacc, kp, vp
-
-    def near_pass(j, qacc):
-        qacc, kp, vp = grad_terms(j, qacc)
-        at = rows_ref[base + j]
-        nk_ref[0, at] += kp
-        nv_ref[0, at] += vp
-        return qacc
-
-    def far_pass(j, qacc):
-        qacc, kp, vp = grad_terms(j, qacc)
-        at = rows_ref[base + j] - near_count
-        fk_ref[0, at] = kp.astype(fk_ref.dtype)
-        fv_ref[0, at] = vp.astype(fv_ref.dtype)
-        return qacc
-
-    qacc = unrolled(near_pass, jnp.zeros((BS, head_size), jnp.float32), 0, L + 1)
-    qacc = unrolled(far_pass, qacc, L + 1, slot_count)
-    qg_ref[0] = (qacc * scale).astype(qg_ref.dtype)
-
-
-def block_attention(rows, counts, seeds, q, g, kt, vt, *, near_count, far_count, scale, use_hash=True):
-    heads, row_count, head_size = q.shape
+            fk_ref[at - near_count] = kp.astype(fk_ref.dtype)
+            fv_ref[at - near_count] = vp.astype(fv_ref.dtype)
+    qg_ref[...] = (pick(qacc, lane_head) * scale).astype(qg_ref.dtype)
+
+
+def block_attention(rows, counts, seeds, q, g, kt, vt, *, near_count, far_count, scale, head_size):
+    row_count, local_width = q.shape
+    width = 2 * head_size
+    groups = local_width // width
     blocks = row_count // BS
     slot_count = 1 + L + E
     kernel = functools.partial(
         attention_kernel, scale=scale, near_count=near_count, slot_count=slot_count,
-        blocks=blocks, use_hash=use_hash,
-    )
-    q_spec = pl.BlockSpec((1, BS, head_size), lambda h, c, *_: (h, c, 0))
-    table_spec = pl.BlockSpec((1, kt.shape[1], head_size), lambda h, c, *_: (h, 0, 0))
-    near_spec = pl.BlockSpec((1, near_count, head_size, BS), lambda h, c, *_: (h, 0, 0, 0))
-    far_spec = pl.BlockSpec((1, far_count, head_size, BS), lambda h, c, *_: (h, 0, 0, 0))
+        blocks=blocks, head_size=head_size,
+    )
+    q_spec = pl.BlockSpec((BS, width), lambda p, c, *_: (c, p))
+    table_spec = pl.BlockSpec((kt.shape[0], width), lambda p, c, *_: (0, p))
+    near_spec = pl.BlockSpec((near_count, width, BS), lambda p, c, *_: (0, p, 0))
+    far_spec = pl.BlockSpec((far_count, width, BS), lambda p, c, *_: (0, p, 0))
     grid_spec = pltpu.PrefetchScalarGridSpec(
         num_scalar_prefetch=3,
-        grid=(heads, blocks),
+        grid=(groups, blocks),
         in_specs=[q_spec, q_spec, table_spec, table_spec],
         out_specs=[q_spec, q_spec, near_spec, near_spec, far_spec, far_spec],
         scratch_shapes=[
-            pltpu.VMEM((slot_count, BS, BS), jnp.float32),
-            pltpu.VMEM((slot_count, BS, BS), jnp.float32),
-            pltpu.VMEM((slot_count, BS, BS), jnp.bfloat16),
+            pltpu.VMEM((2, slot_count, BS, BS), jnp.float32),
+            pltpu.VMEM((2, slot_count, BS, BS), jnp.float32),
+            pltpu.VMEM((2, slot_count, BS, BS), jnp.bfloat16),
         ],
     )
-    flops = 6 * 2 * heads * blocks * slot_count * BS * BS * head_size
+    heads = local_width // head_size
+    flops = 6 * 2 * heads * blocks * slot_count * BS * BS * width
     cost = pl.CostEstimate(
         flops=flops,
         transcendentals=heads * blocks * slot_count * BS * BS,
-        bytes_accessed=2 * (q.size * 4 + kt.size * 2) + 4 * heads * (near_count + far_count) * BS * head_size * 2,
+        bytes_accessed=2 * (q.size * 4 + kt.size * 2) + 4 * (near_count + far_count) * BS * local_width * 2,
     )
     return pl.pallas_call(
         kernel,
@@ -211,10 +220,10 @@
         out_shape=[
             jax.ShapeDtypeStruct(q.shape, jnp.bfloat16),
             jax.ShapeDtypeStruct(q.shape, jnp.bfloat16),
-            jax.ShapeDtypeStruct((heads, near_count, head_size, BS), jnp.float32),
-            jax.ShapeDtypeStruct((heads, near_count, head_size, BS), jnp.float32),
-            jax.ShapeDtypeStruct((heads, far_count, head_size, BS), jnp.bfloat16),
-            jax.ShapeDtypeStruct((heads, far_count, head_size, BS), jnp.bfloat16),
+            jax.ShapeDtypeStruct((near_count, local_width, BS), jnp.float32),
+            jax.ShapeDtypeStruct((near_count, local_width, BS), jnp.float32),
+            jax.ShapeDtypeStruct((far_count, local_width, BS), jnp.bfloat16),
+            jax.ShapeDtypeStruct((far_count, local_width, BS), jnp.bfloat16),
         ],
         compiler_params=pltpu.CompilerParams(
             dimension_semantics=("arbitrary", "arbitrary"), vmem_limit_bytes=48 * 1024 * 1024
@@ -315,44 +324,24 @@
     seed_flat = drop_seed.reshape(-1).astype(jnp.int32)
     table_count = key_table.shape[0]
 
-    def head_major(rows):
-        return rows.reshape(-1, local_heads, head_size).transpose(1, 0, 2)
-
     att_out, qg_out, nk, nv, fk, fv = block_attention(
         slot_rows,
         live_count.astype(jnp.int32),
         seed_flat,
-        head_major(query_local),
-        head_major(grad_local),
-        head_major(key_table.reshape(table_count * BS, local_width)),
-        head_major(value_table.reshape(table_count * BS, local_width)),
+        query_local,
+        grad_local,
+        key_table.reshape(table_count * BS, local_width),
+        value_table.reshape(table_count * BS, local_width),
         near_count=near_count,
         far_count=far_total_count,
         scale=score_scale,
-    )
-
-    def row_major(arr, count):
-        return arr.reshape(local_heads, count, BS, head_size).transpose(1, 2, 0, 3).reshape(
-            count, BS, local_width
-        )
-
-    def from_columns(arr, count):
-        return arr.transpose(1, 3, 0, 2).reshape(count, BS, local_width)
-
-    near_total = jnp.stack([from_columns(nk, near_count), from_columns(nv, near_count)], axis=1)
-    far_key_total = from_columns(fk, far_total_count)
-    far_value_total = from_columns(fv, far_total_count)
-    outputs = (
-        row_major(att_out, QB_DEV),
-        row_major(qg_out, QB_DEV),
-    )
+        head_size=head_size,
+    )
+    outputs = (att_out, qg_out)
+    column_shape = (peer_count, capacity, local_width, BS)
     back_key, back_value = (
-        lax.all_to_all(
-            far_key_total.reshape(reply_shape), "blk", split_axis=0, concat_axis=0, tiled=True
-        ),
-        lax.all_to_all(
-            far_value_total.reshape(reply_shape), "blk", split_axis=0, concat_axis=0, tiled=True
-        ),
+        lax.all_to_all(fk.reshape(column_shape), "blk", split_axis=0, concat_axis=0, tiled=True),
+        lax.all_to_all(fv.reshape(column_shape), "blk", split_axis=0, concat_axis=0, tiled=True),
     )
     owner_match = (
         jnp.arange(QB_DEV, dtype=jnp.int32)[:, None] == wanted_here.reshape(1, -1)
@@ -361,12 +350,13 @@
         owner_match,
         back_key.reshape(far_total_count, BS * local_width),
         preferred_element_type=jnp.float32,
-    )
+    ).reshape(QB_DEV, local_width, BS)
     far_value_sum = jnp.dot(
         owner_match,
         back_value.reshape(far_total_count, BS * local_width),
         preferred_element_type=jnp.float32,
-    )
+    ).reshape(QB_DEV, local_width, BS)
+    near_total = jnp.stack([nk, nv], axis=1)
     from_below = shifted(near_total[QB_DEV + W :].astype(jnp.bfloat16), "blk", 1).astype(
         jnp.float32
     )
@@ -375,12 +365,8 @@
     own_total = own_total.at[:W].add(from_below)
     own_total = own_total.at[QB_DEV - W :].add(from_above)
     block_rows = QB_DEV * BS
-    key_grad = (own_total[:, 0].reshape(QB_DEV, BS * local_width) + far_key_sum).astype(
-        jnp.bfloat16
-    )
-    value_grad = (own_total[:, 1].reshape(QB_DEV, BS * local_width) + far_value_sum).astype(
-        jnp.bfloat16
-    )
+    key_grad = (own_total[:, 0] + far_key_sum).astype(jnp.bfloat16).transpose(0, 2, 1)
+    value_grad = (own_total[:, 1] + far_value_sum).astype(jnp.bfloat16).transpose(0, 2, 1)
     results = (
         outputs[0].reshape(block_rows, local_width),
         outputs[1].reshape(block_rows, local_width),

time: 611 us -> 572 us (0.936)
  local copies, waits for them, and re-layouts: 126 us -> 24.2 us
  waiting for transfers between devices: 247 us -> 314 us
  Pallas kernels: 146 us -> 135 us
    ppermute x2, waiting for transfers between devices: 0.01 us -> 46 us  [shifted(): return lax.ppermute(block, axis, route)]
    another operation x4 -> x0, local copies, waits for them, and re-layouts: 36.5 us -> none  [head_major(): return rows.reshape(-1, local_heads, head_size).transpose(1, 0, 2)]
    all_gather x1, waiting for transfers between devices: 0.01 us -> 34.7 us  [on_device(): lax.all_gather(results[2], 'head', axis=1, tiled=True)]
    all_to_all x2, waiting for transfers between devices: 74.9 us -> 50.8 us  [the longest x1 50.8 us: on_device(): lax.all_to_all(fk.reshape(column_shape), 'blk', split_axis=0, concat_axis...]
    all_to_all x2 -> x0, local copies, waits for them, and re-layouts: 22.6 us -> none  [the longest x1 11.3 us: on_device(): lax.all_to_all(jnp.where(asked_mask, value_blocks[chosen], zero_block).re...]
    unnamed x27 -> x9, local copies, waits for them, and re-layouts: 21.9 us -> 0.78 us
    transpose x4 -> x2, local copies, waits for them, and re-layouts: 13.4 us -> 2.04 us  [the longest x1 1.03 us: on_device(): (own_total[:, 1] + far_value_sum).astype(jnp.bfloat16).transpose(0, 2, 1)]
    pallas_call x1, Pallas kernels: 146 us -> 135 us  [block_attention(): pl.pallas_call(kernel, grid_spec=grid_spec, out_shape=[jax.ShapeDtypeStru...]
  transfers between devices with their start and end apart: 17 -> 17, of which waited for: 9 -> 10; matrix products, arithmetic and copies ran while one was open for 16% -> 8% of each run, Pallas kernels for 0% -> 0%
where the time goes in v3:
time: 572 us; the launch traced here: 571 us
  waiting for transfers between devices  314 us (55%)
  Pallas kernels  135 us (24%)
  starting transfers between devices  43.5 us (8%)
  other arithmetic  30.7 us (5%)
  local copies, waits for them, and re-layouts  24.2 us (4%)
  between operations  14.3 us (2%)
  matrix products  9.01 us (2%)
    pallas_call x1, Pallas kernels, block_attention(): pl.pallas_call(kernel, grid_spec=grid_spec, out_shape=[jax.ShapeDtypeStru...  135 us
    all_to_all x1, waiting for transfers between devices, on_device(): lax.all_to_all(fk.reshape(column_shape), 'blk', split_axis=0, concat_axis...  50.8 us
    all_to_all x1, waiting for transfers between devices, on_device(): lax.all_to_all(jnp.where(asked_mask, value_blocks[chosen], zero_block).re...  50.7 us
    ppermute x2, waiting for transfers between devices, shifted(): return lax.ppermute(block, axis, route)  46 us
    all_gather x1, waiting for transfers between devices, on_device(): lax.all_gather(results[2], 'head', axis=1, tiled=True)  34.7 us
    all_gather x1, waiting for transfers between devices, on_device(): lax.all_gather(results[3], 'head', axis=1, tiled=True)  30.3 us
    all_gather x1, waiting for transfers between devices, on_device(): lax.all_gather(out_grad, 'head', axis=0, tiled=True)  29 us
    all_gather x1, waiting for transfers between devices, on_device(): lax.all_gather(key_rows, 'head', axis=0, tiled=True)  28.5 us
  transfers between devices with their start and end apart: 17, of which 10 were waited for; matrix products, arithmetic and copies ran while one was open for 8% of the time, Pallas kernels for 0%

profile of v3, /device:TPU:8, one launch (start us, length us, event | category | flops | bytes accessed | tf_op | source)
XLA Modules:
  0.0 570.8 jit_solution(9410605847358646469)
XLA Ops:
  12.2 8.5 %all-to-all-start = ((s32[32,1,2]{2,1,0:T(1,128)}), s32[32,1,2]{2,1,0:T(1,128)S(1)}, u32[]{:S(2)}, u32[]{:S(2)}) async-start(s32[32,1,2]{2,1,0:T(1,128)} %bitcast.5), calls=%async_computation | async-start | bytes 32768 | tf_op jit(solution)/shard_map/all_to_all | solution.py:280
  20.8 6.1 %all-to-all-done = s32[32,1,2]{2,1,0:T(1,128)S(1)} async-done(((s32[32,1,2]{2,1,0:T(1,128)}), s32[32,1,2]{2,1,0:T(1,128)S(1)}, u32[]{:S(2)}, u32[]{:S(2)}) %all-to-all-start) | async-done | bytes 288 | tf_op jit(solution)/shard_map/all_to_all | solution.py:280
  28.5 14.2 %all-gather.15.cloned.1.call-done = bf16[1024,1024]{1,0:T(8,128)(2,1)} async-done(((bf16[256,1024]{1,0:T(8,128)(2,1)}), bf16[1024,1024]{1,0:T(8,128)(2,1)}) %all-gather.15.cloned.1.call-update) | async-done | bytes 2097168 | tf_op jit(solution)/shard_map/all_gather | solution.py:257
  43.8 2.9 gather_fusion.1
  46.7 28.5 %all-gather.13.cloned.1.call-done = bf16[1024,1024]{1,0:T(8,128)(2,1)} async-done(((bf16[256,1024]{1,0:T(8,128)(2,1)}), bf16[1024,1024]{1,0:T(8,128)(2,1)}) %all-gather.13.cloned.1.call-update) | async-done | bytes 2097168 | tf_op jit(solution)/shard_map/all_gather | solution.py:256
  76.3 2.8 gather_fusion
  79.1 5.9 %broadcast_select_fusion = (bf16[32,2,128,256]{3,2,1,0:T(8,128)(2,1)}, bf16[32,2,128,256]{3,2,1,0:T(8,128)(2,1)}) fusion(bf16[32,2,128,256]{3,2,1,0:T(8,128)(2,1)} %bitcast.95, pred[32,2]{1,0:T(8,128)(4,1)S(1)} %copy.36, bf16[32,2,128,256]{3,2,1,0:T(8,128)(2,1)} %bitcast.96), kind=kLoop, calls=%fused_computation.19 | loop fusion | flops 4194304 | bytes 16777280 | tf_op jit(solution)/shard_map/jit(_where)/select_n | solution.py:301
  85.0 7.6 %all-to-all-start.2 = ((bf16[32,2,128,256]{3,2,1,0:T(8,128)(2,1)}), bf16[32,2,128,256]{3,2,1,0:T(8,128)(2,1)}, u32[]{:S(2)}, u32[]{:S(2)}) async-start(bf16[32,2,128,256]{3,2,1,0:T(8,128)(2,1)} %get-tuple-element.50), calls=%async_computation.2 | async-start | bytes 8388608 | tf_op jit(solution)/shard_map/all_to_all | solution.py:300
  93.4 50.7 %all-to-all-done.2 = bf16[32,2,128,256]{3,2,1,0:T(8,128)(2,1)} async-done(((bf16[32,2,128,256]{3,2,1,0:T(8,128)(2,1)}), bf16[32,2,128,256]{3,2,1,0:T(8,128)(2,1)}, u32[]{:S(2)}, u32[]{:S(2)}) %all-to-all-start.2) | async-done | bytes 4194336 | tf_op jit(solution)/shard_map/all_to_all | solution.py:300
  144.0 7.3 %all-to-all-start.1 = ((bf16[32,2,128,256]{3,2,1,0:T(8,128)(2,1)}), bf16[32,2,128,256]{3,2,1,0:T(8,128)(2,1)}, u32[]{:S(2)}, u32[]{:S(2)}) async-start(bf16[32,2,128,256]{3,2,1,0:T(8,128)(2,1)} %get-tuple-element.51), calls=%async_computation.1 | async-start | bytes 8388608 | tf_op jit(solution)/shard_map/all_to_all | solution.py:293
  155.3 29.0 %all-gather.11.cloned.1.call-done = bf16[1024,1024]{1,0:T(8,128)(2,1)} async-done(((bf16[256,1024]{1,0:T(8,128)(2,1)}), bf16[1024,1024]{1,0:T(8,128)(2,1)}) %all-gather.11.cloned.1.call-update) | async-done | bytes 2097168 | tf_op jit(solution)/shard_map/all_gather | solution.py:258
  185.3 20.2 %collective-permute-done = bf16[4,2,128,256]{3,2,0,1:T(8,128)(2,1)} collective-permute-done((bf16[4,2,128,256]{3,2,0,1:T(8,128)(2,1)S(1)}, bf16[4,2,128,256]{3,2,0,1:T(8,128)(2,1)}, u32[]{:S(2)}, u32[]{:S(2)}) %collective-permute-start) | collective-permute-done | bytes 524320 | tf_op jit(solution)/shard_map/ppermute | solution.py:28
  207.2 5.0 pad_maximum_fusion.2
  212.2 5.0 pad_maximum_fusion.1
  217.3 134.9 %shard_map.120 = (bf16[1024,256]{1,0:T(8,128)(2,1)}, bf16[1024,256]{1,0:T(8,128)(2,1)}, f32[16,256,128]{2,1,0:T(8,128)S(1)}, f32[16,256,128]{2,1,0:T(8,128)}, bf...) custom-call(s32[128]{0:T(128)S(1)} %reshape.216.rows_ref, s32[8]{0:T(128)S(1)} %copy-done, ...), custom_call_target="tpu_custom_call" | custom-call | flops 12884901888 | bytes 33554432 | tf_op jit(solution)/shard_map/pallas_call | solution.py:217
  352.1 8.7 %all-to-all-start.3 = ((bf16[32,2,256,128]{3,2,1,0:T(8,128)(2,1)}), bf16[32,2,256,128]{3,2,1,0:T(8,128)(2,1)}, u32[]{:S(2)}, u32[]{:S(2)}) async-start(bf16[32,2,256,128]{3,2,1,0:T(8,128)(2,1)} %bitcast.100), calls=%async_computation.3 | async-start | bytes 8388608 | tf_op jit(solution)/shard_map/all_to_all | solution.py:343
  361.4 50.8 %all-to-all-done.3 = bf16[32,2,256,128]{3,2,1,0:T(8,128)(2,1)} async-done(((bf16[32,2,256,128]{3,2,1,0:T(8,128)(2,1)}), bf16[32,2,256,128]{3,2,1,0:T(8,128)(2,1)}, u32[]{:S(2)}, u32[]{:S(2)}) %all-to-all-start.3) | async-done | bytes 4194336 | tf_op jit(solution)/shard_map/all_to_all | solution.py:343
  412.2 7.5 %all-to-all-start.4 = ((bf16[32,2,256,128]{3,2,1,0:T(8,128)(2,1)}), bf16[32,2,256,128]{3,2,1,0:T(8,128)(2,1)}, u32[]{:S(2)}, u32[]{:S(2)}) async-start(bf16[32,2,256,128]{3,2,1,0:T(8,128)(2,1)} %bitcast.99), calls=%async_computation.4 | async-start | bytes 8388608 | tf_op jit(solution)/shard_map/all_to_all | solution.py:344
  420.3 1.9 fusion
  425.0 2.9 fusion.7
  427.9 46.0 %collective-permute-done.2 = bf16[4,2,256,128]{3,2,0,1:T(8,128)(2,1)} collective-permute-done((bf16[4,2,256,128]{3,2,0,1:T(8,128)(2,1)}, bf16[4,2,256,128]{3,2,0,1:T(8,128)(2,1)}, u32[]{:S(2)}, u32[]{:S(2)}) %collective-permute-start.2) | collective-permute-done | bytes 524320 | tf_op jit(solution)/shard_map/ppermute | solution.py:39
  473.9 2.1 fusion.10
  476.0 2.3 fusion.15
  478.3 4.5 fusion.4
  482.8 4.5 fusion.1
  487.3 2.0 fusion.18
  491.5 1.9 constant_dynamic-slice_fusion.3
  493.4 1.9 constant_dynamic-slice_fusion.2
  495.3 30.3 %all-gather.23.cloned.1.call-done = bf16[1024,1024]{1,0:T(8,128)(2,1)} async-done(((bf16[1024,256]{1,0:T(8,128)(2,1)}), bf16[1024,1024]{1,0:T(8,128)(2,1)}) %all-gather.23.cloned.1.call-update) | async-done | bytes 2097168 | tf_op jit(solution)/shard_map/all_gather | solution.py:380
  525.6 1.9 constant_dynamic-slice_fusion
  527.4 34.7 %all-gather.21.cloned.1.call-done = bf16[1024,1024]{1,0:T(8,128)(2,1)} async-done(((bf16[1024,256]{1,0:T(8,128)(2,1)}), bf16[1024,1024]{1,0:T(8,128)(2,1)}) %all-gather.21.cloned.1.call-update) | async-done | bytes 2097168 | tf_op jit(solution)/shard_map/all_gather | solution.py:379
  562.1 1.9 constant_dynamic-slice_fusion.1
  (74 shorter events, 22.2 us)
Async XLA Ops:
  7.2 35.6 %all-gather.15.cloned.1.call-start = ((), (), s32[]{:S(2)}) async-start(), calls=%async_computation.8 | async-start | bytes 2621440 | tf_op jit(solution)/shard_map/all_gather | solution.py:257
  7.9 67.3 %all-gather.13.cloned.1.call-start = ((), (), s32[]{:S(2)}) async-start(), calls=%async_computation.7 | async-start | bytes 2621440 | tf_op jit(solution)/shard_map/all_gather | solution.py:256
  12.2 14.7 %all-to-all-start = ((s32[32,1,2]{2,1,0:T(1,128)}), s32[32,1,2]{2,1,0:T(1,128)S(1)}, u32[]{:S(2)}, u32[]{:S(2)}) async-start(s32[32,1,2]{2,1,0:T(1,128)} %bitcast.5), calls=%async_computation | async-start | bytes 32768 | tf_op jit(solution)/shard_map/all_to_all | solution.py:280
  85.0 59.1 %all-to-all-start.2 = ((bf16[32,2,128,256]{3,2,1,0:T(8,128)(2,1)}), bf16[32,2,128,256]{3,2,1,0:T(8,128)(2,1)}, u32[]{:S(2)}, u32[]{:S(2)}) async-start(bf16[32,2,128,256]{3,2,1,0:T(8,128)(2,1)} %get-tuple-element.50), calls=%async_computation.2 | async-start | bytes 8388608 | tf_op jit(solution)/shard_map/all_to_all | solution.py:300
  92.6 61.6 %all-gather.9.cloned.1.call-start = ((), (), s32[]{:S(2)}) async-start(), calls=%async_computation.5 | async-start | bytes 2621440 | tf_op jit(solution)/shard_map/all_gather | solution.py:255
  144.0 68.2 %all-to-all-start.1 = ((bf16[32,2,128,256]{3,2,1,0:T(8,128)(2,1)}), bf16[32,2,128,256]{3,2,1,0:T(8,128)(2,1)}, u32[]{:S(2)}, u32[]{:S(2)}) async-start(bf16[32,2,128,256]{3,2,1,0:T(8,128)(2,1)} %get-tuple-element.51), calls=%async_computation.1 | async-start | bytes 8388608 | tf_op jit(solution)/shard_map/all_to_all | solution.py:293
  151.4 2.5 copy-start.3
  151.4 2.6 copy-start.2
  151.4 32.9 %all-gather.11.cloned.1.call-start = ((), (), s32[]{:S(2)}) async-start(), calls=%async_computation.6 | async-start | bytes 2621440 | tf_op jit(solution)/shard_map/all_gather | solution.py:258
  152.1 53.5 %collective-permute-start = (bf16[4,2,128,256]{3,2,0,1:T(8,128)(2,1)S(1)}, bf16[4,2,128,256]{3,2,0,1:T(8,128)(2,1)}, u32[]{:S(2)}, u32[]{:S(2)}) collective-permute-start(bf16[4,2,128,256]{3,2,0,1:T(8,128)(2,1)S(1)} %get-tuple-element.48), channel_id=1, source_target_pairs={{0,4},{4,8},{8,12},{12,16},{16,20},{20,24},{24,28},{28,32},{32,36}... | collective-permute-start | bytes 1572872 | tf_op jit(solution)/shard_map/ppermute | solution.py:28
  152.3 53.3 %collective-permute-start.1 = (bf16[4,2,128,256]{3,2,0,1:T(8,128)(2,1)S(1)}, bf16[4,2,128,256]{3,2,0,1:T(8,128)(2,1)}, u32[]{:S(2)}, u32[]{:S(2)}) collective-permute-start(bf16[4,2,128,256]{3,2,0,1:T(8,128)(2,1)S(1)} %get-tuple-element.49), channel_id=1, source_target_pairs={{4,0},{8,4},{12,8},{16,12},{20,16},{24,20},{28,24},{32,28},{36,32}... | collective-permute-start | bytes 1572872 | tf_op jit(solution)/shard_map/ppermute | solution.py:31
  212.2 5.0 copy-start
  352.1 60.1 %all-to-all-start.3 = ((bf16[32,2,256,128]{3,2,1,0:T(8,128)(2,1)}), bf16[32,2,256,128]{3,2,1,0:T(8,128)(2,1)}, u32[]{:S(2)}, u32[]{:S(2)}) async-start(bf16[32,2,256,128]{3,2,1,0:T(8,128)(2,1)} %bitcast.100), calls=%async_computation.3 | async-start | bytes 8388608 | tf_op jit(solution)/shard_map/all_to_all | solution.py:343
  360.8 130.7 %all-gather.17.cloned.1.call-start = ((), (), s32[]{:S(2)}) async-start(), calls=%async_computation.9 | async-start | bytes 2621440 | tf_op jit(solution)/shard_map/all_gather | solution.py:377
  412.2 70.6 %all-to-all-start.4 = ((bf16[32,2,256,128]{3,2,1,0:T(8,128)(2,1)}), bf16[32,2,256,128]{3,2,1,0:T(8,128)(2,1)}, u32[]{:S(2)}, u32[]{:S(2)}) async-start(bf16[32,2,256,128]{3,2,1,0:T(8,128)(2,1)} %bitcast.99), calls=%async_computation.4 | async-start | bytes 8388608 | tf_op jit(solution)/shard_map/all_to_all | solution.py:344
  419.7 73.7 %all-gather.19.cloned.1.call-start = ((), (), s32[]{:S(2)}) async-start(), calls=%async_computation.10 | async-start | bytes 2621440 | tf_op jit(solution)/shard_map/all_gather | solution.py:378
  420.3 105.3 %all-gather.23.cloned.1.call-start = ((), (), s32[]{:S(2)}) async-start(), calls=%async_computation.12 | async-start | bytes 2621440 | tf_op jit(solution)/shard_map/all_gather | solution.py:380
  423.2 50.7 %collective-permute-start.2 = (bf16[4,2,256,128]{3,2,0,1:T(8,128)(2,1)}, bf16[4,2,256,128]{3,2,0,1:T(8,128)(2,1)}, u32[]{:S(2)}, u32[]{:S(2)}) collective-permute-start(bf16[4,2,256,128]{3,2,0,1:T(8,128)(2,1)} %get-tuple-element.45), channel_id=1, source_target_pairs={{124,0},{0,4},{4,8},{8,12},{12,16},{16,20},{20,24},{24,28},{28,32}... | collective-permute-start | bytes 1572872 | tf_op jit(solution)/shard_map/ppermute | solution.py:39
  423.3 52.7 %collective-permute-start.3 = (bf16[4,2,256,128]{3,2,0,1:T(8,128)(2,1)S(1)}, bf16[4,2,256,128]{3,2,0,1:T(8,128)(2,1)S(1)}, u32[]{:S(2)}, u32[]{:S(2)}) collective-permute-start(bf16[4,2,256,128]{3,2,0,1:T(8,128)(2,1)S(1)} %get-tuple-element.44), channel_id=1, source_target_pairs={{4,0},{8,4},{12,8},{16,12},{20,16},{24,20},{28,24},{32,28},{36,32}... | collective-permute-start | bytes 1572872 | tf_op jit(solution)/shard_map/ppermute | solution.py:39
  425.0 48.9 %copy-start.1 = (f32[16,256,128]{2,1,0:T(8,128)S(1)}, f32[16,256,128]{2,1,0:T(8,128)}, u32[]{:S(2)}) copy-start(f32[16,256,128]{2,1,0:T(8,128)} %get-tuple-element.37) | copy-start | bytes 6291460
  490.4 71.7 %all-gather.21.cloned.1.call-start = ((), (), s32[]{:S(2)}) async-start(), calls=%async_computation.11 | async-start | bytes 2621440 | tf_op jit(solution)/shard_map/all_gather | solution.py:379
Sparse Core Ops, SparseCore 0:
  9.6 33.0 all-gather.14
  44.4 30.7 all-gather.12
  95.1 30.5 all-gather.8
  153.5 30.6 all-gather.10
  363.5 33.7 all-gather.16
  422.4 33.8 all-gather.18
  490.5 34.9 all-gather.22
  527.2 34.8 all-gather.20

commit v4 on v3

--- a/solution.py
+++ b/solution.py
@@ -251,16 +251,16 @@
     head_size = local_width // local_heads
     score_scale = head_size ** (-0.5)
     slot_count = 1 + L + E
-    gathered = (
-        lax.all_gather(query_rows, "head", axis=0, tiled=True),
-        lax.all_gather(key_rows, "head", axis=0, tiled=True),
-        lax.all_gather(value_rows, "head", axis=0, tiled=True),
-        lax.all_gather(out_grad, "head", axis=0, tiled=True),
-    )
-    first_col = head_index * local_width
-    query_local, key_local, value_local, grad_local = [
-        lax.dynamic_slice_in_dim(member, first_col, local_width, 1) for member in gathered
-    ]
+    exchanged = lax.all_to_all(
+        jnp.stack([query_rows, key_rows, value_rows, out_grad]),
+        "head",
+        split_axis=2,
+        concat_axis=1,
+        tiled=True,
+    )
+    query_local, key_local, value_local, grad_local = (
+        exchanged[0], exchanged[1], exchanged[2], exchanged[3]
+    )
     peer_count = lax.axis_size("blk")
     capacity = min(QB_DEV, max(2, (2 * QB_DEV * E + peer_count - 1) // peer_count))
     flat_device = expander_device.reshape(-1)
@@ -373,16 +373,8 @@
         key_grad.reshape(block_rows, local_width),
         value_grad.reshape(block_rows, local_width),
     )
-    full_results = (
-        lax.all_gather(results[0], "head", axis=1, tiled=True),
-        lax.all_gather(results[1], "head", axis=1, tiled=True),
-        lax.all_gather(results[2], "head", axis=1, tiled=True),
-        lax.all_gather(results[3], "head", axis=1, tiled=True),
-    )
-    first_row = head_index * share_rows
-    return tuple(
-        (lax.dynamic_slice_in_dim(member, first_row, share_rows, 0) for member in full_results)
-    )
+    returned = lax.all_to_all(jnp.stack(results), "head", split_axis=1, concat_axis=2, tiled=True)
+    return tuple(returned[i] for i in range(len(results)))
 
 
 def solution(mesh):

time: 572 us -> 501 us (0.88)
  waiting for transfers between devices: 314 us -> 125 us
  blocking collectives: 0 us -> 143 us
  starting transfers between devices: 43.5 us -> 28.3 us
  between operations: 14.3 us -> 0.86 us
  local copies, waits for them, and re-layouts: 24.2 us -> 31.5 us
    all_to_all x0 -> x3, blocking collectives: none -> 143 us  [the longest x1 58.4 us: on_device(): lax.all_to_all(fk.reshape(column_shape), 'blk', split_axis=0, concat_axis...]
    all_gather x8 -> x0, waiting for transfers between devices: 137 us -> none  [the longest x1 34.7 us: on_device(): lax.all_gather(results[2], 'head', axis=1, tiled=True)]
    all_to_all x2 -> x1, waiting for transfers between devices: 102 us -> 24.7 us  [on_device(): lax.all_to_all(jnp.stack([query_rows, key_rows, value_rows, out_grad]), '...]
    ppermute x1, waiting for transfers between devices: 20.2 us -> 51.9 us  [padded(): lax.ppermute(lax.slice_in_dim(block, block.shape[dim] - width, None, axis...]
    all_to_all x2 -> x1, starting transfers between devices: 16.3 us -> 4.29 us  [on_device(): lax.all_to_all(jnp.stack([query_rows, key_rows, value_rows, out_grad]), '...]
    dynamic_slice x8 -> x0, local copies, waits for them, and re-layouts: 11.8 us -> none  [the longest x4 7.48 us: on_device(): lax.dynamic_slice_in_dim(member, first_row, share_rows, 0)]
    slice x0 -> x6, local copies, waits for them, and re-layouts: none -> 7.5 us  [the longest x5 5.85 us: on_device(): return tuple((returned[i] for i in range(len(results))))]
    unnamed x9 -> x25, local copies, waits for them, and re-layouts: 0.78 us -> 7.08 us
  transfers between devices with their start and end apart: 17 -> 8, of which waited for: 10 -> 4; matrix products, arithmetic and copies ran while one was open for 8% -> 5% of each run, Pallas kernels for 0% -> 0%
where the time goes in v4:
time: 501 us
  blocking collectives  143 us (29%)
  Pallas kernels  135 us (27%)
  waiting for transfers between devices  125 us (25%)
  local copies, waits for them, and re-layouts  31.5 us (6%)
  other arithmetic  30 us (6%)
  starting transfers between devices  28.3 us (6%)
  matrix products  6.83 us (1%)
    pallas_call x1, Pallas kernels, block_attention(): pl.pallas_call(kernel, grid_spec=grid_spec, out_shape=[jax.ShapeDtypeStru...  135 us
    all_to_all x1, blocking collectives, on_device(): lax.all_to_all(fk.reshape(column_shape), 'blk', split_axis=0, concat_axis...  58.4 us
    all_to_all x1, blocking collectives, on_device(): lax.all_to_all(jnp.where(asked_mask, value_blocks[chosen], zero_block).re...  55.6 us
    ppermute x1, waiting for transfers between devices, padded(): lax.ppermute(lax.slice_in_dim(block, block.shape[dim] - width, None, axis...  51.9 us
    ppermute x2, waiting for transfers between devices, shifted(): return lax.ppermute(block, axis, route)  46.6 us
    all_to_all x1, blocking collectives, on_device(): lax.all_to_all(jnp.stack(results), 'head', split_axis=1, concat_axis=2, t...  29.1 us
    all_to_all x1, waiting for transfers between devices, on_device(): lax.all_to_all(jnp.stack([query_rows, key_rows, value_rows, out_grad]), '...  24.7 us
  transfers between devices with their start and end apart: 8, of which 4 were waited for; matrix products, arithmetic and copies ran while one was open for 5% of the time, Pallas kernels for 0%

profile of v4, /device:TPU:8, one launch (start us, length us, event | category | flops | bytes accessed | tf_op | source)
XLA Modules:
  0.0 500.6 jit_solution(8365256748495202387)
XLA Ops:
  4.2 8.5 %all-to-all-start.1 = ((s32[32,1,2]{2,1,0:T(1,128)}), s32[32,1,2]{2,1,0:T(1,128)S(1)}, u32[]{:S(2)}, u32[]{:S(2)}) async-start(s32[32,1,2]{2,1,0:T(1,128)} %bitcast.13), calls=%async_computation.1 | async-start | bytes 32768 | tf_op jit(solution)/shard_map/all_to_all | solution.py:280
  12.8 1.8 pad_maximum_fusion.3
  14.6 2.6 copy.65
  17.2 1.7 all-to-all-done.1
  18.9 4.3 all-to-all-start
  24.8 24.7 %all-to-all-done = bf16[4,256,1024]{1,0,2:T(4,128)(2,1)S(1)} async-done(((bf16[4,256,1024]{1,0,2:T(4,128)(2,1)}), bf16[4,256,1024]{1,0,2:T(4,128)(2,1)S(1)}, u32[]{:S(2)}, u32[]{:S(2)}) %all-to-all-start) | async-done | bytes 2097184 | tf_op jit(solution)/shard_map/all_to_all | solution.py:254
  49.5 2.6 copy.66
  52.1 1.7 fusion.33
  53.8 2.9 gather_fusion
  56.7 2.8 gather_fusion.1
  59.5 5.2 %broadcast_select_fusion = (bf16[32,2,128,256]{3,2,1,0:T(8,128)(2,1)S(1)}, bf16[32,2,128,256]{3,2,1,0:T(8,128)(2,1)}) fusion(bf16[32,2,128,256]{3,2,1,0:T(8,128)(2,1)} %bitcast.126, pred[32,2]{1,0:T(8,128)(4,1)S(1)} %copy.70, bf16[32,2,128,256]{3,2,1,0:T(8,128)(2,1)} %bitcast.125), kind=kLoop, calls=%fused_computation.19 | loop fusion | flops 4194304 | bytes 16777280 | tf_op jit(solution)/shard_map/jit(_where)/select_n | solution.py:301
  64.7 55.6 %all_to_all.59 = bf16[32,2,128,256]{3,2,1,0:T(8,128)(2,1)} all-to-all(bf16[32,2,128,256]{3,2,1,0:T(8,128)(2,1)S(1)} %get-tuple-element.58), channel_id=1, replica_groups=mesh['blk'=32,'head'=4] {'blk'}, dimensions={0} | all-to-all | bytes 8388608 | tf_op jit(solution)/shard_map/all_to_all | solution.py:300
  120.2 6.0 %all-to-all-start.2 = ((bf16[32,2,128,256]{3,2,1,0:T(8,128)(2,1)}), bf16[32,2,128,256]{3,2,1,0:T(8,128)(2,1)}, u32[]{:S(2)}, u32[]{:S(2)}) async-start(bf16[32,2,128,256]{3,2,1,0:T(8,128)(2,1)} %get-tuple-element.59), calls=%async_computation.2 | async-start | bytes 8388608 | tf_op jit(solution)/shard_map/all_to_all | solution.py:293
  126.7 1.6 collective-permute-start.1
  128.5 51.9 %collective-permute-done = bf16[4,2,128,256]{3,2,0,1:T(8,128)(2,1)} collective-permute-done((bf16[4,2,128,256]{3,2,0,1:T(8,128)(2,1)S(1)}, bf16[4,2,128,256]{3,2,0,1:T(8,128)(2,1)}, u32[]{:S(2)}, u32[]{:S(2)}) %collective-permute-start) | collective-permute-done | bytes 524320 | tf_op jit(solution)/shard_map/ppermute | solution.py:28
  182.2 2.0 copy-done.6
  184.1 2.8 pad_maximum_fusion.2
  186.9 5.0 %pad_maximum_fusion.1 = bf16[80,128,256]{2,1,0:T(8,128)(2,1)} fusion(bf16[64,128,256]{2,1,0:T(8,128)(2,1)} %bitcast.18, bf16[16,128,256]{2,1,0:T(8,128)(2,1)S(1)} %get-tuple-element.51), kind=kLoop, calls=%fused_computation.8 | loop fusion | flops 2621440 | bytes 10485760 | tf_op jit(solution)/shard_map/concatenate | solution.py:310
  191.9 135.0 %shard_map.120 = (bf16[1024,256]{1,0:T(8,128)(2,1)S(1)}, bf16[1024,256]{1,0:T(8,128)(2,1)S(1)}, f32[16,256,128]{2,1,0:T(8,128)S(1)}, f32[16,256,128]{2,1,0:T(8,1...) custom-call(s32[128]{0:T(128)S(1)} %reshape.222.rows_ref, s32[8]{0:T(128)S(1)} %copy-done.4, ...), custom_call_target="tpu_custom_call" | custom-call | flops 12884901888 | bytes 33554432 | tf_op jit(solution)/shard_map/pallas_call | solution.py:217
  326.9 58.4 %all_to_all.60 = bf16[32,2,256,128]{3,2,1,0:T(8,128)(2,1)} all-to-all(bf16[32,2,256,128]{3,2,1,0:T(8,128)(2,1)} %bitcast.134), channel_id=1, replica_groups=mesh['blk'=32,'head'=4] {'blk'}, dimensions={0} | all-to-all | bytes 8388608 | tf_op jit(solution)/shard_map/all_to_all | solution.py:343
  385.4 5.9 %all-to-all-start.5 = ((bf16[32,2,256,128]{3,2,1,0:T(8,128)(2,1)}), bf16[32,2,256,128]{3,2,1,0:T(8,128)(2,1)}, u32[]{:S(2)}, u32[]{:S(2)}) async-start(bf16[32,2,256,128]{3,2,1,0:T(8,128)(2,1)} %bitcast.132), calls=%async_computation.5 | async-start | bytes 8388608 | tf_op jit(solution)/shard_map/all_to_all | solution.py:344
  391.3 1.9 fusion
  394.3 1.6 collective-permute-start.3
  396.0 2.9 fusion.7
  398.9 46.6 %collective-permute-done.2 = bf16[4,2,256,128]{3,2,0,1:T(8,128)(2,1)} collective-permute-done((bf16[4,2,256,128]{3,2,0,1:T(8,128)(2,1)}, bf16[4,2,256,128]{3,2,0,1:T(8,128)(2,1)}, u32[]{:S(2)}, u32[]{:S(2)}) %collective-permute-start.2) | collective-permute-done | bytes 524320 | tf_op jit(solution)/shard_map/ppermute | solution.py:39
  445.5 2.3 fusion.10
  447.8 2.3 fusion.15
  450.1 2.3 fusion.4
  452.4 4.5 fusion.1
  456.9 2.0 fusion.17
  462.1 29.1 %all_to_all.61 = bf16[4,1024,256]{2,0,1:T(4,128)(2,1)S(1)} all-to-all(bf16[4,1024,256]{2,0,1:T(4,128)(2,1)S(1)} %copy.77), channel_id=1, replica_groups=mesh['blk'=32,'head'=4] {'head'}, dimensions={1} | all-to-all | bytes 4194304 | tf_op jit(solution)/shard_map/all_to_all | solution.py:376
  491.1 3.1 fusion.31
  (70 shorter events, 17.9 us)
Async XLA Ops:
  4.2 14.7 %all-to-all-start.1 = ((s32[32,1,2]{2,1,0:T(1,128)}), s32[32,1,2]{2,1,0:T(1,128)S(1)}, u32[]{:S(2)}, u32[]{:S(2)}) async-start(s32[32,1,2]{2,1,0:T(1,128)} %bitcast.13), calls=%async_computation.1 | async-start | bytes 32768 | tf_op jit(solution)/shard_map/all_to_all | solution.py:280
  18.9 30.7 %all-to-all-start = ((bf16[4,256,1024]{1,0,2:T(4,128)(2,1)}), bf16[4,256,1024]{1,0,2:T(4,128)(2,1)S(1)}, u32[]{:S(2)}, u32[]{:S(2)}) async-start(bf16[4,256,1024]{1,0,2:T(4,128)(2,1)} %copy.65), calls=%async_computation | async-start | bytes 4194304 | tf_op jit(solution)/shard_map/all_to_all | solution.py:254
  120.2 6.0 %copy-start.8 = (s32[4,8,16]{2,1,0:T(8,128)S(1)}, s32[4,8,16]{2,1,0:T(8,128)}, u32[]{:S(2)}) copy-start(s32[4,8,16]{2,1,0:T(8,128)} %param.21) | copy-start | bytes 6148
  120.2 66.7 %all-to-all-start.2 = ((bf16[32,2,128,256]{3,2,1,0:T(8,128)(2,1)}), bf16[32,2,128,256]{3,2,1,0:T(8,128)(2,1)}, u32[]{:S(2)}, u32[]{:S(2)}) async-start(bf16[32,2,128,256]{3,2,1,0:T(8,128)(2,1)} %get-tuple-element.59), calls=%async_computation.2 | async-start | bytes 8388608 | tf_op jit(solution)/shard_map/all_to_all | solution.py:293
  126.3 2.0 copy-start.9
  126.5 54.0 %collective-permute-start = (bf16[4,2,128,256]{3,2,0,1:T(8,128)(2,1)S(1)}, bf16[4,2,128,256]{3,2,0,1:T(8,128)(2,1)}, u32[]{:S(2)}, u32[]{:S(2)}) collective-permute-start(bf16[4,2,128,256]{3,2,0,1:T(8,128)(2,1)S(1)} %get-tuple-element.56), channel_id=1, source_target_pairs={{0,4},{4,8},{8,12},{12,16},{16,20},{20,24},{24,28},{28,32},{32,36}... | collective-permute-start | bytes 1572872 | tf_op jit(solution)/shard_map/ppermute | solution.py:28
  126.7 53.8 %collective-permute-start.1 = (bf16[4,2,128,256]{3,2,0,1:T(8,128)(2,1)S(1)}, bf16[4,2,128,256]{3,2,0,1:T(8,128)(2,1)}, u32[]{:S(2)}, u32[]{:S(2)}) collective-permute-start(bf16[4,2,128,256]{3,2,0,1:T(8,128)(2,1)S(1)} %get-tuple-element.57), channel_id=1, source_target_pairs={{4,0},{8,4},{12,8},{16,12},{20,16},{24,20},{28,24},{32,28},{36,32}... | collective-permute-start | bytes 1572872 | tf_op jit(solution)/shard_map/ppermute | solution.py:31
  181.9 2.2 copy-start.6
  186.9 5.0 %copy-start.4 = (s32[8]{0:T(128)S(1)}, s32[8]{0:T(128)}, u32[]{:S(2)}) copy-start(s32[8]{0:T(128)} %count_ref.1) | copy-start | bytes 100
  326.9 58.4 %copy-start = (bf16[1024,256]{1,0:T(8,128)(2,1)}, bf16[1024,256]{1,0:T(8,128)(2,1)S(1)}, u32[]{:S(2)}) copy-start(bf16[1024,256]{1,0:T(8,128)(2,1)S(1)} %get-tuple-element.34) | copy-start | bytes 1572868
  326.9 58.4 %copy-start.2 = (bf16[1024,256]{1,0:T(8,128)(2,1)}, bf16[1024,256]{1,0:T(8,128)(2,1)S(1)}, u32[]{:S(2)}) copy-start(bf16[1024,256]{1,0:T(8,128)(2,1)S(1)} %get-tuple-element.35) | copy-start | bytes 1572868
  385.4 67.0 %all-to-all-start.5 = ((bf16[32,2,256,128]{3,2,1,0:T(8,128)(2,1)}), bf16[32,2,256,128]{3,2,1,0:T(8,128)(2,1)}, u32[]{:S(2)}, u32[]{:S(2)}) async-start(bf16[32,2,256,128]{3,2,1,0:T(8,128)(2,1)} %bitcast.132), calls=%async_computation.5 | async-start | bytes 8388608 | tf_op jit(solution)/shard_map/all_to_all | solution.py:344
  394.1 51.4 %collective-permute-start.2 = (bf16[4,2,256,128]{3,2,0,1:T(8,128)(2,1)}, bf16[4,2,256,128]{3,2,0,1:T(8,128)(2,1)}, u32[]{:S(2)}, u32[]{:S(2)}) collective-permute-start(bf16[4,2,256,128]{3,2,0,1:T(8,128)(2,1)} %get-tuple-element.49), channel_id=1, source_target_pairs={{124,0},{0,4},{4,8},{8,12},{12,16},{16,20},{20,24},{24,28},{28,32}... | collective-permute-start | bytes 1572872 | tf_op jit(solution)/shard_map/ppermute | solution.py:39
  394.3 53.6 %collective-permute-start.3 = (bf16[4,2,256,128]{3,2,0,1:T(8,128)(2,1)S(1)}, bf16[4,2,256,128]{3,2,0,1:T(8,128)(2,1)S(1)}, u32[]{:S(2)}, u32[]{:S(2)}) collective-permute-start(bf16[4,2,256,128]{3,2,0,1:T(8,128)(2,1)S(1)} %get-tuple-element.48), channel_id=1, source_target_pairs={{4,0},{8,4},{12,8},{16,12},{20,16},{24,20},{28,24},{32,28},{36,32}... | collective-permute-start | bytes 1572872 | tf_op jit(solution)/shard_map/ppermute | solution.py:39
  396.0 49.5 %copy-start.5 = (f32[16,256,128]{2,1,0:T(8,128)S(1)}, f32[16,256,128]{2,1,0:T(8,128)}, u32[]{:S(2)}) copy-start(f32[16,256,128]{2,1,0:T(8,128)} %get-tuple-element.37) | copy-start | bytes 6291460
  445.5 4.6 copy-start.7
  459.0 1.0 copy-start.1
  459.0 1.2 copy-start.3

commit v5 on v4

--- a/solution.py
+++ b/solution.py
@@ -71,10 +71,10 @@
     rows_ref, count_ref, seed_ref, q_ref, g_ref, kt_ref, vt_ref,
     att_ref, qg_ref, nk_ref, nv_ref, fk_ref, fv_ref,
     s_scr, keep_scr, drop_scr,
-    *, scale, near_count, slot_count, blocks, head_size,
+    *, scale, near_count, slot_count, blocks, head_size, group,
 ):
-    p = pl.program_id(0)
-    c = pl.program_id(1)
+    p = group
+    c = pl.program_id(0)
     width = q_ref.shape[-1]
     pair = width // head_size
 
@@ -182,51 +182,51 @@
     qg_ref[...] = (pick(qacc, lane_head) * scale).astype(qg_ref.dtype)
 
 
-def block_attention(rows, counts, seeds, q, g, kt, vt, *, near_count, far_count, scale, head_size):
-    row_count, local_width = q.shape
+def block_attention(rows, counts, seeds, q, g, kt, vt, *, near_count, far_count, scale, head_size, group):
+    row_count = q.shape[0]
     width = 2 * head_size
-    groups = local_width // width
     blocks = row_count // BS
     slot_count = 1 + L + E
     kernel = functools.partial(
         attention_kernel, scale=scale, near_count=near_count, slot_count=slot_count,
-        blocks=blocks, head_size=head_size,
-    )
-    q_spec = pl.BlockSpec((BS, width), lambda p, c, *_: (c, p))
-    table_spec = pl.BlockSpec((kt.shape[0], width), lambda p, c, *_: (0, p))
-    near_spec = pl.BlockSpec((near_count, width, BS), lambda p, c, *_: (0, p, 0))
-    far_spec = pl.BlockSpec((far_count, width, BS), lambda p, c, *_: (0, p, 0))
+        blocks=blocks, head_size=head_size, group=group,
+    )
+    q_spec = pl.BlockSpec((BS, width), lambda c, *_: (c, group))
+    out_spec = pl.BlockSpec((BS, width), lambda c, *_: (c, 0))
+    table_spec = pl.BlockSpec((kt.shape[0], width), lambda c, *_: (0, 0))
+    near_spec = pl.BlockSpec((near_count, width, BS), lambda c, *_: (0, 0, 0))
+    far_spec = pl.BlockSpec((far_count, width, BS), lambda c, *_: (0, 0, 0))
     grid_spec = pltpu.PrefetchScalarGridSpec(
         num_scalar_prefetch=3,
-        grid=(groups, blocks),
+        grid=(blocks,),
         in_specs=[q_spec, q_spec, table_spec, table_spec],
-        out_specs=[q_spec, q_spec, near_spec, near_spec, far_spec, far_spec],
+        out_specs=[out_spec, out_spec, near_spec, near_spec, far_spec, far_spec],
         scratch_shapes=[
             pltpu.VMEM((2, slot_count, BS, BS), jnp.float32),
             pltpu.VMEM((2, slot_count, BS, BS), jnp.float32),
             pltpu.VMEM((2, slot_count, BS, BS), jnp.bfloat16),
         ],
     )
-    heads = local_width // head_size
+    heads = width // head_size
     flops = 6 * 2 * heads * blocks * slot_count * BS * BS * width
     cost = pl.CostEstimate(
         flops=flops,
         transcendentals=heads * blocks * slot_count * BS * BS,
-        bytes_accessed=2 * (q.size * 4 + kt.size * 2) + 4 * (near_count + far_count) * BS * local_width * 2,
+        bytes_accessed=2 * (row_count * width * 4 + kt.size * 2) + 4 * (near_count + far_count) * BS * width * 2,
     )
     return pl.pallas_call(
         kernel,
         grid_spec=grid_spec,
         out_shape=[
-            jax.ShapeDtypeStruct(q.shape, jnp.bfloat16),
-            jax.ShapeDtypeStruct(q.shape, jnp.bfloat16),
-            jax.ShapeDtypeStruct((near_count, local_width, BS), jnp.float32),
-            jax.ShapeDtypeStruct((near_count, local_width, BS), jnp.float32),
-            jax.ShapeDtypeStruct((far_count, local_width, BS), jnp.bfloat16),
-            jax.ShapeDtypeStruct((far_count, local_width, BS), jnp.bfloat16),
+            jax.ShapeDtypeStruct((row_count, width), jnp.bfloat16),
+            jax.ShapeDtypeStruct((row_count, width), jnp.bfloat16),
+            jax.ShapeDtypeStruct((near_count, width, BS), jnp.float32),
+            jax.ShapeDtypeStruct((near_count, width, BS), jnp.float32),
+            jax.ShapeDtypeStruct((far_count, width, BS), jnp.bfloat16),
+            jax.ShapeDtypeStruct((far_count, width, BS), jnp.bfloat16),
         ],
         compiler_params=pltpu.CompilerParams(
-            dimension_semantics=("arbitrary", "arbitrary"), vmem_limit_bytes=48 * 1024 * 1024
+            dimension_semantics=("arbitrary",), vmem_limit_bytes=48 * 1024 * 1024
         ),
         cost_estimate=cost,
     )(rows, counts, seeds, q, g, kt, vt)
@@ -289,30 +289,10 @@
     asked_mask = (wanted_flat >= 0)[:, None, None]
     zero_block = jnp.zeros((), jnp.bfloat16)
     reply_shape = (peer_count, capacity, BS, local_width)
-    far_key, far_value = (
-        lax.all_to_all(
-            jnp.where(asked_mask, key_blocks[chosen], zero_block).reshape(reply_shape),
-            "blk",
-            split_axis=0,
-            concat_axis=0,
-            tiled=True,
-        ),
-        lax.all_to_all(
-            jnp.where(asked_mask, value_blocks[chosen], zero_block).reshape(reply_shape),
-            "blk",
-            split_axis=0,
-            concat_axis=0,
-            tiled=True,
-        ),
-    )
     near_count = QB_DEV + 2 * W
     far_total_count = peer_count * capacity
-    key_table = jnp.concatenate(
-        [widened[:, 0], far_key.reshape(far_total_count, BS, local_width)], axis=0
-    )
-    value_table = jnp.concatenate(
-        [widened[:, 1], far_value.reshape(far_total_count, BS, local_width)], axis=0
-    )
+    key_asked = jnp.where(asked_mask, key_blocks[chosen], zero_block)
+    value_asked = jnp.where(asked_mask, value_blocks[chosen], zero_block)
     local_block = jnp.arange(QB_DEV, dtype=jnp.int32)[:, None]
     self_slot = local_block + W
     near_slot = local_block + W + local_offset
@@ -322,40 +302,61 @@
     live_slots = (slot_number <= L) | (slot_number - 1 - L < live_count[:, None])
     slot_rows = table_rows.reshape(-1).astype(jnp.int32)
     seed_flat = drop_seed.reshape(-1).astype(jnp.int32)
-    table_count = key_table.shape[0]
-
-    att_out, qg_out, nk, nv, fk, fv = block_attention(
-        slot_rows,
-        live_count.astype(jnp.int32),
-        seed_flat,
-        query_local,
-        grad_local,
-        key_table.reshape(table_count * BS, local_width),
-        value_table.reshape(table_count * BS, local_width),
-        near_count=near_count,
-        far_count=far_total_count,
-        scale=score_scale,
-        head_size=head_size,
-    )
-    outputs = (att_out, qg_out)
-    column_shape = (peer_count, capacity, local_width, BS)
-    back_key, back_value = (
-        lax.all_to_all(fk.reshape(column_shape), "blk", split_axis=0, concat_axis=0, tiled=True),
-        lax.all_to_all(fv.reshape(column_shape), "blk", split_axis=0, concat_axis=0, tiled=True),
-    )
+    width = 2 * head_size
+    pair_shape = (peer_count, capacity, BS, width)
+    column_shape = (peer_count, capacity, width, BS)
     owner_match = (
         jnp.arange(QB_DEV, dtype=jnp.int32)[:, None] == wanted_here.reshape(1, -1)
     ).astype(jnp.bfloat16)
-    far_key_sum = jnp.dot(
-        owner_match,
-        back_key.reshape(far_total_count, BS * local_width),
-        preferred_element_type=jnp.float32,
-    ).reshape(QB_DEV, local_width, BS)
-    far_value_sum = jnp.dot(
-        owner_match,
-        back_value.reshape(far_total_count, BS * local_width),
-        preferred_element_type=jnp.float32,
-    ).reshape(QB_DEV, local_width, BS)
+
+    def owner_sum(back):
+        return jnp.dot(
+            owner_match,
+            back.reshape(far_total_count, width * BS),
+            preferred_element_type=jnp.float32,
+        ).reshape(QB_DEV, width, BS)
+
+    pieces = []
+    for group in range(local_width // width):
+        cols = slice(group * width, (group + 1) * width)
+        far_key, far_value = (
+            lax.all_to_all(
+                key_asked[:, :, cols].reshape(pair_shape), "blk", split_axis=0, concat_axis=0, tiled=True
+            ),
+            lax.all_to_all(
+                value_asked[:, :, cols].reshape(pair_shape), "blk", split_axis=0, concat_axis=0, tiled=True
+            ),
+        )
+        key_table = jnp.concatenate(
+            [widened[:, 0, :, cols], far_key.reshape(far_total_count, BS, width)], axis=0
+        )
+        value_table = jnp.concatenate(
+            [widened[:, 1, :, cols], far_value.reshape(far_total_count, BS, width)], axis=0
+        )
+        table_count = key_table.shape[0]
+        att_p, qg_p, nk_p, nv_p, fk_p, fv_p = block_attention(
+            slot_rows,
+            live_count.astype(jnp.int32),
+            seed_flat,
+            query_local,
+            grad_local,
+            key_table.reshape(table_count * BS, width),
+            value_table.reshape(table_count * BS, width),
+            near_count=near_count,
+            far_count=far_total_count,
+            scale=score_scale,
+            head_size=head_size,
+            group=group,
+        )
+        back_key, back_value = (
+            lax.all_to_all(fk_p.reshape(column_shape), "blk", split_axis=0, concat_axis=0, tiled=True),
+            lax.all_to_all(fv_p.reshape(column_shape), "blk", split_axis=0, concat_axis=0, tiled=True),
+        )
+        pieces.append((att_p, qg_p, nk_p, nv_p, owner_sum(back_key), owner_sum(back_value)))
+    att_out, qg_out, nk, nv, far_key_sum, far_value_sum = [
+        jnp.concatenate([piece[i] for piece in pieces], axis=1) for i in range(6)
+    ]
+    outputs = (att_out, qg_out)
     near_total = jnp.stack([nk, nv], axis=1)
     from_below = shifted(near_total[QB_DEV + W :].astype(jnp.bfloat16), "blk", 1).astype(
         jnp.float32

time: 501 us -> 536 us (1.070); the launches traced: 501 us -> 528 us
  waiting for transfers between devices: 125 us -> 104 us
  blocking collectives: 143 us -> 162 us
  starting transfers between devices: 28.3 us -> 44.2 us
  local copies, waits for them, and re-layouts: 31.5 us -> 43.7 us
    ppermute x1, waiting for transfers between devices: 51.9 us -> 0.56 us  [padded(): lax.ppermute(lax.slice_in_dim(block, block.shape[dim] - width, None, axis...]
    ppermute x1, waiting for transfers between devices: 0.01 us -> 27.5 us  [padded(): lax.ppermute(lax.slice_in_dim(block, 0, width, axis=dim), axis, backward)]
    all_to_all x2 -> x4, waiting for transfers between devices: 0.01 us -> 24.7 us  [the longest x2 24.7 us: on_device(): lax.all_to_all(fv_p.reshape(column_shape), 'blk', split_axis=0, concat_ax...]
    ppermute x2, waiting for transfers between devices: 46.6 us -> 24.1 us  [shifted(): return lax.ppermute(block, axis, route)]
    all_to_all x2 -> x4, blocking collectives: 114 us -> 132 us  [the longest x2 65.2 us: on_device(): lax.all_to_all(key_asked[:, :, cols].reshape(pair_shape), 'blk', split_ax...]
    all_to_all x2 -> x4, starting transfers between devices: 11.9 us -> 28.3 us  [the longest x2 12.7 us: on_device(): lax.all_to_all(fv_p.reshape(column_shape), 'blk', split_axis=0, concat_ax...]
    unnamed x25 -> x65, local copies, waits for them, and re-layouts: 7.08 us -> 11.8 us
    pallas_call x1 -> x2, Pallas kernels: 135 us -> 138 us  [block_attention(): pl.pallas_call(kernel, grid_spec=grid_spec, out_shape=[jax.ShapeDtypeStru...]
  transfers between devices with their start and end apart: 8 -> 10, of which waited for: 4 -> 6; matrix products, arithmetic and copies ran while one was open for 5% -> 6% of each run, Pallas kernels for 0% -> 26%
where the time goes in v5:
time: 536 us; the launch traced here: 528 us
  blocking collectives  162 us (30%)
  Pallas kernels  138 us (26%)
  waiting for transfers between devices  104 us (19%)
  starting transfers between devices  44.2 us (8%)
  local copies, waits for them, and re-layouts  43.7 us (8%)
  other arithmetic  25.1 us (5%)
  matrix products  10.6 us (2%)
    pallas_call x2, Pallas kernels, block_attention(): pl.pallas_call(kernel, grid_spec=grid_spec, out_shape=[jax.ShapeDtypeStru...  138 us
    all_to_all x2, blocking collectives, on_device(): lax.all_to_all(key_asked[:, :, cols].reshape(pair_shape), 'blk', split_ax...  65.2 us
    all_to_all x1, blocking collectives, on_device(): lax.all_to_all(fk_p.reshape(column_shape), 'blk', split_axis=0, concat_ax...  34.6 us
    all_to_all x1, blocking collectives, on_device(): lax.all_to_all(value_asked[:, :, cols].reshape(pair_shape), 'blk', split_...  32.1 us
    all_to_all x1, blocking collectives, on_device(): lax.all_to_all(jnp.stack(results), 'head', split_axis=1, concat_axis=2, t...  29.6 us
    ppermute x1, waiting for transfers between devices, padded(): lax.ppermute(lax.slice_in_dim(block, 0, width, axis=dim), axis, backward)  27.5 us
    all_to_all x1, waiting for transfers between devices, on_device(): lax.all_to_all(jnp.stack([query_rows, key_rows, value_rows, out_grad]), '...  24.9 us
    all_to_all x2, waiting for transfers between devices, on_device(): lax.all_to_all(fv_p.reshape(column_shape), 'blk', split_axis=0, concat_ax...  24.7 us
  transfers between devices with their start and end apart: 10, of which 6 were waited for; matrix products, arithmetic and copies ran while one was open for 6% of the time, Pallas kernels for 26%

profile of v5, /device:TPU:8, one launch (start us, length us, event | category | flops | bytes accessed | tf_op | source)
XLA Modules:
  0.0 528.1 jit_solution(2263400989405211843)
XLA Ops:
  4.2 8.5 %all-to-all-start.1 = ((s32[32,1,2]{2,1,0:T(1,128)}), s32[32,1,2]{2,1,0:T(1,128)S(1)}, u32[]{:S(2)}, u32[]{:S(2)}) async-start(s32[32,1,2]{2,1,0:T(1,128)} %bitcast.13), calls=%async_computation.1 | async-start | bytes 32768 | tf_op jit(solution)/shard_map/all_to_all | solution.py:280
  12.8 1.8 pad_maximum_fusion.5
  14.6 2.6 copy.69
  18.9 4.3 all-to-all-start
  24.7 24.9 %all-to-all-done = bf16[4,256,1024]{1,0,2:T(4,128)(2,1)S(1)} async-done(((bf16[4,256,1024]{1,0,2:T(4,128)(2,1)}), bf16[4,256,1024]{1,0,2:T(4,128)(2,1)S(1)}, u32[]{:S(2)}, u32[]{:S(2)}) %all-to-all-start) | async-done | bytes 2097184 | tf_op jit(solution)/shard_map/all_to_all | solution.py:254
  49.5 2.6 copy.70
  53.8 2.8 gather_fusion.1
  56.6 2.8 gather_fusion
  59.4 3.9 broadcast_select_fusion
  63.3 2.7 fusion.41
  66.0 33.1 %all_to_all.79 = bf16[32,2,128,128]{3,2,1,0:T(8,128)(2,1)} all-to-all(bf16[32,2,128,128]{3,2,1,0:T(8,128)(2,1)S(1)} %bitcast.172), channel_id=1, replica_groups=mesh['blk'=32,'head'=4] {'blk'}, dimensions={0} | all-to-all | bytes 4194304 | tf_op jit(solution)/shard_map/all_to_all | solution.py:323
  99.1 32.1 %all_to_all.80 = bf16[32,2,128,128]{3,2,1,0:T(8,128)(2,1)} all-to-all(bf16[32,2,128,128]{3,2,1,0:T(8,128)(2,1)S(1)} %bitcast.171), channel_id=1, replica_groups=mesh['blk'=32,'head'=4] {'blk'}, dimensions={0} | all-to-all | bytes 4194304 | tf_op jit(solution)/shard_map/all_to_all | solution.py:326
  131.2 32.1 %all_to_all.81 = bf16[32,2,128,128]{3,2,1,0:T(8,128)(2,1)} all-to-all(bf16[32,2,128,128]{3,2,1,0:T(8,128)(2,1)S(1)} %bitcast.170), channel_id=1, replica_groups=mesh['blk'=32,'head'=4] {'blk'}, dimensions={0} | all-to-all | bytes 4194304 | tf_op jit(solution)/shard_map/all_to_all | solution.py:323
  163.3 5.8 %all-to-all-start.3 = ((bf16[32,2,128,128]{3,2,1,0:T(8,128)(2,1)}), bf16[32,2,128,128]{3,2,1,0:T(8,128)(2,1)}, u32[]{:S(2)}, u32[]{:S(2)}) async-start(bf16[32,2,128,128]{3,2,1,0:T(8,128)(2,1)} %bitcast.169), calls=%async_computation.3 | async-start | bytes 4194304 | tf_op jit(solution)/shard_map/all_to_all | solution.py:326
  170.7 27.5 %collective-permute-done.1 = bf16[4,2,128,256]{3,2,0,1:T(8,128)(2,1)} collective-permute-done((bf16[4,2,128,256]{3,2,0,1:T(8,128)(2,1)S(1)}, bf16[4,2,128,256]{3,2,0,1:T(8,128)(2,1)}, u32[]{:S(2)}, u32[]{:S(2)}) %collective-permute-start.1) | collective-permute-done | bytes 524320 | tf_op jit(solution)/shard_map/ppermute | solution.py:31
  204.4 1.7 pad_maximum_fusion.4
  206.1 69.4 %shard_map.121 = (bf16[1024,128]{1,0:T(8,128)(2,1)S(1)}, bf16[1024,128]{1,0:T(8,128)(2,1)S(1)}, f32[16,128,128]{2,1,0:T(8,128)S(1)}, f32[16,128,128]{2,1,0:T(8,1...) custom-call(s32[128]{0:T(128)S(1)} %reshape.254.rows_ref, s32[8]{0:T(128)S(1)} %copy-done.16, ...), custom_call_target="tpu_custom_call" | custom-call | flops 6442450944 | bytes 16777216 | tf_op jit(solution)/shard_map/pallas_call | solution.py:217
  277.2 9.8 %all-to-all-start.7 = ((bf16[32,2,128,128]{3,2,1,0:T(8,128)(2,1)}), bf16[32,2,128,128]{3,2,1,0:T(8,128)(2,1)}, u32[]{:S(2)}, u32[]{:S(2)}) async-start(bf16[32,2,128,128]{3,2,1,0:T(8,128)(2,1)} %bitcast.40), calls=%async_computation.7 | async-start | bytes 4194304 | tf_op jit(solution)/shard_map/all_to_all | solution.py:352
  287.1 3.3 pad_maximum_fusion.1
  290.4 3.4 pad_maximum_fusion.2
  293.8 68.6 %shard_map.120 = (bf16[1024,128]{1,0:T(8,128)(2,1)S(1)}, bf16[1024,128]{1,0:T(8,128)(2,1)S(1)}, f32[16,128,128]{2,1,0:T(8,128)S(1)}, f32[16,128,128]{2,1,0:T(8,1...) custom-call(s32[128]{0:T(128)S(1)} %reshape.254.rows_ref, s32[8]{0:T(128)S(1)} %copy-done.16, ...), custom_call_target="tpu_custom_call" | custom-call | flops 6442450944 | bytes 16777216 | tf_op jit(solution)/shard_map/pallas_call | solution.py:217
  365.8 34.6 %all_to_all.82 = bf16[32,2,128,128]{3,2,1,0:T(8,128)(2,1)} all-to-all(bf16[32,2,128,128]{3,2,1,0:T(8,128)(2,1)S(1)} %bitcast.152), channel_id=1, replica_groups=mesh['blk'=32,'head'=4] {'blk'}, dimensions={0} | all-to-all | bytes 4194304 | tf_op jit(solution)/shard_map/all_to_all | solution.py:352
  400.4 5.9 %all-to-all-start.9 = ((bf16[32,2,128,128]{3,2,1,0:T(8,128)(2,1)}), bf16[32,2,128,128]{3,2,1,0:T(8,128)(2,1)}, u32[]{:S(2)}, u32[]{:S(2)}) async-start(bf16[32,2,128,128]{3,2,1,0:T(8,128)(2,1)} %bitcast.183), calls=%async_computation.9 | async-start | bytes 4194304 | tf_op jit(solution)/shard_map/all_to_all | solution.py:353
  409.7 24.7 %all-to-all-done.9 = bf16[32,2,128,128]{3,2,1,0:T(8,128)(2,1)} async-done(((bf16[32,2,128,128]{3,2,1,0:T(8,128)(2,1)}), bf16[32,2,128,128]{3,2,1,0:T(8,128)(2,1)}, u32[]{:S(2)}, u32[]{:S(2)}) %all-to-all-start.9) | async-done | bytes 2097184 | tf_op jit(solution)/shard_map/all_to_all | solution.py:353
  434.5 6.8 %all-to-all-start.8 = ((bf16[32,2,128,128]{3,2,1,0:T(8,128)(2,1)}), bf16[32,2,128,128]{3,2,1,0:T(8,128)(2,1)}, u32[]{:S(2)}, u32[]{:S(2)}) async-start(bf16[32,2,128,128]{3,2,1,0:T(8,128)(2,1)} %bitcast.181), calls=%async_computation.8 | async-start | bytes 4194304 | tf_op jit(solution)/shard_map/all_to_all | solution.py:353
  442.9 1.8 collective-permute-start.3
  446.7 24.1 %collective-permute-done.2 = bf16[4,2,256,128]{3,2,0,1:T(8,128)(2,1)S(1)} collective-permute-done((bf16[4,2,256,128]{3,2,0,1:T(8,128)(2,1)S(1)}, bf16[4,2,256,128]{3,2,0,1:T(8,128)(2,1)S(1)}, u32[]{:S(2)}, u32[]{:S(2)}) %collective-permute-start.2) | collective-permute-done | bytes 524320 | tf_op jit(solution)/shard_map/ppermute | solution.py:39
  471.2 3.6 fusion.8
  476.2 2.8 fusion.2
  479.9 3.0 fusion.5
  488.8 29.6 %all_to_all.83 = bf16[4,1024,256]{2,0,1:T(4,128)(2,1)S(1)} all-to-all(bf16[4,1024,256]{2,0,1:T(4,128)(2,1)S(1)} %copy.83), channel_id=1, replica_groups=mesh['blk'=32,'head'=4] {'head'}, dimensions={1} | all-to-all | bytes 4194304 | tf_op jit(solution)/shard_map/all_to_all | solution.py:377
  518.4 3.1 fusion.43
  (128 shorter events, 42.8 us)
Async XLA Ops:
  4.2 14.7 %all-to-all-start.1 = ((s32[32,1,2]{2,1,0:T(1,128)}), s32[32,1,2]{2,1,0:T(1,128)S(1)}, u32[]{:S(2)}, u32[]{:S(2)}) async-start(s32[32,1,2]{2,1,0:T(1,128)} %bitcast.13), calls=%async_computation.1 | async-start | bytes 32768 | tf_op jit(solution)/shard_map/all_to_all | solution.py:280
  18.9 30.7 %all-to-all-start = ((bf16[4,256,1024]{1,0,2:T(4,128)(2,1)}), bf16[4,256,1024]{1,0,2:T(4,128)(2,1)S(1)}, u32[]{:S(2)}, u32[]{:S(2)}) async-start(bf16[4,256,1024]{1,0,2:T(4,128)(2,1)} %copy.69), calls=%async_computation | async-start | bytes 4194304 | tf_op jit(solution)/shard_map/all_to_all | solution.py:254
  53.8 152.3 %copy-start.6 = (bf16[1,4,256,256]{3,2,1,0:T(8,128)(2,1)}, bf16[1,4,256,256]{3,2,1,0:T(8,128)(2,1)S(1)}, u32[]{:S(2)}) copy-start(bf16[1,4,256,256]{3,2,1,0:T(8,128)(2,1)S(1)} %get-tuple-element.72) | copy-start | bytes 1572868
  53.8 152.3 %copy-start.8 = (bf16[1,4,256,256]{3,2,1,0:T(8,128)(2,1)}, bf16[1,4,256,256]{3,2,1,0:T(8,128)(2,1)S(1)}, u32[]{:S(2)}) copy-start(bf16[1,4,256,256]{3,2,1,0:T(8,128)(2,1)S(1)} %get-tuple-element.73) | copy-start | bytes 1572868
  163.3 113.2 %all-to-all-start.3 = ((bf16[32,2,128,128]{3,2,1,0:T(8,128)(2,1)}), bf16[32,2,128,128]{3,2,1,0:T(8,128)(2,1)}, u32[]{:S(2)}, u32[]{:S(2)}) async-start(bf16[32,2,128,128]{3,2,1,0:T(8,128)(2,1)} %bitcast.169), calls=%async_computation.3 | async-start | bytes 4194304 | tf_op jit(solution)/shard_map/all_to_all | solution.py:326
  169.2 1.4 copy-start.28
  169.3 29.0 %collective-permute-start.1 = (bf16[4,2,128,256]{3,2,0,1:T(8,128)(2,1)S(1)}, bf16[4,2,128,256]{3,2,0,1:T(8,128)(2,1)}, u32[]{:S(2)}, u32[]{:S(2)}) collective-permute-start(bf16[4,2,128,256]{3,2,0,1:T(8,128)(2,1)S(1)} %get-tuple-element.75), channel_id=1, source_target_pairs={{4,0},{8,4},{12,8},{16,12},{20,16},{24,20},{28,24},{32,28},{36,32}... | collective-permute-start | bytes 1572872 | tf_op jit(solution)/shard_map/ppermute | solution.py:31
  169.5 29.3 %collective-permute-start = (bf16[4,2,128,256]{3,2,0,1:T(8,128)(2,1)S(1)}, bf16[4,2,128,256]{3,2,0,1:T(8,128)(2,1)}, u32[]{:S(2)}, u32[]{:S(2)}) collective-permute-start(bf16[4,2,128,256]{3,2,0,1:T(8,128)(2,1)S(1)} %get-tuple-element.74), channel_id=1, source_target_pairs={{0,4},{4,8},{8,12},{12,16},{16,20},{20,24},{24,28},{28,32},{32,36}... | collective-permute-start | bytes 1572872 | tf_op jit(solution)/shard_map/ppermute | solution.py:28
  200.3 1.6 copy-start.22
  201.9 2.5 copy-start.21
  204.4 1.7 copy-start.16
  276.5 10.5 %copy-start.25 = (bf16[16,128,128]{2,1,0:T(8,128)(2,1)S(1)}, bf16[16,128,128]{2,1,0:T(8,128)(2,1)}, u32[]{:S(2)}) copy-start(bf16[16,128,128]{2,1,0:T(8,128)(2,1)} %get-tuple-element.69) | copy-start | bytes 1572868
  277.2 88.6 %all-to-all-start.7 = ((bf16[32,2,128,128]{3,2,1,0:T(8,128)(2,1)}), bf16[32,2,128,128]{3,2,1,0:T(8,128)(2,1)}, u32[]{:S(2)}, u32[]{:S(2)}) async-start(bf16[32,2,128,128]{3,2,1,0:T(8,128)(2,1)} %bitcast.40), calls=%async_computation.7 | async-start | bytes 4194304 | tf_op jit(solution)/shard_map/all_to_all | solution.py:352
  290.3 3.4 copy-start.7
  290.3 3.4 copy-start.9
  400.4 5.9 %copy-start.1 = (f32[16,128,128]{2,1,0:T(8,128)S(1)}, f32[16,128,128]{2,1,0:T(8,128)}, u32[]{:S(2)}) copy-start(f32[16,128,128]{2,1,0:T(8,128)} %copy-done) | copy-start | bytes 3145732
  400.4 6.0 %copy-start.5 = (f32[16,128,128]{2,1,0:T(8,128)S(1)}, f32[16,128,128]{2,1,0:T(8,128)}, u32[]{:S(2)}) copy-start(f32[16,128,128]{2,1,0:T(8,128)} %copy-done.4) | copy-start | bytes 3145732
  400.4 34.0 %all-to-all-start.9 = ((bf16[32,2,128,128]{3,2,1,0:T(8,128)(2,1)}), bf16[32,2,128,128]{3,2,1,0:T(8,128)(2,1)}, u32[]{:S(2)}, u32[]{:S(2)}) async-start(bf16[32,2,128,128]{3,2,1,0:T(8,128)(2,1)} %bitcast.183), calls=%async_computation.9 | async-start | bytes 4194304 | tf_op jit(solution)/shard_map/all_to_all | solution.py:353
  406.4 1.5 copy-start.3
  434.5 45.5 %all-to-all-start.8 = ((bf16[32,2,128,128]{3,2,1,0:T(8,128)(2,1)}), bf16[32,2,128,128]{3,2,1,0:T(8,128)(2,1)}, u32[]{:S(2)}, u32[]{:S(2)}) async-start(bf16[32,2,128,128]{3,2,1,0:T(8,128)(2,1)} %bitcast.181), calls=%async_computation.8 | async-start | bytes 4194304 | tf_op jit(solution)/shard_map/all_to_all | solution.py:353
  441.2 3.5 copy-start.11
  441.3 3.5 copy-start.15
  441.3 4.3 copy-start.13
  441.3 5.2 copy-start.18
  442.7 28.1 %collective-permute-start.2 = (bf16[4,2,256,128]{3,2,0,1:T(8,128)(2,1)S(1)}, bf16[4,2,256,128]{3,2,0,1:T(8,128)(2,1)S(1)}, u32[]{:S(2)}, u32[]{:S(2)}) collective-permute-start(bf16[4,2,256,128]{3,2,0,1:T(8,128)(2,1)S(1)} %get-tuple-element.65), channel_id=1, source_target_pairs={{124,0},{0,4},{4,8},{8,12},{12,16},{16,20},{20,24},{24,28},{28,32}... | collective-permute-start | bytes 1572872 | tf_op jit(solution)/shard_map/ppermute | solution.py:39
  442.9 28.0 %collective-permute-start.3 = (bf16[4,2,256,128]{3,2,0,1:T(8,128)(2,1)S(1)}, bf16[4,2,256,128]{3,2,0,1:T(8,128)(2,1)S(1)}, u32[]{:S(2)}, u32[]{:S(2)}) collective-permute-start(bf16[4,2,256,128]{3,2,0,1:T(8,128)(2,1)S(1)} %get-tuple-element.64), channel_id=1, source_target_pairs={{4,0},{8,4},{12,8},{16,12},{20,16},{24,20},{28,24},{32,28},{36,32}... | collective-permute-start | bytes 1572872 | tf_op jit(solution)/shard_map/ppermute | solution.py:39
  471.2 5.0 copy-start.19
  471.2 3.7 copy-start.24
  479.9 3.1 copy-start.20
  479.9 3.1 copy-start.23
  484.3 2.6 copy-start.26
  484.3 2.6 copy-start.27
  (8 other events, 7.8 us)

commit v6 on v4

--- a/solution.py
+++ b/solution.py
@@ -289,22 +289,20 @@
     asked_mask = (wanted_flat >= 0)[:, None, None]
     zero_block = jnp.zeros((), jnp.bfloat16)
     reply_shape = (peer_count, capacity, BS, local_width)
-    far_key, far_value = (
-        lax.all_to_all(
-            jnp.where(asked_mask, key_blocks[chosen], zero_block).reshape(reply_shape),
-            "blk",
-            split_axis=0,
-            concat_axis=0,
-            tiled=True,
-        ),
-        lax.all_to_all(
-            jnp.where(asked_mask, value_blocks[chosen], zero_block).reshape(reply_shape),
-            "blk",
-            split_axis=0,
-            concat_axis=0,
-            tiled=True,
-        ),
-    )
+    far_both = lax.all_to_all(
+        jnp.stack(
+            [
+                jnp.where(asked_mask, key_blocks[chosen], zero_block),
+                jnp.where(asked_mask, value_blocks[chosen], zero_block),
+            ],
+            axis=1,
+        ).reshape((peer_count, capacity, 2, BS, local_width)),
+        "blk",
+        split_axis=0,
+        concat_axis=0,
+        tiled=True,
+    )
+    far_key, far_value = far_both[:, :, 0], far_both[:, :, 1]
     near_count = QB_DEV + 2 * W
     far_total_count = peer_count * capacity
     key_table = jnp.concatenate(
@@ -339,10 +337,14 @@
     )
     outputs = (att_out, qg_out)
     column_shape = (peer_count, capacity, local_width, BS)
-    back_key, back_value = (
-        lax.all_to_all(fk.reshape(column_shape), "blk", split_axis=0, concat_axis=0, tiled=True),
-        lax.all_to_all(fv.reshape(column_shape), "blk", split_axis=0, concat_axis=0, tiled=True),
-    )
+    back_both = lax.all_to_all(
+        jnp.stack([fk, fv], axis=1).reshape((peer_count, capacity, 2, local_width, BS)),
+        "blk",
+        split_axis=0,
+        concat_axis=0,
+        tiled=True,
+    )
+    back_key, back_value = back_both[:, :, 0], back_both[:, :, 1]
     owner_match = (
         jnp.arange(QB_DEV, dtype=jnp.int32)[:, None] == wanted_here.reshape(1, -1)
     ).astype(jnp.bfloat16)

time: 501 us -> 510 us (1.018)
  blocking collectives: 143 us -> 29.7 us
  waiting for transfers between devices: 125 us -> 221 us
  other arithmetic: 30 us -> 43.2 us
  local copies, waits for them, and re-layouts: 31.5 us -> 38.3 us
  starting transfers between devices: 28.3 us -> 34.8 us
    all_to_all x2 -> x0, blocking collectives: 114 us -> none  [the longest x1 58.4 us: on_device(): lax.all_to_all(fk.reshape(column_shape), 'blk', split_axis=0, concat_axis...]
    ppermute x1, waiting for transfers between devices: 51.9 us -> 99.1 us  [padded(): lax.ppermute(lax.slice_in_dim(block, block.shape[dim] - width, None, axis...]
    ppermute x2, waiting for transfers between devices: 46.6 us -> 93.6 us  [shifted(): return lax.ppermute(block, axis, route)]
    another operation x1 -> x3, other arithmetic: 1.95 us -> 16.9 us  [the longest x1 7.48 us: on_device(): jnp.stack([jnp.where(asked_mask, key_blocks[chosen], zero_block), jnp.whe...]
    slice x1 -> x3, local copies, waits for them, and re-layouts: 1.65 us -> 9.65 us  [the longest x1 4.03 us: on_device(): far_key, far_value = (far_both[:, :, 0], far_both[:, :, 1])]
    all_to_all x2, starting transfers between devices: 11.9 us -> 18.4 us  [the longest x1 12.3 us: on_device(): lax.all_to_all(jnp.stack([fk, fv], axis=1).reshape((peer_count, capacity,...]
  transfers between devices with their start and end apart: 8 -> 8, of which waited for: 4 -> 5; matrix products, arithmetic and copies ran while one was open for 5% -> 4% of each run, Pallas kernels for 0% -> 0%
where the time goes in v6:
time: 510 us; the launch traced here: 507 us
  waiting for transfers between devices  221 us (43%)
  Pallas kernels  135 us (26%)
  other arithmetic  43.2 us (8%)
  local copies, waits for them, and re-layouts  38.3 us (8%)
  starting transfers between devices  34.8 us (7%)
  blocking collectives  29.7 us (6%)
    pallas_call x1, Pallas kernels, block_attention(): pl.pallas_call(kernel, grid_spec=grid_spec, out_shape=[jax.ShapeDtypeStru...  135 us
    ppermute x1, waiting for transfers between devices, padded(): lax.ppermute(lax.slice_in_dim(block, block.shape[dim] - width, None, axis...  99.1 us
    ppermute x2, waiting for transfers between devices, shifted(): return lax.ppermute(block, axis, route)  93.6 us
    all_to_all x1, blocking collectives, on_device(): lax.all_to_all(jnp.stack(results), 'head', split_axis=1, concat_axis=2, t...  29.7 us
    all_to_all x1, waiting for transfers between devices, on_device(): lax.all_to_all(jnp.stack([query_rows, key_rows, value_rows, out_grad]), '...  24.7 us
    all_to_all x1, starting transfers between devices, on_device(): lax.all_to_all(jnp.stack([fk, fv], axis=1).reshape((peer_count, capacity,...  12.3 us
  transfers between devices with their start and end apart: 8, of which 5 were waited for; matrix products, arithmetic and copies ran while one was open for 4% of the time, Pallas kernels for 0%

profile of v6, /device:TPU:8, one launch (start us, length us, event | category | flops | bytes accessed | tf_op | source)
XLA Modules:
  0.0 507.3 jit_solution(12856128319238327799)
XLA Ops:
  4.2 8.5 %all-to-all-start.1 = ((s32[32,1,2]{2,1,0:T(1,128)}), s32[32,1,2]{2,1,0:T(1,128)S(1)}, u32[]{:S(2)}, u32[]{:S(2)}) async-start(s32[32,1,2]{2,1,0:T(1,128)} %bitcast.13), calls=%async_computation.1 | async-start | bytes 32768 | tf_op jit(solution)/shard_map/all_to_all | solution.py:280
  12.8 1.8 pad_maximum_fusion.5
  14.6 2.7 copy.67
  17.2 1.7 all-to-all-done.1
  18.9 4.3 all-to-all-start
  24.8 24.7 %all-to-all-done = bf16[4,256,1024]{1,0,2:T(4,128)(2,1)S(1)} async-done(((bf16[4,256,1024]{1,0,2:T(4,128)(2,1)}), bf16[4,256,1024]{1,0,2:T(4,128)(2,1)S(1)}, u32[]{:S(2)}, u32[]{:S(2)}) %all-to-all-start) | async-done | bytes 2097184 | tf_op jit(solution)/shard_map/all_to_all | solution.py:254
  49.5 2.6 copy.68
  52.1 1.7 fusion.35
  53.8 2.8 gather_fusion.1
  56.6 2.8 gather_fusion
  59.4 5.8 %broadcast_select_fusion.1 = (bf16[32,2,1,128,256]{4,3,1,2,0:T(8,128)(2,1)}, bf16[32,2,1,128,256]{4,3,1,2,0:T(8,128)(2,1)}) fusion(bf16[32,2,1,128,256]{4,3,1,2,0:T(8,128)(2,1)} %bitcast.132, pred[32,2]{1,0:T(8,128)(4,1)S(1)} %copy.72, bf16[32,2,1,128,256]{4,3,1,2,0:T(8,128)(2,1)} %bitcast.131), kind=kLoop, calls=%fused_computation.22 | loop fusion | flops 4194304 | bytes 16777280 | tf_op jit(solution)/shard_map/jit(_where)/select_n | solution.py:295
  65.2 7.5 %pad_maximum_fusion = bf16[32,2,2,128,256]{4,3,1,2,0:T(8,128)(2,1)} fusion(bf16[32,2,1,128,256]{4,3,1,2,0:T(8,128)(2,1)} %get-tuple-element.63, bf16[32,2,1,128,256]{4,3,1,2,0:T(8,128)(2,1)} %get-tuple-element.62), kind=kLoop, calls=%fused_computation.3 | loop fusion | flops 4194304 | bytes 16777216 | tf_op jit(solution)/shard_map/stack | solution.py:293
  72.6 6.2 %all-to-all-start.2 = ((bf16[32,2,2,128,256]{4,3,1,2,0:T(8,128)(2,1)}), bf16[32,2,2,128,256]{4,3,1,2,0:T(8,128)(2,1)}, u32[]{:S(2)}, u32[]{:S(2)}) async-start(bf16[32,2,2,128,256]{4,3,1,2,0:T(8,128)(2,1)} %pad_maximum_fusion), calls=%async_computation.2 | async-start | bytes 16777216 | tf_op jit(solution)/shard_map/all_to_all | solution.py:292
  79.2 1.6 collective-permute-start.1
  81.1 99.1 %collective-permute-done = bf16[4,2,128,256]{3,2,0,1:T(8,128)(2,1)} collective-permute-done((bf16[4,2,128,256]{3,2,0,1:T(8,128)(2,1)S(1)}, bf16[4,2,128,256]{3,2,0,1:T(8,128)(2,1)}, u32[]{:S(2)}, u32[]{:S(2)}) %collective-permute-start) | collective-permute-done | bytes 524320 | tf_op jit(solution)/shard_map/ppermute | solution.py:28
  180.2 1.7 collective-permute-done.1
  183.6 4.0 fusion.32
  187.6 5.5 %pad_maximum_fusion.3 = (bf16[80,128,256]{2,1,0:T(8,128)(2,1)}, bf16[80,128,256]{2,1,0:T(8,128)(2,1)}) fusion(bf16[64,128,256]{2,1,0:T(8,128)(2,1)S(1)} %bitcast.134, bf16[16,128,256]{2,1,0:T(8,128)(2,1)S(1)} %get-tuple-element.55, bf16[64,128,256]{2,1,0:T(8,128)(2,1)S(1)} %bitcast.133, bf16[16,128,256]{2,1,0:T(8,128)(2,1)S(1)} %get-tuple-element.54), kind=kLoop, calls=%fused_computation.10 | loop fusion | flops 5242880 | bytes 20971520 | tf_op jit(solution)/shard_map/concatenate | solution.py:308
  193.1 134.9 %shard_map.120 = (bf16[1024,256]{1,0:T(8,128)(2,1)S(1)}, bf16[1024,256]{1,0:T(8,128)(2,1)S(1)}, f32[16,256,128]{2,1,0:T(8,128)S(1)}, f32[16,256,128]{2,1,0:T(8,1...) custom-call(s32[128]{0:T(128)S(1)} %reshape.230.rows_ref, s32[8]{0:T(128)S(1)} %copy-done.4, ...), custom_call_target="tpu_custom_call" | custom-call | flops 12884901888 | bytes 33554432 | tf_op jit(solution)/shard_map/pallas_call | solution.py:217
  329.6 7.5 %pad_maximum_fusion.1 = bf16[32,2,2,256,128]{4,3,1,2,0:T(8,128)(2,1)} fusion(bf16[32,2,1,256,128]{4,3,1,2,0:T(8,128)(2,1)} %bitcast.140, bf16[32,2,1,256,128]{4,3,1,2,0:T(8,128)(2,1)} %bitcast.139), kind=kLoop, calls=%fused_computation.4 | loop fusion | flops 4194304 | bytes 16777216 | tf_op jit(solution)/shard_map/stack | solution.py:341
  337.0 12.3 %all-to-all-start.3 = ((bf16[32,2,2,256,128]{4,3,1,2,0:T(8,128)(2,1)}), bf16[32,2,2,256,128]{4,3,1,2,0:T(8,128)(2,1)}, u32[]{:S(2)}, u32[]{:S(2)}) async-start(bf16[32,2,2,256,128]{4,3,1,2,0:T(8,128)(2,1)} %pad_maximum_fusion.1), calls=%async_computation.3 | async-start | bytes 16777216 | tf_op jit(solution)/shard_map/all_to_all | solution.py:340
  349.3 2.0 fusion
  354.0 2.9 fusion.7
  356.9 93.6 %collective-permute-done.2 = bf16[4,2,256,128]{3,2,0,1:T(8,128)(2,1)} collective-permute-done((bf16[4,2,256,128]{3,2,0,1:T(8,128)(2,1)}, bf16[4,2,256,128]{3,2,0,1:T(8,128)(2,1)}, u32[]{:S(2)}, u32[]{:S(2)}) %collective-permute-start.2) | collective-permute-done | bytes 524320 | tf_op jit(solution)/shard_map/ppermute | solution.py:39
  450.6 2.2 fusion.10
  452.7 2.3 fusion.15
  455.0 4.0 fusion.31
  459.0 2.3 fusion.4
  461.3 2.3 fusion.1
  463.7 2.1 fusion.17
  468.1 29.7 %all_to_all.49 = bf16[4,1024,256]{2,0,1:T(4,128)(2,1)S(1)} all-to-all(bf16[4,1024,256]{2,0,1:T(4,128)(2,1)S(1)} %copy.81), channel_id=1, replica_groups=mesh['blk'=32,'head'=4] {'head'}, dimensions={1} | all-to-all | bytes 4194304 | tf_op jit(solution)/shard_map/all_to_all | solution.py:378
  497.8 3.1 fusion.33
  (67 shorter events, 20.4 us)
Async XLA Ops:
  4.2 14.7 %all-to-all-start.1 = ((s32[32,1,2]{2,1,0:T(1,128)}), s32[32,1,2]{2,1,0:T(1,128)S(1)}, u32[]{:S(2)}, u32[]{:S(2)}) async-start(s32[32,1,2]{2,1,0:T(1,128)} %bitcast.13), calls=%async_computation.1 | async-start | bytes 32768 | tf_op jit(solution)/shard_map/all_to_all | solution.py:280
  18.9 30.7 %all-to-all-start = ((bf16[4,256,1024]{1,0,2:T(4,128)(2,1)}), bf16[4,256,1024]{1,0,2:T(4,128)(2,1)S(1)}, u32[]{:S(2)}, u32[]{:S(2)}) async-start(bf16[4,256,1024]{1,0,2:T(4,128)(2,1)} %copy.67), calls=%async_computation | async-start | bytes 4194304 | tf_op jit(solution)/shard_map/all_to_all | solution.py:254
  72.6 6.2 %copy-start.6 = (s32[4,8,16]{2,1,0:T(8,128)S(1)}, s32[4,8,16]{2,1,0:T(8,128)}, u32[]{:S(2)}) copy-start(s32[4,8,16]{2,1,0:T(8,128)} %param.21) | copy-start | bytes 6148
  72.6 8.2 %copy-start.7 = (s32[8,11]{1,0:T(8,128)S(1)}, s32[8,11]{1,0:T(8,128)}, u32[]{:S(2)}) copy-start(s32[8,11]{1,0:T(8,128)} %param.19) | copy-start | bytes 1060
  72.6 110.9 %all-to-all-start.2 = ((bf16[32,2,2,128,256]{4,3,1,2,0:T(8,128)(2,1)}), bf16[32,2,2,128,256]{4,3,1,2,0:T(8,128)(2,1)}, u32[]{:S(2)}, u32[]{:S(2)}) async-start(bf16[32,2,2,128,256]{4,3,1,2,0:T(8,128)(2,1)} %pad_maximum_fusion), calls=%async_computation.2 | async-start | bytes 16777216 | tf_op jit(solution)/shard_map/all_to_all | solution.py:292
  79.0 101.2 %collective-permute-start = (bf16[4,2,128,256]{3,2,0,1:T(8,128)(2,1)S(1)}, bf16[4,2,128,256]{3,2,0,1:T(8,128)(2,1)}, u32[]{:S(2)}, u32[]{:S(2)}) collective-permute-start(bf16[4,2,128,256]{3,2,0,1:T(8,128)(2,1)S(1)} %get-tuple-element.60), channel_id=1, source_target_pairs={{0,4},{4,8},{8,12},{12,16},{16,20},{20,24},{24,28},{28,32},{32,36}... | collective-permute-start | bytes 1572872 | tf_op jit(solution)/shard_map/ppermute | solution.py:28
  79.2 102.7 %collective-permute-start.1 = (bf16[4,2,128,256]{3,2,0,1:T(8,128)(2,1)S(1)}, bf16[4,2,128,256]{3,2,0,1:T(8,128)(2,1)}, u32[]{:S(2)}, u32[]{:S(2)}) collective-permute-start(bf16[4,2,128,256]{3,2,0,1:T(8,128)(2,1)S(1)} %get-tuple-element.61), channel_id=1, source_target_pairs={{4,0},{8,4},{12,8},{16,12},{20,16},{24,20},{28,24},{32,28},{36,32}... | collective-permute-start | bytes 1572872 | tf_op jit(solution)/shard_map/ppermute | solution.py:31
  187.6 5.5 %copy-start.4 = (s32[8]{0:T(128)S(1)}, s32[8]{0:T(128)}, u32[]{:S(2)}) copy-start(s32[8]{0:T(128)} %count_ref.1) | copy-start | bytes 100
  328.0 0.8 copy-start
  328.8 0.8 copy-start.2
  337.0 118.0 %all-to-all-start.3 = ((bf16[32,2,2,256,128]{4,3,1,2,0:T(8,128)(2,1)}), bf16[32,2,2,256,128]{4,3,1,2,0:T(8,128)(2,1)}, u32[]{:S(2)}, u32[]{:S(2)}) async-start(bf16[32,2,2,256,128]{4,3,1,2,0:T(8,128)(2,1)} %pad_maximum_fusion.1), calls=%async_computation.3 | async-start | bytes 16777216 | tf_op jit(solution)/shard_map/all_to_all | solution.py:340
  352.2 98.4 %collective-permute-start.2 = (bf16[4,2,256,128]{3,2,0,1:T(8,128)(2,1)}, bf16[4,2,256,128]{3,2,0,1:T(8,128)(2,1)}, u32[]{:S(2)}, u32[]{:S(2)}) collective-permute-start(bf16[4,2,256,128]{3,2,0,1:T(8,128)(2,1)} %get-tuple-element.53), channel_id=1, source_target_pairs={{124,0},{0,4},{4,8},{8,12},{12,16},{16,20},{20,24},{24,28},{28,32}... | collective-permute-start | bytes 1572872 | tf_op jit(solution)/shard_map/ppermute | solution.py:39
  352.3 100.5 %collective-permute-start.3 = (bf16[4,2,256,128]{3,2,0,1:T(8,128)(2,1)S(1)}, bf16[4,2,256,128]{3,2,0,1:T(8,128)(2,1)S(1)}, u32[]{:S(2)}, u32[]{:S(2)}) collective-permute-start(bf16[4,2,256,128]{3,2,0,1:T(8,128)(2,1)S(1)} %get-tuple-element.52), channel_id=1, source_target_pairs={{4,0},{8,4},{12,8},{16,12},{20,16},{24,20},{28,24},{32,28},{36,32}... | collective-permute-start | bytes 1572872 | tf_op jit(solution)/shard_map/ppermute | solution.py:39
  354.0 96.6 %copy-start.5 = (f32[16,256,128]{2,1,0:T(8,128)S(1)}, f32[16,256,128]{2,1,0:T(8,128)}, u32[]{:S(2)}) copy-start(f32[16,256,128]{2,1,0:T(8,128)} %get-tuple-element.37) | copy-start | bytes 6291460
  463.7 2.6 copy-start.1
  463.7 2.6 copy-start.3

commit v7 on v4

--- a/solution.py
+++ b/solution.py
@@ -251,16 +251,11 @@
     head_size = local_width // local_heads
     score_scale = head_size ** (-0.5)
     slot_count = 1 + L + E
-    exchanged = lax.all_to_all(
-        jnp.stack([query_rows, key_rows, value_rows, out_grad]),
-        "head",
-        split_axis=2,
-        concat_axis=1,
-        tiled=True,
-    )
-    query_local, key_local, value_local, grad_local = (
-        exchanged[0], exchanged[1], exchanged[2], exchanged[3]
-    )
+    def to_columns(arrays):
+        return lax.all_to_all(jnp.stack(arrays), "head", split_axis=2, concat_axis=1, tiled=True)
+
+    key_local, value_local = to_columns([key_rows, value_rows])
+    query_local, grad_local = to_columns([query_rows, out_grad])
     peer_count = lax.axis_size("blk")
     capacity = min(QB_DEV, max(2, (2 * QB_DEV * E + peer_count - 1) // peer_count))
     flat_device = expander_device.reshape(-1)
@@ -272,13 +267,17 @@
     far_position = flat_device * capacity + slot_rank
     far_live = jnp.arange(E, dtype=jnp.int32)[None, :] < live_count[:, None]
     asked_block = jnp.where(far_live, expander_block, -1)
-    wanted = (
-        jnp.full((peer_count * capacity,), -1, jnp.int32)
-        .at[far_position]
-        .set(asked_block.reshape(-1))
-    )
-    wanted_here = lax.all_to_all(
-        wanted.reshape(peer_count, capacity), "blk", split_axis=0, concat_axis=0, tiled=True
+    listing = lax.all_gather(
+        jnp.stack([flat_device, asked_block.reshape(-1)]), "blk", axis=0, tiled=False
+    )
+    hit = (listing[:, 0] == lax.axis_index("blk")).astype(jnp.int32)
+    hit_rank = jnp.cumsum(hit, axis=1) - hit
+    wanted_here = jnp.stack(
+        [
+            jnp.sum(jnp.where((hit > 0) & (hit_rank == r), listing[:, 1] + 1, 0), axis=1) - 1
+            for r in range(capacity)
+        ],
+        axis=1,
     )
     key_blocks = key_local.reshape(QB_DEV, BS, local_width)
     value_blocks = value_local.reshape(QB_DEV, BS, local_width)
@@ -367,14 +366,18 @@
     block_rows = QB_DEV * BS
     key_grad = (own_total[:, 0] + far_key_sum).astype(jnp.bfloat16).transpose(0, 2, 1)
     value_grad = (own_total[:, 1] + far_value_sum).astype(jnp.bfloat16).transpose(0, 2, 1)
-    results = (
+    def to_rows(arrays):
+        return lax.all_to_all(jnp.stack(arrays), "head", split_axis=1, concat_axis=2, tiled=True)
+
+    attended, query_grad = to_rows([
         outputs[0].reshape(block_rows, local_width),
         outputs[1].reshape(block_rows, local_width),
+    ])
+    key_grad, value_grad = to_rows([
         key_grad.reshape(block_rows, local_width),
         value_grad.reshape(block_rows, local_width),
-    )
-    returned = lax.all_to_all(jnp.stack(results), "head", split_axis=1, concat_axis=2, tiled=True)
-    return tuple(returned[i] for i in range(len(results)))
+    ])
+    return attended, query_grad, key_grad, value_grad
 
 
 def solution(mesh):

time: 501 us -> 484 us (0.966)
  waiting for transfers between devices: 125 us -> 112 us
    all_to_all x1 -> x0, blocking collectives: 29.1 us -> none  [on_device(): lax.all_to_all(jnp.stack(results), 'head', split_axis=1, concat_axis=2, t...]
    all_gather x0 -> x1, blocking collectives: none -> 25.5 us  [on_device(): lax.all_gather(jnp.stack([flat_device, asked_block.reshape(-1)]), 'blk',...]
    another operation x2 -> x17, local copies, waits for them, and re-layouts: 4.27 us -> 13.6 us  [the longest x2 4.15 us: to_rows(): jnp.stack(arrays)]
    slice x6 -> x1, local copies, waits for them, and re-layouts: 7.5 us -> 0.03 us  [on_device(): hit = (listing[:, 0] == lax.axis_index('blk')).astype(jnp.int32)]
    all_to_all x2 -> x4, waiting for transfers between devices: 26.4 us -> 19.6 us  [the longest x2 16 us: to_rows(): lax.all_to_all(jnp.stack(arrays), 'head', split_axis=1, concat_axis=2, ti...]
    all_to_all x2 -> x4, starting transfers between devices: 12.8 us -> 16.4 us  [the longest x2 9.1 us: to_columns(): lax.all_to_all(jnp.stack(arrays), 'head', split_axis=2, concat_axis=1, ti...]
  transfers between devices with their start and end apart: 8 -> 10, of which waited for: 4 -> 5; matrix products, arithmetic and copies ran while one was open for 5% -> 11% of each run, Pallas kernels for 0% -> 0%
where the time goes in v7:
time: 484 us; the launch traced here: 483 us
  blocking collectives  139 us (29%)
  Pallas kernels  135 us (28%)
  waiting for transfers between devices  112 us (23%)
  starting transfers between devices  32.1 us (7%)
  other arithmetic  28.8 us (6%)
  local copies, waits for them, and re-layouts  27.9 us (6%)
  matrix products  6.83 us (1%)
    pallas_call x1, Pallas kernels, block_attention(): pl.pallas_call(kernel, grid_spec=grid_spec, out_shape=[jax.ShapeDtypeStru...  135 us
    all_to_all x1, blocking collectives, on_device(): lax.all_to_all(fk.reshape(column_shape), 'blk', split_axis=0, concat_axis...  58.4 us
    all_to_all x1, blocking collectives, on_device(): lax.all_to_all(jnp.where(asked_mask, value_blocks[chosen], zero_block).re...  55.4 us
    ppermute x1, waiting for transfers between devices, padded(): lax.ppermute(lax.slice_in_dim(block, block.shape[dim] - width, None, axis...  47.3 us
    ppermute x2, waiting for transfers between devices, shifted(): return lax.ppermute(block, axis, route)  45.1 us
    all_gather x1, blocking collectives, on_device(): lax.all_gather(jnp.stack([flat_device, asked_block.reshape(-1)]), 'blk',...  25.5 us
    all_to_all x2, waiting for transfers between devices, to_rows(): lax.all_to_all(jnp.stack(arrays), 'head', split_axis=1, concat_axis=2, ti...  16 us
  transfers between devices with their start and end apart: 10, of which 5 were waited for; matrix products, arithmetic and copies ran while one was open for 11% of the time, Pallas kernels for 0%

profile of v7, /device:TPU:8, one launch (start us, length us, event | category | flops | bytes accessed | tf_op | source)
XLA Modules:
  0.0 483.0 jit_solution(725706088870960601)
XLA Ops:
  2.1 2.0 copy.135
  4.1 4.3 all-to-all-start.1
  8.8 25.5 %all-gather.1 = s32[32,2,32]{2,1,0:T(2,128)S(1)} all-gather(s32[1,2,32]{2,1,0:T(2,128)S(1)} %add_bitcast_fusion), channel_id=2, replica_groups=mesh['blk'=32,'head'=4] {'blk'}, dimensions={0}, use_global_device_ids=true | all-gather | bytes 8448 | tf_op jit(solution)/shard_map/all_gather | solution.py:270
  35.0 2.1 copy.133
  37.1 4.8 all-to-all-start
  42.6 2.8 gather_fusion
  45.3 2.8 gather_fusion.1
  48.1 5.9 %broadcast_select_fusion = (bf16[32,2,128,256]{3,2,1,0:T(8,128)(2,1)}, bf16[32,2,128,256]{3,2,1,0:T(8,128)(2,1)}) fusion(bf16[32,2,128,256]{3,2,1,0:T(8,128)(2,1)} %bitcast.137, pred[32,2]{1,0:T(8,128)(4,1)S(1)} %copy.143, bf16[32,2,128,256]{3,2,1,0:T(8,128)(2,1)} %bitcast.136), kind=kLoop, calls=%fused_computation.18 | loop fusion | flops 4194304 | bytes 16777280 | tf_op jit(solution)/shard_map/jit(_where)/select_n | solution.py:300
  54.0 3.6 all-to-all-done
  57.5 55.4 %all_to_all.80 = bf16[32,2,128,256]{3,2,1,0:T(8,128)(2,1)} all-to-all(bf16[32,2,128,256]{3,2,1,0:T(8,128)(2,1)} %get-tuple-element.76), channel_id=1, replica_groups=mesh['blk'=32,'head'=4] {'blk'}, dimensions={0} | all-to-all | bytes 8388608 | tf_op jit(solution)/shard_map/all_to_all | solution.py:299
  112.9 6.0 %all-to-all-start.2 = ((bf16[32,2,128,256]{3,2,1,0:T(8,128)(2,1)}), bf16[32,2,128,256]{3,2,1,0:T(8,128)(2,1)}, u32[]{:S(2)}, u32[]{:S(2)}) async-start(bf16[32,2,128,256]{3,2,1,0:T(8,128)(2,1)} %get-tuple-element.77), calls=%async_computation.2 | async-start | bytes 8388608 | tf_op jit(solution)/shard_map/all_to_all | solution.py:292
  122.6 2.0 copy.134
  125.8 47.3 %collective-permute-done = bf16[4,2,128,256]{3,2,0,1:T(8,128)(2,1)} collective-permute-done((bf16[4,2,128,256]{3,2,0,1:T(8,128)(2,1)}, bf16[4,2,128,256]{3,2,0,1:T(8,128)(2,1)}, u32[]{:S(2)}, u32[]{:S(2)}) %collective-permute-start) | collective-permute-done | bytes 524320 | tf_op jit(solution)/shard_map/ppermute | solution.py:28
  174.8 2.8 pad_maximum_fusion.2
  177.6 5.0 %pad_maximum_fusion.1 = bf16[80,128,256]{2,1,0:T(8,128)(2,1)} fusion(bf16[64,128,256]{2,1,0:T(8,128)(2,1)} %bitcast.22, bf16[16,128,256]{2,1,0:T(8,128)(2,1)S(1)} %get-tuple-element.63), kind=kLoop, calls=%fused_computation.7 | loop fusion | flops 2621440 | bytes 10485760 | tf_op jit(solution)/shard_map/concatenate | solution.py:309
  182.6 135.2 %shard_map.120 = (bf16[1024,256]{1,0:T(8,128)(2,1)S(1)}, bf16[1024,256]{1,0:T(8,128)(2,1)S(1)}, f32[16,256,128]{2,1,0:T(8,128)S(1)}, f32[16,256,128]{2,1,0:T(8,1...) custom-call(s32[128]{0:T(128)S(1)} %reshape.205.rows_ref, s32[8]{0:T(128)S(1)} %copy-done.4, ...), custom_call_target="tpu_custom_call" | custom-call | flops 12884901888 | bytes 33554432 | tf_op jit(solution)/shard_map/pallas_call | solution.py:217
  317.8 58.4 %all_to_all.81 = bf16[32,2,256,128]{3,2,1,0:T(8,128)(2,1)} all-to-all(bf16[32,2,256,128]{3,2,1,0:T(8,128)(2,1)} %bitcast.144), channel_id=1, replica_groups=mesh['blk'=32,'head'=4] {'blk'}, dimensions={0} | all-to-all | bytes 8388608 | tf_op jit(solution)/shard_map/all_to_all | solution.py:342
  376.2 5.9 %all-to-all-start.6 = ((bf16[32,2,256,128]{3,2,1,0:T(8,128)(2,1)}), bf16[32,2,256,128]{3,2,1,0:T(8,128)(2,1)}, u32[]{:S(2)}, u32[]{:S(2)}) async-start(bf16[32,2,256,128]{3,2,1,0:T(8,128)(2,1)} %bitcast.142), calls=%async_computation.6 | async-start | bytes 8388608 | tf_op jit(solution)/shard_map/all_to_all | solution.py:343
  382.2 2.1 fusion
  385.6 1.9 collective-permute-start.3
  387.6 2.1 copy.147
  391.2 45.1 %collective-permute-done.2 = bf16[4,2,256,128]{3,2,0,1:T(8,128)(2,1)} collective-permute-done((bf16[4,2,256,128]{3,2,0,1:T(8,128)(2,1)}, bf16[4,2,256,128]{3,2,0,1:T(8,128)(2,1)}, u32[]{:S(2)}, u32[]{:S(2)}) %collective-permute-start.2) | collective-permute-done | bytes 524320 | tf_op jit(solution)/shard_map/ppermute | solution.py:39
  436.3 2.2 fusion.10
  438.5 2.3 fusion.15
  440.9 2.3 fusion.4
  443.2 3.5 all-to-all-start.4
  446.7 4.5 fusion.1
  451.2 2.0 fusion.17
  453.8 2.1 copy.157
  455.9 6.3 %all-to-all-done.4 = bf16[2,1024,256]{2,0,1:T(2,128)(2,1)S(1)} async-done(((bf16[2,1024,256]{2,0,1:T(2,128)(2,1)}), bf16[2,1024,256]{2,0,1:T(2,128)(2,1)S(1)}, u32[]{:S(2)}, u32[]{:S(2)}) %all-to-all-start.4) | async-done | bytes 1048608 | tf_op jit(solution)/shard_map/all_to_all | solution.py:370
  462.2 3.8 all-to-all-start.7
  470.6 9.7 %all-to-all-done.7 = bf16[2,1024,256]{2,0,1:T(2,128)(2,1)S(1)} async-done(((bf16[2,1024,256]{2,0,1:T(2,128)(2,1)}), bf16[2,1024,256]{2,0,1:T(2,128)(2,1)S(1)}, u32[]{:S(2)}, u32[]{:S(2)}) %all-to-all-start.7) | async-done | bytes 1048608 | tf_op jit(solution)/shard_map/all_to_all | solution.py:370
  (95 shorter events, 20.5 us)
Async XLA Ops:
  0.6 7.8 %copy-start.4 = (s32[8]{0:T(128)S(1)}, s32[8]{0:T(128)}, u32[]{:S(2)}) copy-start(s32[8]{0:T(128)} %count_ref.1) | copy-start | bytes 100
  0.6 7.8 %copy-start.13 = (s32[8,4]{0,1:T(4,128)S(1)}, s32[8,4]{0,1:T(4,128)}, u32[]{:S(2)}) copy-start(s32[8,4]{0,1:T(4,128)} %param.18) | copy-start | bytes 388
  0.7 7.9 %copy-start.12 = (s32[8,4]{0,1:T(4,128)S(1)}, s32[8,4]{0,1:T(4,128)}, u32[]{:S(2)}) copy-start(s32[8,4]{0,1:T(4,128)} %param.17) | copy-start | bytes 388
  0.7 34.3 %copy-start.8 = (bf16[256,1024]{1,0:T(8,128)(2,1)S(1)}, bf16[256,1024]{1,0:T(8,128)(2,1)}, u32[]{:S(2)}) copy-start(bf16[256,1024]{1,0:T(8,128)(2,1)} %param.16) | copy-start | bytes 1572868
  0.7 34.3 %copy-start.9 = (bf16[256,1024]{1,0:T(8,128)(2,1)S(1)}, bf16[256,1024]{1,0:T(8,128)(2,1)}, u32[]{:S(2)}) copy-start(bf16[256,1024]{1,0:T(8,128)(2,1)} %param.13) | copy-start | bytes 1572868
  4.1 33.0 %all-to-all-start.1 = ((bf16[2,256,1024]{1,0,2:T(2,128)(2,1)}), bf16[2,256,1024]{1,0,2:T(2,128)(2,1)S(1)}, u32[]{:S(2)}, u32[]{:S(2)}) async-start(bf16[2,256,1024]{1,0,2:T(2,128)(2,1)} %copy.135), calls=%async_computation.1 | async-start | bytes 2097152 | tf_op jit(solution)/shard_map/all_to_all | solution.py:255
  37.1 20.4 %all-to-all-start = ((bf16[2,256,1024]{1,0,2:T(2,128)(2,1)}), bf16[2,256,1024]{1,0,2:T(2,128)(2,1)S(1)}, u32[]{:S(2)}, u32[]{:S(2)}) async-start(bf16[2,256,1024]{1,0,2:T(2,128)(2,1)} %copy.133), calls=%async_computation | async-start | bytes 2097152 | tf_op jit(solution)/shard_map/all_to_all | solution.py:255
  112.9 9.3 %copy-start.11 = (s32[8,11]{1,0:T(8,128)S(1)}, s32[8,11]{1,0:T(8,128)}, u32[]{:S(2)}) copy-start(s32[8,11]{1,0:T(8,128)} %param.19) | copy-start | bytes 1060
  112.9 9.4 %copy-start.10 = (s32[4,8,16]{2,1,0:T(8,128)S(1)}, s32[4,8,16]{2,1,0:T(8,128)}, u32[]{:S(2)}) copy-start(s32[4,8,16]{2,1,0:T(8,128)} %param.21) | copy-start | bytes 6148
  112.9 64.7 %all-to-all-start.2 = ((bf16[32,2,128,256]{3,2,1,0:T(8,128)(2,1)}), bf16[32,2,128,256]{3,2,1,0:T(8,128)(2,1)}, u32[]{:S(2)}, u32[]{:S(2)}) async-start(bf16[32,2,128,256]{3,2,1,0:T(8,128)(2,1)} %get-tuple-element.77), calls=%async_computation.2 | async-start | bytes 8388608 | tf_op jit(solution)/shard_map/all_to_all | solution.py:292
  120.5 52.6 %collective-permute-start = (bf16[4,2,128,256]{3,2,0,1:T(8,128)(2,1)}, bf16[4,2,128,256]{3,2,0,1:T(8,128)(2,1)}, u32[]{:S(2)}, u32[]{:S(2)}) collective-permute-start(bf16[4,2,128,256]{3,2,0,1:T(8,128)(2,1)} %get-tuple-element.68), channel_id=1, source_target_pairs={{0,4},{4,8},{8,12},{12,16},{16,20},{20,24},{24,28},{28,32},{32,36}... | collective-permute-start | bytes 1572872 | tf_op jit(solution)/shard_map/ppermute | solution.py:28
  120.6 52.5 %collective-permute-start.1 = (bf16[4,2,128,256]{3,2,0,1:T(8,128)(2,1)}, bf16[4,2,128,256]{3,2,0,1:T(8,128)(2,1)}, u32[]{:S(2)}, u32[]{:S(2)}) collective-permute-start(bf16[4,2,128,256]{3,2,0,1:T(8,128)(2,1)} %get-tuple-element.69), channel_id=1, source_target_pairs={{4,0},{8,4},{12,8},{16,12},{20,16},{24,20},{28,24},{32,28},{36,32}... | collective-permute-start | bytes 1572872 | tf_op jit(solution)/shard_map/ppermute | solution.py:31
  125.8 49.0 %copy-start.6 = (bf16[32,2,128,256]{3,2,1,0:T(8,128)(2,1)S(1)}, bf16[32,2,128,256]{3,2,1,0:T(8,128)(2,1)}, u32[]{:S(2)}) copy-start(bf16[32,2,128,256]{3,2,1,0:T(8,128)(2,1)} %all_to_all.80) | copy-start | bytes 12582916
  317.8 58.4 %copy-start = (bf16[1024,256]{1,0:T(8,128)(2,1)}, bf16[1024,256]{1,0:T(8,128)(2,1)S(1)}, u32[]{:S(2)}) copy-start(bf16[1024,256]{1,0:T(8,128)(2,1)S(1)} %get-tuple-element.34) | copy-start | bytes 1572868
  317.8 58.4 %copy-start.2 = (bf16[1024,256]{1,0:T(8,128)(2,1)}, bf16[1024,256]{1,0:T(8,128)(2,1)S(1)}, u32[]{:S(2)}) copy-start(bf16[1024,256]{1,0:T(8,128)(2,1)S(1)} %get-tuple-element.35) | copy-start | bytes 1572868
  376.2 66.9 %all-to-all-start.6 = ((bf16[32,2,256,128]{3,2,1,0:T(8,128)(2,1)}), bf16[32,2,256,128]{3,2,1,0:T(8,128)(2,1)}, u32[]{:S(2)}, u32[]{:S(2)}) async-start(bf16[32,2,256,128]{3,2,1,0:T(8,128)(2,1)} %bitcast.142), calls=%async_computation.6 | async-start | bytes 8388608 | tf_op jit(solution)/shard_map/all_to_all | solution.py:343
  382.1 5.4 %copy-start.1 = (bf16[1024,256]{1,0:T(8,128)(2,1)S(1)}, bf16[1024,256]{1,0:T(8,128)(2,1)}, u32[]{:S(2)}) copy-start(bf16[1024,256]{1,0:T(8,128)(2,1)} %copy-done) | copy-start | bytes 1572868
  382.2 5.4 %copy-start.3 = (bf16[1024,256]{1,0:T(8,128)(2,1)S(1)}, bf16[1024,256]{1,0:T(8,128)(2,1)}, u32[]{:S(2)}) copy-start(bf16[1024,256]{1,0:T(8,128)(2,1)} %copy-done.2) | copy-start | bytes 1572868
  385.3 51.1 %collective-permute-start.2 = (bf16[4,2,256,128]{3,2,0,1:T(8,128)(2,1)}, bf16[4,2,256,128]{3,2,0,1:T(8,128)(2,1)}, u32[]{:S(2)}, u32[]{:S(2)}) collective-permute-start(bf16[4,2,256,128]{3,2,0,1:T(8,128)(2,1)} %get-tuple-element.61), channel_id=1, source_target_pairs={{124,0},{0,4},{4,8},{8,12},{12,16},{16,20},{20,24},{24,28},{28,32}... | collective-permute-start | bytes 1572872 | tf_op jit(solution)/shard_map/ppermute | solution.py:39
  385.6 4.1 copy-start.5
  385.6 52.9 %collective-permute-start.3 = (bf16[4,2,256,128]{3,2,0,1:T(8,128)(2,1)}, bf16[4,2,256,128]{3,2,0,1:T(8,128)(2,1)S(1)}, u32[]{:S(2)}, u32[]{:S(2)}) collective-permute-start(bf16[4,2,256,128]{3,2,0,1:T(8,128)(2,1)} %get-tuple-element.60), channel_id=1, source_target_pairs={{4,0},{8,4},{12,8},{16,12},{20,16},{24,20},{28,24},{32,28},{36,32}... | collective-permute-start | bytes 1572872 | tf_op jit(solution)/shard_map/ppermute | solution.py:39
  391.2 49.6 %copy-start.7 = (bf16[32,2,256,128]{3,2,1,0:T(8,128)(2,1)S(1)}, bf16[32,2,256,128]{3,2,1,0:T(8,128)(2,1)}, u32[]{:S(2)}) copy-start(bf16[32,2,256,128]{3,2,1,0:T(8,128)(2,1)} %all_to_all.81) | copy-start | bytes 12582916
  443.2 19.0 %all-to-all-start.4 = ((bf16[2,1024,256]{2,0,1:T(2,128)(2,1)}), bf16[2,1024,256]{2,0,1:T(2,128)(2,1)S(1)}, u32[]{:S(2)}, u32[]{:S(2)}) async-start(bf16[2,1024,256]{2,0,1:T(2,128)(2,1)} %copy.147), calls=%async_computation.4 | async-start | bytes 2097152 | tf_op jit(solution)/shard_map/all_to_all | solution.py:370
  462.2 18.2 %all-to-all-start.7 = ((bf16[2,1024,256]{2,0,1:T(2,128)(2,1)}), bf16[2,1024,256]{2,0,1:T(2,128)(2,1)S(1)}, u32[]{:S(2)}, u32[]{:S(2)}) async-start(bf16[2,1024,256]{2,0,1:T(2,128)(2,1)} %copy.157), calls=%async_computation.7 | async-start | bytes 2097152 | tf_op jit(solution)/shard_map/all_to_all | solution.py:370

commit v8 on v7

--- a/solution.py
+++ b/solution.py
@@ -116,10 +116,13 @@
     nt = (((1,), (1,)), ((), ()))
     f32 = jnp.float32
     m = [jnp.full((BS, BS), -jnp.inf, f32) for _ in range(pair)]
+    q_stack = jnp.concatenate(q_parts, axis=0)
+    g_stack = jnp.concatenate(g_parts, axis=0)
     for j in range(slot_count):
         k = keys(j)
+        s_both = lax.dot_general(q_stack, k, nt, preferred_element_type=f32)
         for a in range(pair):
-            s = lax.dot_general(q_parts[a], k, nt, preferred_element_type=f32)
+            s = s_both[a * BS : (a + 1) * BS]
             if j > L:
                 s = jnp.where(j < live_end, s, MASKED)
             s_scr[a, j] = s
@@ -136,9 +139,10 @@
         lax.broadcasted_iota(jnp.int32, (BS, BS), 0) * BS
         + lax.broadcasted_iota(jnp.int32, (BS, BS), 1)
     )
-    acc = [jnp.zeros((BS, width), f32) for _ in range(pair)]
+    acc_both = jnp.zeros((pair * BS, width), f32)
     for j in range(slot_count):
         v = values(j)
+        drops = []
         for a in range(pair):
             att = s_scr[a, j] * inv[a]
             s_scr[a, j] = att
@@ -152,26 +156,36 @@
             keep_scr[a, j] = keep
             dropped = (att * keep).astype(jnp.bfloat16)
             drop_scr[a, j] = dropped
-            acc[a] = acc[a] + jnp.dot(dropped, v, preferred_element_type=f32)
+            drops.append(dropped)
+        acc_both = acc_both + jnp.dot(
+            jnp.concatenate(drops, axis=0), v, preferred_element_type=f32
+        )
+    acc = [acc_both[a * BS : (a + 1) * BS] for a in range(pair)]
     attended = pick(acc, lane_head)
     att_ref[...] = attended.astype(att_ref.dtype)
     spread = g.astype(f32) * attended
     delta = [
         jnp.sum(jnp.where(lane_head == a, spread, 0.0), axis=1, keepdims=True) for a in range(pair)
     ]
-    qacc = [jnp.zeros((BS, width), f32) for _ in range(pair)]
+    qacc_both = jnp.zeros((pair * BS, width), f32)
     for j in range(slot_count):
         k = keys(j)
         v = values(j)
-        kps, vps = [], []
+        dg_both = lax.dot_general(g_stack, v, nt, preferred_element_type=f32)
+        sgs = []
         for a in range(pair):
-            dg = lax.dot_general(g_parts[a], v, nt, preferred_element_type=f32)
-            sg = (s_scr[a, j] * (dg * keep_scr[a, j] - delta[a])).astype(jnp.bfloat16)
-            qacc[a] = qacc[a] + jnp.dot(sg, k, preferred_element_type=f32)
-            kps.append(jnp.dot(q_t, sg, preferred_element_type=f32))
-            vps.append(jnp.dot(g_t, drop_scr[a, j], preferred_element_type=f32))
-        kp = pick(kps, row_head)
-        vp = pick(vps, row_head)
+            dg = dg_both[a * BS : (a + 1) * BS]
+            sgs.append((s_scr[a, j] * (dg * keep_scr[a, j] - delta[a])).astype(jnp.bfloat16))
+        qacc_both = qacc_both + jnp.dot(
+            jnp.concatenate(sgs, axis=0), k, preferred_element_type=f32
+        )
+        kp_both = jnp.dot(q_t, jnp.concatenate(sgs, axis=1), preferred_element_type=f32)
+        vp_both = jnp.dot(
+            g_t, jnp.concatenate([drop_scr[a, j] for a in range(pair)], axis=1),
+            preferred_element_type=f32,
+        )
+        kp = pick([kp_both[:, a * BS : (a + 1) * BS] for a in range(pair)], row_head)
+        vp = pick([vp_both[:, a * BS : (a + 1) * BS] for a in range(pair)], row_head)
         at = rows_ref[base + j]
         if j <= L:
             nk_ref[at] += kp
@@ -179,6 +193,7 @@
         else:
             fk_ref[at - near_count] = kp.astype(fk_ref.dtype)
             fv_ref[at - near_count] = vp.astype(fv_ref.dtype)
+    qacc = [qacc_both[a * BS : (a + 1) * BS] for a in range(pair)]
     qg_ref[...] = (pick(qacc, lane_head) * scale).astype(qg_ref.dtype)
 
 

time: 484 us -> 427 us (0.88)
  Pallas kernels: 135 us -> 78 us
    pallas_call x1, Pallas kernels: 135 us -> 78 us  [block_attention(): pl.pallas_call(kernel, grid_spec=grid_spec, out_shape=[jax.ShapeDtypeStru...]
  transfers between devices with their start and end apart: 10 -> 10, of which waited for: 5 -> 5; matrix products, arithmetic and copies ran while one was open for 11% -> 12% of each run, Pallas kernels for 0% -> 0%
where the time goes in v8:
time: 427 us; the launch traced here: 426 us
  blocking collectives  139 us (33%)
  waiting for transfers between devices  112 us (26%)
  Pallas kernels  78 us (18%)
  starting transfers between devices  32 us (7%)
  other arithmetic  28.8 us (7%)
  local copies, waits for them, and re-layouts  27.9 us (7%)
  matrix products  6.83 us (2%)
    pallas_call x1, Pallas kernels, block_attention(): pl.pallas_call(kernel, grid_spec=grid_spec, out_shape=[jax.ShapeDtypeStru...  78 us
    all_to_all x1, blocking collectives, on_device(): lax.all_to_all(fk.reshape(column_shape), 'blk', split_axis=0, concat_axis...  58.4 us
    all_to_all x1, blocking collectives, on_device(): lax.all_to_all(jnp.where(asked_mask, value_blocks[chosen], zero_block).re...  55.4 us
    ppermute x1, waiting for transfers between devices, padded(): lax.ppermute(lax.slice_in_dim(block, block.shape[dim] - width, None, axis...  47.3 us
    ppermute x2, waiting for transfers between devices, shifted(): return lax.ppermute(block, axis, route)  45.3 us
    all_gather x1, blocking collectives, on_device(): lax.all_gather(jnp.stack([flat_device, asked_block.reshape(-1)]), 'blk',...  25.5 us
    all_to_all x2, waiting for transfers between devices, to_rows(): lax.all_to_all(jnp.stack(arrays), 'head', split_axis=1, concat_axis=2, ti...  16.1 us
    all_to_all x2, starting transfers between devices, to_columns(): lax.all_to_all(jnp.stack(arrays), 'head', split_axis=2, concat_axis=1, ti...  9.1 us
  transfers between devices with their start and end apart: 10, of which 5 were waited for; matrix products, arithmetic and copies ran while one was open for 12% of the time, Pallas kernels for 0%

profile of v8, /device:TPU:8, one launch (start us, length us, event | category | flops | bytes accessed | tf_op | source)
XLA Modules:
  0.0 426.0 jit_solution(13825228017245305101)
XLA Ops:
  2.1 2.0 copy.135
  4.1 4.3 %all-to-all-start.1 = ((bf16[2,256,1024]{1,0,2:T(2,128)(2,1)}), bf16[2,256,1024]{1,0,2:T(2,128)(2,1)S(1)}, u32[]{:S(2)}, u32[]{:S(2)}) async-start(bf16[2,256,1024]{1,0,2:T(2,128)(2,1)} %copy.135), calls=%async_computation.1 | async-start | bytes 2097152 | tf_op jit(solution)/shard_map/all_to_all | solution.py:270
  8.8 25.5 %all-gather.1 = s32[32,2,32]{2,1,0:T(2,128)S(1)} all-gather(s32[1,2,32]{2,1,0:T(2,128)S(1)} %add_bitcast_fusion), channel_id=2, replica_groups=mesh['blk'=32,'head'=4] {'blk'}, dimensions={0}, use_global_device_ids=true | all-gather | bytes 8448 | tf_op jit(solution)/shard_map/all_gather | solution.py:285
  35.0 2.1 copy.133
  37.1 4.8 %all-to-all-start = ((bf16[2,256,1024]{1,0,2:T(2,128)(2,1)}), bf16[2,256,1024]{1,0,2:T(2,128)(2,1)S(1)}, u32[]{:S(2)}, u32[]{:S(2)}) async-start(bf16[2,256,1024]{1,0,2:T(2,128)(2,1)} %copy.133), calls=%async_computation | async-start | bytes 2097152 | tf_op jit(solution)/shard_map/all_to_all | solution.py:270
  42.6 2.8 gather_fusion
  45.3 2.8 gather_fusion.1
  48.1 5.9 %broadcast_select_fusion = (bf16[32,2,128,256]{3,2,1,0:T(8,128)(2,1)}, bf16[32,2,128,256]{3,2,1,0:T(8,128)(2,1)}) fusion(bf16[32,2,128,256]{3,2,1,0:T(8,128)(2,1)} %bitcast.137, pred[32,2]{1,0:T(8,128)(4,1)S(1)} %copy.143, bf16[32,2,128,256]{3,2,1,0:T(8,128)(2,1)} %bitcast.136), kind=kLoop, calls=%fused_computation.18 | loop fusion | flops 4194304 | bytes 16777280 | tf_op jit(solution)/shard_map/jit(_where)/select_n | solution.py:315
  54.0 3.6 all-to-all-done
  57.5 55.4 %all_to_all.80 = bf16[32,2,128,256]{3,2,1,0:T(8,128)(2,1)} all-to-all(bf16[32,2,128,256]{3,2,1,0:T(8,128)(2,1)} %get-tuple-element.76), channel_id=1, replica_groups=mesh['blk'=32,'head'=4] {'blk'}, dimensions={0} | all-to-all | bytes 8388608 | tf_op jit(solution)/shard_map/all_to_all | solution.py:314
  112.9 6.0 %all-to-all-start.2 = ((bf16[32,2,128,256]{3,2,1,0:T(8,128)(2,1)}), bf16[32,2,128,256]{3,2,1,0:T(8,128)(2,1)}, u32[]{:S(2)}, u32[]{:S(2)}) async-start(bf16[32,2,128,256]{3,2,1,0:T(8,128)(2,1)} %get-tuple-element.77), calls=%async_computation.2 | async-start | bytes 8388608 | tf_op jit(solution)/shard_map/all_to_all | solution.py:307
  122.6 2.0 copy.134
  125.8 47.3 %collective-permute-done = bf16[4,2,128,256]{3,2,0,1:T(8,128)(2,1)} collective-permute-done((bf16[4,2,128,256]{3,2,0,1:T(8,128)(2,1)}, bf16[4,2,128,256]{3,2,0,1:T(8,128)(2,1)}, u32[]{:S(2)}, u32[]{:S(2)}) %collective-permute-start) | collective-permute-done | bytes 524320 | tf_op jit(solution)/shard_map/ppermute | solution.py:28
  174.8 2.8 pad_maximum_fusion.2
  177.6 5.0 %pad_maximum_fusion.1 = bf16[80,128,256]{2,1,0:T(8,128)(2,1)} fusion(bf16[64,128,256]{2,1,0:T(8,128)(2,1)} %bitcast.22, bf16[16,128,256]{2,1,0:T(8,128)(2,1)S(1)} %get-tuple-element.63), kind=kLoop, calls=%fused_computation.7 | loop fusion | flops 2621440 | bytes 10485760 | tf_op jit(solution)/shard_map/concatenate | solution.py:324
  182.6 78.0 %shard_map.120 = (bf16[1024,256]{1,0:T(8,128)(2,1)S(1)}, bf16[1024,256]{1,0:T(8,128)(2,1)S(1)}, f32[16,256,128]{2,1,0:T(8,128)S(1)}, f32[16,256,128]{2,1,0:T(8,1...) custom-call(s32[128]{0:T(128)S(1)} %reshape.205.rows_ref, s32[8]{0:T(128)S(1)} %copy-done.4, ...), custom_call_target="tpu_custom_call" | custom-call | flops 12884901888 | bytes 33554432 | tf_op jit(solution)/shard_map/pallas_call | solution.py:232
  260.6 58.4 %all_to_all.81 = bf16[32,2,256,128]{3,2,1,0:T(8,128)(2,1)} all-to-all(bf16[32,2,256,128]{3,2,1,0:T(8,128)(2,1)} %bitcast.144), channel_id=1, replica_groups=mesh['blk'=32,'head'=4] {'blk'}, dimensions={0} | all-to-all | bytes 8388608 | tf_op jit(solution)/shard_map/all_to_all | solution.py:357
  319.1 6.1 %all-to-all-start.6 = ((bf16[32,2,256,128]{3,2,1,0:T(8,128)(2,1)}), bf16[32,2,256,128]{3,2,1,0:T(8,128)(2,1)}, u32[]{:S(2)}, u32[]{:S(2)}) async-start(bf16[32,2,256,128]{3,2,1,0:T(8,128)(2,1)} %bitcast.142), calls=%async_computation.6 | async-start | bytes 8388608 | tf_op jit(solution)/shard_map/all_to_all | solution.py:358
  325.2 2.1 fusion
  328.6 1.7 collective-permute-start.3
  330.4 2.1 copy.147
  334.0 45.3 %collective-permute-done.2 = bf16[4,2,256,128]{3,2,0,1:T(8,128)(2,1)} collective-permute-done((bf16[4,2,256,128]{3,2,0,1:T(8,128)(2,1)}, bf16[4,2,256,128]{3,2,0,1:T(8,128)(2,1)}, u32[]{:S(2)}, u32[]{:S(2)}) %collective-permute-start.2) | collective-permute-done | bytes 524320 | tf_op jit(solution)/shard_map/ppermute | solution.py:39
  379.3 2.2 fusion.10
  381.5 2.3 fusion.15
  383.9 2.3 fusion.4
  386.2 3.5 all-to-all-start.4
  389.7 4.5 %fusion.1 = f32[8,256,128]{2,0,1:T(8,128)S(1)} fusion(s32[64]{0:T(128)S(1)} %eq.52, bf16[8,8,256,128]{3,2,1,0:T(8,128)(2,1)} %bitcast.68), kind=kOutput, calls=%fused_computation.12 | convolution fusion | flops 33554944 | bytes 5243136 | tf_op jit(solution)/shard_map/dot_general | solution.py:368
  394.2 2.0 fusion.17
  396.8 2.1 copy.157
  398.9 6.3 %all-to-all-done.4 = bf16[2,1024,256]{2,0,1:T(2,128)(2,1)S(1)} async-done(((bf16[2,1024,256]{2,0,1:T(2,128)(2,1)}), bf16[2,1024,256]{2,0,1:T(2,128)(2,1)S(1)}, u32[]{:S(2)}, u32[]{:S(2)}) %all-to-all-start.4) | async-done | bytes 1048608 | tf_op jit(solution)/shard_map/all_to_all | solution.py:385
  405.2 3.7 all-to-all-start.7
  413.6 9.7 %all-to-all-done.7 = bf16[2,1024,256]{2,0,1:T(2,128)(2,1)S(1)} async-done(((bf16[2,1024,256]{2,0,1:T(2,128)(2,1)}), bf16[2,1024,256]{2,0,1:T(2,128)(2,1)S(1)}, u32[]{:S(2)}, u32[]{:S(2)}) %all-to-all-start.7) | async-done | bytes 1048608 | tf_op jit(solution)/shard_map/all_to_all | solution.py:385
  (95 shorter events, 20.5 us)
Async XLA Ops:
  0.6 7.8 %copy-start.4 = (s32[8]{0:T(128)S(1)}, s32[8]{0:T(128)}, u32[]{:S(2)}) copy-start(s32[8]{0:T(128)} %count_ref.1) | copy-start | bytes 100
  0.6 7.8 %copy-start.13 = (s32[8,4]{0,1:T(4,128)S(1)}, s32[8,4]{0,1:T(4,128)}, u32[]{:S(2)}) copy-start(s32[8,4]{0,1:T(4,128)} %param.18) | copy-start | bytes 388
  0.7 7.9 %copy-start.12 = (s32[8,4]{0,1:T(4,128)S(1)}, s32[8,4]{0,1:T(4,128)}, u32[]{:S(2)}) copy-start(s32[8,4]{0,1:T(4,128)} %param.17) | copy-start | bytes 388
  0.7 34.3 %copy-start.8 = (bf16[256,1024]{1,0:T(8,128)(2,1)S(1)}, bf16[256,1024]{1,0:T(8,128)(2,1)}, u32[]{:S(2)}) copy-start(bf16[256,1024]{1,0:T(8,128)(2,1)} %param.16) | copy-start | bytes 1572868
  0.7 34.3 %copy-start.9 = (bf16[256,1024]{1,0:T(8,128)(2,1)S(1)}, bf16[256,1024]{1,0:T(8,128)(2,1)}, u32[]{:S(2)}) copy-start(bf16[256,1024]{1,0:T(8,128)(2,1)} %param.13) | copy-start | bytes 1572868
  4.1 33.0 %all-to-all-start.1 = ((bf16[2,256,1024]{1,0,2:T(2,128)(2,1)}), bf16[2,256,1024]{1,0,2:T(2,128)(2,1)S(1)}, u32[]{:S(2)}, u32[]{:S(2)}) async-start(bf16[2,256,1024]{1,0,2:T(2,128)(2,1)} %copy.135), calls=%async_computation.1 | async-start | bytes 2097152 | tf_op jit(solution)/shard_map/all_to_all | solution.py:270
  37.1 20.4 %all-to-all-start = ((bf16[2,256,1024]{1,0,2:T(2,128)(2,1)}), bf16[2,256,1024]{1,0,2:T(2,128)(2,1)S(1)}, u32[]{:S(2)}, u32[]{:S(2)}) async-start(bf16[2,256,1024]{1,0,2:T(2,128)(2,1)} %copy.133), calls=%async_computation | async-start | bytes 2097152 | tf_op jit(solution)/shard_map/all_to_all | solution.py:270
  112.9 9.3 %copy-start.11 = (s32[8,11]{1,0:T(8,128)S(1)}, s32[8,11]{1,0:T(8,128)}, u32[]{:S(2)}) copy-start(s32[8,11]{1,0:T(8,128)} %param.19) | copy-start | bytes 1060
  112.9 9.4 %copy-start.10 = (s32[4,8,16]{2,1,0:T(8,128)S(1)}, s32[4,8,16]{2,1,0:T(8,128)}, u32[]{:S(2)}) copy-start(s32[4,8,16]{2,1,0:T(8,128)} %param.21) | copy-start | bytes 6148
  112.9 64.7 %all-to-all-start.2 = ((bf16[32,2,128,256]{3,2,1,0:T(8,128)(2,1)}), bf16[32,2,128,256]{3,2,1,0:T(8,128)(2,1)}, u32[]{:S(2)}, u32[]{:S(2)}) async-start(bf16[32,2,128,256]{3,2,1,0:T(8,128)(2,1)} %get-tuple-element.77), calls=%async_computation.2 | async-start | bytes 8388608 | tf_op jit(solution)/shard_map/all_to_all | solution.py:307
  120.5 52.6 %collective-permute-start = (bf16[4,2,128,256]{3,2,0,1:T(8,128)(2,1)}, bf16[4,2,128,256]{3,2,0,1:T(8,128)(2,1)}, u32[]{:S(2)}, u32[]{:S(2)}) collective-permute-start(bf16[4,2,128,256]{3,2,0,1:T(8,128)(2,1)} %get-tuple-element.68), channel_id=1, source_target_pairs={{0,4},{4,8},{8,12},{12,16},{16,20},{20,24},{24,28},{28,32},{32,36}... | collective-permute-start | bytes 1572872 | tf_op jit(solution)/shard_map/ppermute | solution.py:28
  120.6 52.5 %collective-permute-start.1 = (bf16[4,2,128,256]{3,2,0,1:T(8,128)(2,1)}, bf16[4,2,128,256]{3,2,0,1:T(8,128)(2,1)}, u32[]{:S(2)}, u32[]{:S(2)}) collective-permute-start(bf16[4,2,128,256]{3,2,0,1:T(8,128)(2,1)} %get-tuple-element.69), channel_id=1, source_target_pairs={{4,0},{8,4},{12,8},{16,12},{20,16},{24,20},{28,24},{32,28},{36,32}... | collective-permute-start | bytes 1572872 | tf_op jit(solution)/shard_map/ppermute | solution.py:31
  125.8 49.0 %copy-start.6 = (bf16[32,2,128,256]{3,2,1,0:T(8,128)(2,1)S(1)}, bf16[32,2,128,256]{3,2,1,0:T(8,128)(2,1)}, u32[]{:S(2)}) copy-start(bf16[32,2,128,256]{3,2,1,0:T(8,128)(2,1)} %all_to_all.80) | copy-start | bytes 12582916
  260.6 58.4 %copy-start = (bf16[1024,256]{1,0:T(8,128)(2,1)}, bf16[1024,256]{1,0:T(8,128)(2,1)S(1)}, u32[]{:S(2)}) copy-start(bf16[1024,256]{1,0:T(8,128)(2,1)S(1)} %get-tuple-element.34) | copy-start | bytes 1572868
  260.6 58.4 %copy-start.2 = (bf16[1024,256]{1,0:T(8,128)(2,1)}, bf16[1024,256]{1,0:T(8,128)(2,1)S(1)}, u32[]{:S(2)}) copy-start(bf16[1024,256]{1,0:T(8,128)(2,1)S(1)} %get-tuple-element.35) | copy-start | bytes 1572868
  319.1 67.1 %all-to-all-start.6 = ((bf16[32,2,256,128]{3,2,1,0:T(8,128)(2,1)}), bf16[32,2,256,128]{3,2,1,0:T(8,128)(2,1)}, u32[]{:S(2)}, u32[]{:S(2)}) async-start(bf16[32,2,256,128]{3,2,1,0:T(8,128)(2,1)} %bitcast.142), calls=%async_computation.6 | async-start | bytes 8388608 | tf_op jit(solution)/shard_map/all_to_all | solution.py:358
  325.1 5.2 %copy-start.1 = (bf16[1024,256]{1,0:T(8,128)(2,1)S(1)}, bf16[1024,256]{1,0:T(8,128)(2,1)}, u32[]{:S(2)}) copy-start(bf16[1024,256]{1,0:T(8,128)(2,1)} %copy-done) | copy-start | bytes 1572868
  325.2 5.1 %copy-start.3 = (bf16[1024,256]{1,0:T(8,128)(2,1)S(1)}, bf16[1024,256]{1,0:T(8,128)(2,1)}, u32[]{:S(2)}) copy-start(bf16[1024,256]{1,0:T(8,128)(2,1)} %copy-done.2) | copy-start | bytes 1572868
  328.3 51.1 %collective-permute-start.2 = (bf16[4,2,256,128]{3,2,0,1:T(8,128)(2,1)}, bf16[4,2,256,128]{3,2,0,1:T(8,128)(2,1)}, u32[]{:S(2)}, u32[]{:S(2)}) collective-permute-start(bf16[4,2,256,128]{3,2,0,1:T(8,128)(2,1)} %get-tuple-element.61), channel_id=1, source_target_pairs={{124,0},{0,4},{4,8},{8,12},{12,16},{16,20},{20,24},{24,28},{28,32}... | collective-permute-start | bytes 1572872 | tf_op jit(solution)/shard_map/ppermute | solution.py:39
  328.6 3.9 copy-start.5
  328.6 52.9 %collective-permute-start.3 = (bf16[4,2,256,128]{3,2,0,1:T(8,128)(2,1)}, bf16[4,2,256,128]{3,2,0,1:T(8,128)(2,1)S(1)}, u32[]{:S(2)}, u32[]{:S(2)}) collective-permute-start(bf16[4,2,256,128]{3,2,0,1:T(8,128)(2,1)} %get-tuple-element.60), channel_id=1, source_target_pairs={{4,0},{8,4},{12,8},{16,12},{20,16},{24,20},{28,24},{32,28},{36,32}... | collective-permute-start | bytes 1572872 | tf_op jit(solution)/shard_map/ppermute | solution.py:39
  334.0 49.9 %copy-start.7 = (bf16[32,2,256,128]{3,2,1,0:T(8,128)(2,1)S(1)}, bf16[32,2,256,128]{3,2,1,0:T(8,128)(2,1)}, u32[]{:S(2)}) copy-start(bf16[32,2,256,128]{3,2,1,0:T(8,128)(2,1)} %all_to_all.81) | copy-start | bytes 12582916
  386.2 19.0 %all-to-all-start.4 = ((bf16[2,1024,256]{2,0,1:T(2,128)(2,1)}), bf16[2,1024,256]{2,0,1:T(2,128)(2,1)S(1)}, u32[]{:S(2)}, u32[]{:S(2)}) async-start(bf16[2,1024,256]{2,0,1:T(2,128)(2,1)} %copy.147), calls=%async_computation.4 | async-start | bytes 2097152 | tf_op jit(solution)/shard_map/all_to_all | solution.py:385
  405.2 18.2 %all-to-all-start.7 = ((bf16[2,1024,256]{2,0,1:T(2,128)(2,1)}), bf16[2,1024,256]{2,0,1:T(2,128)(2,1)S(1)}, u32[]{:S(2)}, u32[]{:S(2)}) async-start(bf16[2,1024,256]{2,0,1:T(2,128)(2,1)} %copy.157), calls=%async_computation.7 | async-start | bytes 2097152 | tf_op jit(solution)/shard_map/all_to_all | solution.py:385

commit v9 on v8

--- a/solution.py
+++ b/solution.py
@@ -269,8 +269,9 @@
     def to_columns(arrays):
         return lax.all_to_all(jnp.stack(arrays), "head", split_axis=2, concat_axis=1, tiled=True)
 
-    key_local, value_local = to_columns([key_rows, value_rows])
-    query_local, grad_local = to_columns([query_rows, out_grad])
+    key_local, value_local, query_local, grad_local = to_columns(
+        [key_rows, value_rows, query_rows, out_grad]
+    )
     peer_count = lax.axis_size("blk")
     capacity = min(QB_DEV, max(2, (2 * QB_DEV * E + peer_count - 1) // peer_count))
     flat_device = expander_device.reshape(-1)

time: 427 us -> 425 us (level)
  starting transfers between devices: 32 us -> 27.1 us
    all_to_all x2 -> x1, starting transfers between devices: 9.1 us -> 4.29 us  [to_columns(): lax.all_to_all(jnp.stack(arrays), 'head', split_axis=2, concat_axis=1, ti...]
  transfers between devices with their start and end apart: 10 -> 9, of which waited for: 5 -> 4; matrix products, arithmetic and copies ran while one was open for 12% -> 8% of each run, Pallas kernels for 0% -> 0%
where the time goes in v9:
time: 425 us; the launch traced here: 423 us
  blocking collectives  142 us (33%)
  waiting for transfers between devices  112 us (26%)
  Pallas kernels  78 us (18%)
  local copies, waits for them, and re-layouts  28.6 us (7%)
  other arithmetic  27.6 us (6%)
  starting transfers between devices  27.1 us (6%)
  matrix products  6.83 us (2%)
    pallas_call x1, Pallas kernels, block_attention(): pl.pallas_call(kernel, grid_spec=grid_spec, out_shape=[jax.ShapeDtypeStru...  78 us
    all_to_all x1, blocking collectives, on_device(): lax.all_to_all(fk.reshape(column_shape), 'blk', split_axis=0, concat_axis...  58.4 us
    all_to_all x1, blocking collectives, on_device(): lax.all_to_all(jnp.where(asked_mask, value_blocks[chosen], zero_block).re...  57.9 us
    ppermute x1, waiting for transfers between devices, padded(): lax.ppermute(lax.slice_in_dim(block, block.shape[dim] - width, None, axis...  51.4 us
    ppermute x2, waiting for transfers between devices, shifted(): return lax.ppermute(block, axis, route)  45.9 us
    all_gather x1, blocking collectives, on_device(): lax.all_gather(jnp.stack([flat_device, asked_block.reshape(-1)]), 'blk',...  25.5 us
    all_to_all x2, waiting for transfers between devices, to_rows(): lax.all_to_all(jnp.stack(arrays), 'head', split_axis=1, concat_axis=2, ti...  15.1 us
  transfers between devices with their start and end apart: 9, of which 4 were waited for; matrix products, arithmetic and copies ran while one was open for 8% of the time, Pallas kernels for 0%

profile of v9, /device:TPU:8, one launch (start us, length us, event | category | flops | bytes accessed | tf_op | source)
XLA Modules:
  0.0 423.2 jit_solution(15486919137560377281)
XLA Ops:
  0.6 1.8 pad_maximum_fusion.3
  2.5 2.6 copy.95
  5.1 4.3 %all-to-all-start = ((bf16[4,256,1024]{1,0,2:T(4,128)(2,1)}), bf16[4,256,1024]{1,0,2:T(4,128)(2,1)S(1)}, u32[]{:S(2)}, u32[]{:S(2)}) async-start(bf16[4,256,1024]{1,0,2:T(4,128)(2,1)} %copy.95), calls=%async_computation | async-start | bytes 4194304 | tf_op jit(solution)/shard_map/all_to_all | solution.py:270
  9.7 25.5 %all-gather.1 = s32[32,2,32]{2,1,0:T(2,128)S(1)} all-gather(s32[1,2,32]{2,1,0:T(2,128)S(1)} %add_bitcast_fusion), channel_id=2, replica_groups=mesh['blk'=32,'head'=4] {'blk'}, dimensions={0}, use_global_device_ids=true | all-gather | bytes 8448 | tf_op jit(solution)/shard_map/all_gather | solution.py:286
  35.9 2.6 copy.96
  38.5 2.6 fusion.30
  41.1 2.9 gather_fusion
  44.1 2.7 gather_fusion.1
  46.8 5.2 %broadcast_select_fusion = (bf16[32,2,128,256]{3,2,1,0:T(8,128)(2,1)S(1)}, bf16[32,2,128,256]{3,2,1,0:T(8,128)(2,1)}) fusion(bf16[32,2,128,256]{3,2,1,0:T(8,128)(2,1)} %bitcast.134, pred[32,2]{1,0:T(8,128)(4,1)S(1)} %copy.101, bf16[32,2,128,256]{3,2,1,0:T(8,128)(2,1)} %bitcast.133), kind=kLoop, calls=%fused_computation.18 | loop fusion | flops 4194304 | bytes 16777280 | tf_op jit(solution)/shard_map/jit(_where)/select_n | solution.py:316
  52.0 57.9 %all_to_all.65 = bf16[32,2,128,256]{3,2,1,0:T(8,128)(2,1)} all-to-all(bf16[32,2,128,256]{3,2,1,0:T(8,128)(2,1)S(1)} %get-tuple-element.72), channel_id=1, replica_groups=mesh['blk'=32,'head'=4] {'blk'}, dimensions={0} | all-to-all | bytes 8388608 | tf_op jit(solution)/shard_map/all_to_all | solution.py:315
  109.9 6.0 %all-to-all-start.1 = ((bf16[32,2,128,256]{3,2,1,0:T(8,128)(2,1)}), bf16[32,2,128,256]{3,2,1,0:T(8,128)(2,1)}, u32[]{:S(2)}, u32[]{:S(2)}) async-start(bf16[32,2,128,256]{3,2,1,0:T(8,128)(2,1)} %get-tuple-element.73), calls=%async_computation.1 | async-start | bytes 8388608 | tf_op jit(solution)/shard_map/all_to_all | solution.py:308
  116.9 1.6 collective-permute-start.1
  118.7 51.4 %collective-permute-done = bf16[4,2,128,256]{3,2,0,1:T(8,128)(2,1)S(1)} collective-permute-done((bf16[4,2,128,256]{3,2,0,1:T(8,128)(2,1)S(1)}, bf16[4,2,128,256]{3,2,0,1:T(8,128)(2,1)S(1)}, u32[]{:S(2)}, u32[]{:S(2)}) %collective-permute-start) | collective-permute-done | bytes 524320 | tf_op jit(solution)/shard_map/ppermute | solution.py:28
  172.5 2.8 pad_maximum_fusion.2
  175.3 5.1 %pad_maximum_fusion.1 = bf16[80,128,256]{2,1,0:T(8,128)(2,1)} fusion(bf16[64,128,256]{2,1,0:T(8,128)(2,1)} %bitcast.19, bf16[16,128,256]{2,1,0:T(8,128)(2,1)S(1)} %get-tuple-element.59), kind=kLoop, calls=%fused_computation.7 | loop fusion | flops 2621440 | bytes 10485760 | tf_op jit(solution)/shard_map/concatenate | solution.py:325
  180.4 78.0 %shard_map.120 = (bf16[1024,256]{1,0:T(8,128)(2,1)S(1)}, bf16[1024,256]{1,0:T(8,128)(2,1)S(1)}, f32[16,256,128]{2,1,0:T(8,128)S(1)}, f32[16,256,128]{2,1,0:T(8,1...) custom-call(s32[128]{0:T(128)S(1)} %reshape.205.rows_ref, s32[8]{0:T(128)S(1)} %copy-done.2, ...), custom_call_target="tpu_custom_call" | custom-call | flops 12884901888 | bytes 33554432 | tf_op jit(solution)/shard_map/pallas_call | solution.py:232
  258.4 58.4 %all_to_all.66 = bf16[32,2,256,128]{3,2,1,0:T(8,128)(2,1)} all-to-all(bf16[32,2,256,128]{3,2,1,0:T(8,128)(2,1)} %bitcast.143), channel_id=1, replica_groups=mesh['blk'=32,'head'=4] {'blk'}, dimensions={0} | all-to-all | bytes 8388608 | tf_op jit(solution)/shard_map/all_to_all | solution.py:358
  316.8 5.9 %all-to-all-start.5 = ((bf16[32,2,256,128]{3,2,1,0:T(8,128)(2,1)}), bf16[32,2,256,128]{3,2,1,0:T(8,128)(2,1)}, u32[]{:S(2)}, u32[]{:S(2)}) async-start(bf16[32,2,256,128]{3,2,1,0:T(8,128)(2,1)} %bitcast.141), calls=%async_computation.5 | async-start | bytes 8388608 | tf_op jit(solution)/shard_map/all_to_all | solution.py:359
  322.8 2.0 fusion
  326.1 1.7 collective-permute-start.3
  327.9 2.1 copy.103
  331.6 45.9 %collective-permute-done.2 = bf16[4,2,256,128]{3,2,0,1:T(8,128)(2,1)} collective-permute-done((bf16[4,2,256,128]{3,2,0,1:T(8,128)(2,1)}, bf16[4,2,256,128]{3,2,0,1:T(8,128)(2,1)}, u32[]{:S(2)}, u32[]{:S(2)}) %collective-permute-start.2) | collective-permute-done | bytes 524320 | tf_op jit(solution)/shard_map/ppermute | solution.py:39
  377.5 2.2 fusion.10
  379.7 2.3 fusion.15
  382.0 2.3 fusion.4
  384.3 3.5 all-to-all-start.3
  387.8 4.5 %fusion.1 = f32[8,256,128]{2,0,1:T(8,128)S(1)} fusion(s32[64]{0:T(128)S(1)} %eq.52, bf16[8,8,256,128]{3,2,1,0:T(8,128)(2,1)} %bitcast.65), kind=kOutput, calls=%fused_computation.12 | convolution fusion | flops 33554944 | bytes 5243136 | tf_op jit(solution)/shard_map/dot_general | solution.py:369
  392.4 2.0 fusion.17
  395.0 2.1 copy.113
  397.0 5.8 %all-to-all-done.3 = bf16[2,1024,256]{2,0,1:T(2,128)(2,1)S(1)} async-done(((bf16[2,1024,256]{2,0,1:T(2,128)(2,1)}), bf16[2,1024,256]{2,0,1:T(2,128)(2,1)S(1)}, u32[]{:S(2)}, u32[]{:S(2)}) %all-to-all-start.3) | async-done | bytes 1048608 | tf_op jit(solution)/shard_map/all_to_all | solution.py:386
  402.8 3.7 all-to-all-start.6
  411.3 9.3 %all-to-all-done.6 = bf16[2,1024,256]{2,0,1:T(2,128)(2,1)S(1)} async-done(((bf16[2,1024,256]{2,0,1:T(2,128)(2,1)}), bf16[2,1024,256]{2,0,1:T(2,128)(2,1)S(1)}, u32[]{:S(2)}, u32[]{:S(2)}) %all-to-all-start.6) | async-done | bytes 1048608 | tf_op jit(solution)/shard_map/all_to_all | solution.py:386
  (81 shorter events, 15.4 us)
Async XLA Ops:
  2.4 7.0 %copy-start.2 = (s32[8]{0:T(128)S(1)}, s32[8]{0:T(128)}, u32[]{:S(2)}) copy-start(s32[8]{0:T(128)} %count_ref.1) | copy-start | bytes 100
  2.4 7.0 %copy-start.10 = (s32[8,4]{0,1:T(4,128)S(1)}, s32[8,4]{0,1:T(4,128)}, u32[]{:S(2)}) copy-start(s32[8,4]{0,1:T(4,128)} %param.18) | copy-start | bytes 388
  2.4 7.1 %copy-start.9 = (s32[8,4]{0,1:T(4,128)S(1)}, s32[8,4]{0,1:T(4,128)}, u32[]{:S(2)}) copy-start(s32[8,4]{0,1:T(4,128)} %param.17) | copy-start | bytes 388
  5.1 30.8 %all-to-all-start = ((bf16[4,256,1024]{1,0,2:T(4,128)(2,1)}), bf16[4,256,1024]{1,0,2:T(4,128)(2,1)S(1)}, u32[]{:S(2)}, u32[]{:S(2)}) async-start(bf16[4,256,1024]{1,0,2:T(4,128)(2,1)} %copy.95), calls=%async_computation | async-start | bytes 4194304 | tf_op jit(solution)/shard_map/all_to_all | solution.py:270
  109.9 6.1 %copy-start.7 = (s32[4,8,16]{2,1,0:T(8,128)S(1)}, s32[4,8,16]{2,1,0:T(8,128)}, u32[]{:S(2)}) copy-start(s32[4,8,16]{2,1,0:T(8,128)} %param.21) | copy-start | bytes 6148
  109.9 8.5 %copy-start.8 = (s32[8,11]{1,0:T(8,128)S(1)}, s32[8,11]{1,0:T(8,128)}, u32[]{:S(2)}) copy-start(s32[8,11]{1,0:T(8,128)} %param.19) | copy-start | bytes 1060
  109.9 65.3 %all-to-all-start.1 = ((bf16[32,2,128,256]{3,2,1,0:T(8,128)(2,1)}), bf16[32,2,128,256]{3,2,1,0:T(8,128)(2,1)}, u32[]{:S(2)}, u32[]{:S(2)}) async-start(bf16[32,2,128,256]{3,2,1,0:T(8,128)(2,1)} %get-tuple-element.73), calls=%async_computation.1 | async-start | bytes 8388608 | tf_op jit(solution)/shard_map/all_to_all | solution.py:308
  116.7 53.4 %collective-permute-start = (bf16[4,2,128,256]{3,2,0,1:T(8,128)(2,1)S(1)}, bf16[4,2,128,256]{3,2,0,1:T(8,128)(2,1)S(1)}, u32[]{:S(2)}, u32[]{:S(2)}) collective-permute-start(bf16[4,2,128,256]{3,2,0,1:T(8,128)(2,1)S(1)} %get-tuple-element.68), channel_id=1, source_target_pairs={{0,4},{4,8},{8,12},{12,16},{16,20},{20,24},{24,28},{28,32},{32,36}... | collective-permute-start | bytes 1572872 | tf_op jit(solution)/shard_map/ppermute | solution.py:28
  116.9 54.0 %collective-permute-start.1 = (bf16[4,2,128,256]{3,2,0,1:T(8,128)(2,1)S(1)}, bf16[4,2,128,256]{3,2,0,1:T(8,128)(2,1)}, u32[]{:S(2)}, u32[]{:S(2)}) collective-permute-start(bf16[4,2,128,256]{3,2,0,1:T(8,128)(2,1)S(1)} %get-tuple-element.69), channel_id=1, source_target_pairs={{4,0},{8,4},{12,8},{16,12},{20,16},{24,20},{28,24},{32,28},{36,32}... | collective-permute-start | bytes 1572872 | tf_op jit(solution)/shard_map/ppermute | solution.py:31
  118.7 53.8 %copy-start.4 = (bf16[32,2,128,256]{3,2,1,0:T(8,128)(2,1)S(1)}, bf16[32,2,128,256]{3,2,1,0:T(8,128)(2,1)}, u32[]{:S(2)}) copy-start(bf16[32,2,128,256]{3,2,1,0:T(8,128)(2,1)} %all_to_all.65) | copy-start | bytes 12582916
  170.1 0.8 copy-start.6
  175.3 5.1 %copy-start = (bf16[1,4,256,256]{3,2,1,0:T(8,128)(2,1)S(1)}, bf16[1,4,256,256]{3,2,1,0:T(8,128)(2,1)}, u32[]{:S(2)}) copy-start(bf16[1,4,256,256]{3,2,1,0:T(8,128)(2,1)} %get-tuple-element.62) | copy-start | bytes 1572868
  175.3 5.1 %copy-start.1 = (bf16[1,4,256,256]{3,2,1,0:T(8,128)(2,1)S(1)}, bf16[1,4,256,256]{3,2,1,0:T(8,128)(2,1)}, u32[]{:S(2)}) copy-start(bf16[1,4,256,256]{3,2,1,0:T(8,128)(2,1)} %get-tuple-element.63) | copy-start | bytes 1572868
  316.8 67.5 %all-to-all-start.5 = ((bf16[32,2,256,128]{3,2,1,0:T(8,128)(2,1)}), bf16[32,2,256,128]{3,2,1,0:T(8,128)(2,1)}, u32[]{:S(2)}, u32[]{:S(2)}) async-start(bf16[32,2,256,128]{3,2,1,0:T(8,128)(2,1)} %bitcast.141), calls=%async_computation.5 | async-start | bytes 8388608 | tf_op jit(solution)/shard_map/all_to_all | solution.py:359
  325.8 51.7 %collective-permute-start.2 = (bf16[4,2,256,128]{3,2,0,1:T(8,128)(2,1)}, bf16[4,2,256,128]{3,2,0,1:T(8,128)(2,1)}, u32[]{:S(2)}, u32[]{:S(2)}) collective-permute-start(bf16[4,2,256,128]{3,2,0,1:T(8,128)(2,1)} %get-tuple-element.57), channel_id=1, source_target_pairs={{124,0},{0,4},{4,8},{8,12},{12,16},{16,20},{20,24},{24,28},{28,32}... | collective-permute-start | bytes 1572872 | tf_op jit(solution)/shard_map/ppermute | solution.py:39
  326.1 3.9 copy-start.3
  326.1 53.6 %collective-permute-start.3 = (bf16[4,2,256,128]{3,2,0,1:T(8,128)(2,1)}, bf16[4,2,256,128]{3,2,0,1:T(8,128)(2,1)S(1)}, u32[]{:S(2)}, u32[]{:S(2)}) collective-permute-start(bf16[4,2,256,128]{3,2,0,1:T(8,128)(2,1)} %get-tuple-element.56), channel_id=1, source_target_pairs={{4,0},{8,4},{12,8},{16,12},{20,16},{24,20},{28,24},{32,28},{36,32}... | collective-permute-start | bytes 1572872 | tf_op jit(solution)/shard_map/ppermute | solution.py:39
  331.6 50.4 %copy-start.5 = (bf16[32,2,256,128]{3,2,1,0:T(8,128)(2,1)S(1)}, bf16[32,2,256,128]{3,2,1,0:T(8,128)(2,1)}, u32[]{:S(2)}) copy-start(bf16[32,2,256,128]{3,2,1,0:T(8,128)(2,1)} %all_to_all.66) | copy-start | bytes 12582916
  384.3 18.5 %all-to-all-start.3 = ((bf16[2,1024,256]{2,0,1:T(2,128)(2,1)}), bf16[2,1024,256]{2,0,1:T(2,128)(2,1)S(1)}, u32[]{:S(2)}, u32[]{:S(2)}) async-start(bf16[2,1024,256]{2,0,1:T(2,128)(2,1)} %copy.103), calls=%async_computation.3 | async-start | bytes 2097152 | tf_op jit(solution)/shard_map/all_to_all | solution.py:386
  402.8 17.7 %all-to-all-start.6 = ((bf16[2,1024,256]{2,0,1:T(2,128)(2,1)}), bf16[2,1024,256]{2,0,1:T(2,128)(2,1)S(1)}, u32[]{:S(2)}, u32[]{:S(2)}) async-start(bf16[2,1024,256]{2,0,1:T(2,128)(2,1)} %copy.113), calls=%async_computation.6 | async-start | bytes 2097152 | tf_op jit(solution)/shard_map/all_to_all | solution.py:386

commit v10 on v8

--- a/solution.py
+++ b/solution.py
@@ -270,7 +270,13 @@
         return lax.all_to_all(jnp.stack(arrays), "head", split_axis=2, concat_axis=1, tiled=True)
 
     key_local, value_local = to_columns([key_rows, value_rows])
-    query_local, grad_local = to_columns([query_rows, out_grad])
+    first_col = head_index * local_width
+    query_local, grad_local = [
+        lax.dynamic_slice_in_dim(
+            lax.all_gather(member, "head", axis=0, tiled=True), first_col, local_width, 1
+        )
+        for member in (query_rows, out_grad)
+    ]
     peer_count = lax.axis_size("blk")
     capacity = min(QB_DEV, max(2, (2 * QB_DEV * E + peer_count - 1) // peer_count))
     flat_device = expander_device.reshape(-1)
@@ -384,10 +390,16 @@
     def to_rows(arrays):
         return lax.all_to_all(jnp.stack(arrays), "head", split_axis=1, concat_axis=2, tiled=True)
 
-    attended, query_grad = to_rows([
-        outputs[0].reshape(block_rows, local_width),
-        outputs[1].reshape(block_rows, local_width),
-    ])
+    first_row = head_index * share_rows
+    attended, query_grad = [
+        lax.dynamic_slice_in_dim(
+            lax.all_gather(member.reshape(block_rows, local_width), "head", axis=1, tiled=True),
+            first_row,
+            share_rows,
+            0,
+        )
+        for member in outputs
+    ]
     key_grad, value_grad = to_rows([
         key_grad.reshape(block_rows, local_width),
         value_grad.reshape(block_rows, local_width),

time: 427 us -> 433 us (1.014)
  blocking collectives: 139 us -> 25.5 us
  waiting for transfers between devices: 112 us -> 212 us
  between operations: 0.96 us -> 14 us
  starting transfers between devices: 32 us -> 42 us
  local copies, waits for them, and re-layouts: 27.9 us -> 21.6 us
    all_to_all x2 -> x0, blocking collectives: 114 us -> none  [the longest x1 58.4 us: on_device(): lax.all_to_all(fk.reshape(column_shape), 'blk', split_axis=0, concat_axis...]
    all_to_all x0 -> x2, waiting for transfers between devices: none -> 101 us  [the longest x1 50.7 us: on_device(): lax.all_to_all(jnp.where(asked_mask, value_blocks[chosen], zero_block).re...]
    all_to_all x0 -> x2, starting transfers between devices: none -> 14.3 us  [the longest x1 8.68 us: on_device(): lax.all_to_all(fk.reshape(column_shape), 'blk', split_axis=0, concat_axis...]
    dynamic_slice x0 -> x4, local copies, waits for them, and re-layouts: none -> 5.9 us  [the longest x2 3.74 us: on_device(): lax.dynamic_slice_in_dim(lax.all_gather(member.reshape(block_rows, local_...]
    all_to_all x2 -> x1, starting transfers between devices: 9.1 us -> 4.29 us  [to_columns(): lax.all_to_all(jnp.stack(arrays), 'head', split_axis=2, concat_axis=1, ti...]
    all_to_all x2 -> x1, waiting for transfers between devices: 16.1 us -> 11.5 us  [to_rows(): lax.all_to_all(jnp.stack(arrays), 'head', split_axis=1, concat_axis=2, ti...]
  transfers between devices with their start and end apart: 10 -> 14, of which waited for: 5 -> 5; matrix products, arithmetic and copies ran while one was open for 12% -> 9% of each run, Pallas kernels for 0% -> 0%
where the time goes in v10:
time: 433 us; the launch traced here: 432 us
  waiting for transfers between devices  212 us (49%)
  Pallas kernels  77.9 us (18%)
  starting transfers between devices  42 us (10%)
  other arithmetic  29.9 us (7%)
  blocking collectives  25.5 us (6%)
  local copies, waits for them, and re-layouts  21.6 us (5%)
  between operations  14 us (3%)
  matrix products  9.01 us (2%)
    pallas_call x1, Pallas kernels, block_attention(): pl.pallas_call(kernel, grid_spec=grid_spec, out_shape=[jax.ShapeDtypeStru...  77.9 us
    all_to_all x1, waiting for transfers between devices, on_device(): lax.all_to_all(jnp.where(asked_mask, value_blocks[chosen], zero_block).re...  50.7 us
    all_to_all x1, waiting for transfers between devices, on_device(): lax.all_to_all(fk.reshape(column_shape), 'blk', split_axis=0, concat_axis...  50.7 us
    ppermute x1, waiting for transfers between devices, padded(): lax.ppermute(lax.slice_in_dim(block, block.shape[dim] - width, None, axis...  50.6 us
    ppermute x2, waiting for transfers between devices, shifted(): return lax.ppermute(block, axis, route)  45.8 us
    all_gather x1, blocking collectives, on_device(): lax.all_gather(jnp.stack([flat_device, asked_block.reshape(-1)]), 'blk',...  25.5 us
    all_to_all x1, waiting for transfers between devices, to_rows(): lax.all_to_all(jnp.stack(arrays), 'head', split_axis=1, concat_axis=2, ti...  11.5 us
    all_to_all x1, starting transfers between devices, on_device(): lax.all_to_all(fk.reshape(column_shape), 'blk', split_axis=0, concat_axis...  8.68 us
  transfers between devices with their start and end apart: 14, of which 5 were waited for; matrix products, arithmetic and copies ran while one was open for 9% of the time, Pallas kernels for 0%

profile of v10, /device:TPU:8, one launch (start us, length us, event | category | flops | bytes accessed | tf_op | source)
XLA Modules:
  0.0 431.7 jit_solution(14540582391889648099)
XLA Ops:
  7.2 1.3 pad_maximum_fusion.4
  8.5 2.1 copy.115
  10.6 4.3 all-to-all-start
  15.2 25.5 %all-gather.1 = s32[32,2,32]{2,1,0:T(2,128)S(1)} all-gather(s32[1,2,32]{2,1,0:T(2,128)S(1)} %add_bitcast_fusion), channel_id=2, replica_groups=mesh['blk'=32,'head'=4] {'blk'}, dimensions={0}, use_global_device_ids=true | all-gather | bytes 8448 | tf_op jit(solution)/shard_map/all_gather | solution.py:291
  42.0 2.8 gather_fusion
  44.8 2.9 gather_fusion.1
  47.7 5.9 %broadcast_select_fusion = (bf16[32,2,128,256]{3,2,1,0:T(8,128)(2,1)}, bf16[32,2,128,256]{3,2,1,0:T(8,128)(2,1)}) fusion(bf16[32,2,128,256]{3,2,1,0:T(8,128)(2,1)} %bitcast.116, pred[32,2]{1,0:T(8,128)(4,1)S(1)} %copy.123, bf16[32,2,128,256]{3,2,1,0:T(8,128)(2,1)} %bitcast.115), kind=kLoop, calls=%fused_computation.18 | loop fusion | flops 4194304 | bytes 16777280 | tf_op jit(solution)/shard_map/jit(_where)/select_n | solution.py:321
  53.6 5.6 %all-to-all-start.2 = ((bf16[32,2,128,256]{3,2,1,0:T(8,128)(2,1)}), bf16[32,2,128,256]{3,2,1,0:T(8,128)(2,1)}, u32[]{:S(2)}, u32[]{:S(2)}) async-start(bf16[32,2,128,256]{3,2,1,0:T(8,128)(2,1)} %get-tuple-element.72), calls=%async_computation.2 | async-start | bytes 8388608 | tf_op jit(solution)/shard_map/all_to_all | solution.py:320
  59.9 50.7 %all-to-all-done.2 = bf16[32,2,128,256]{3,2,1,0:T(8,128)(2,1)} async-done(((bf16[32,2,128,256]{3,2,1,0:T(8,128)(2,1)}), bf16[32,2,128,256]{3,2,1,0:T(8,128)(2,1)}, u32[]{:S(2)}, u32[]{:S(2)}) %all-to-all-start.2) | async-done | bytes 4194336 | tf_op jit(solution)/shard_map/all_to_all | solution.py:320
  110.6 7.4 %all-to-all-start.1 = ((bf16[32,2,128,256]{3,2,1,0:T(8,128)(2,1)}), bf16[32,2,128,256]{3,2,1,0:T(8,128)(2,1)}, u32[]{:S(2)}, u32[]{:S(2)}) async-start(bf16[32,2,128,256]{3,2,1,0:T(8,128)(2,1)} %get-tuple-element.73), calls=%async_computation.1 | async-start | bytes 8388608 | tf_op jit(solution)/shard_map/all_to_all | solution.py:313
  119.7 1.6 collective-permute-start.1
  121.6 50.6 %collective-permute-done = bf16[4,2,128,256]{3,2,0,1:T(8,128)(2,1)S(1)} collective-permute-done((bf16[4,2,128,256]{3,2,0,1:T(8,128)(2,1)S(1)}, bf16[4,2,128,256]{3,2,0,1:T(8,128)(2,1)S(1)}, u32[]{:S(2)}, u32[]{:S(2)}) %collective-permute-start) | collective-permute-done | bytes 524320 | tf_op jit(solution)/shard_map/ppermute | solution.py:28
  174.9 5.0 %pad_maximum_fusion.2 = bf16[80,128,256]{2,1,0:T(8,128)(2,1)} fusion(bf16[64,128,256]{2,1,0:T(8,128)(2,1)} %bitcast.21, bf16[16,128,256]{2,1,0:T(8,128)(2,1)S(1)} %get-tuple-element.62), kind=kLoop, calls=%fused_computation.8 | loop fusion | flops 2621440 | bytes 10485760 | tf_op jit(solution)/shard_map/concatenate | solution.py:333
  179.9 5.0 %pad_maximum_fusion.1 = bf16[80,128,256]{2,1,0:T(8,128)(2,1)} fusion(bf16[64,128,256]{2,1,0:T(8,128)(2,1)} %bitcast.16, bf16[16,128,256]{2,1,0:T(8,128)(2,1)S(1)} %get-tuple-element.63), kind=kLoop, calls=%fused_computation.7 | loop fusion | flops 2621440 | bytes 10485760 | tf_op jit(solution)/shard_map/concatenate | solution.py:330
  184.9 77.9 %shard_map.120 = (bf16[1024,256]{1,0:T(8,128)(2,1)}, bf16[1024,256]{1,0:T(8,128)(2,1)}, f32[16,256,128]{2,1,0:T(8,128)S(1)}, f32[16,256,128]{2,1,0:T(8,128)}, bf...) custom-call(s32[128]{0:T(128)S(1)} %reshape.197.rows_ref, s32[8]{0:T(128)S(1)} %copy-done, ...), custom_call_target="tpu_custom_call" | custom-call | flops 12884901888 | bytes 33554432 | tf_op jit(solution)/shard_map/pallas_call | solution.py:232
  262.7 8.7 %all-to-all-start.3 = ((bf16[32,2,256,128]{3,2,1,0:T(8,128)(2,1)}), bf16[32,2,256,128]{3,2,1,0:T(8,128)(2,1)}, u32[]{:S(2)}, u32[]{:S(2)}) async-start(bf16[32,2,256,128]{3,2,1,0:T(8,128)(2,1)} %bitcast.120), calls=%async_computation.3 | async-start | bytes 8388608 | tf_op jit(solution)/shard_map/all_to_all | solution.py:363
  272.2 50.7 %all-to-all-done.3 = bf16[32,2,256,128]{3,2,1,0:T(8,128)(2,1)} async-done(((bf16[32,2,256,128]{3,2,1,0:T(8,128)(2,1)}), bf16[32,2,256,128]{3,2,1,0:T(8,128)(2,1)}, u32[]{:S(2)}, u32[]{:S(2)}) %all-to-all-start.3) | async-done | bytes 4194336 | tf_op jit(solution)/shard_map/all_to_all | solution.py:363
  322.8 7.3 %all-to-all-start.4 = ((bf16[32,2,256,128]{3,2,1,0:T(8,128)(2,1)}), bf16[32,2,256,128]{3,2,1,0:T(8,128)(2,1)}, u32[]{:S(2)}, u32[]{:S(2)}) async-start(bf16[32,2,256,128]{3,2,1,0:T(8,128)(2,1)} %bitcast.119), calls=%async_computation.4 | async-start | bytes 8388608 | tf_op jit(solution)/shard_map/all_to_all | solution.py:364
  330.7 2.0 fusion
  333.7 1.6 collective-permute-start.3
  335.5 3.0 fusion.7
  338.5 45.8 %collective-permute-done.2 = bf16[4,2,256,128]{3,2,0,1:T(8,128)(2,1)} collective-permute-done((bf16[4,2,256,128]{3,2,0,1:T(8,128)(2,1)}, bf16[4,2,256,128]{3,2,0,1:T(8,128)(2,1)}, u32[]{:S(2)}, u32[]{:S(2)}) %collective-permute-start.2) | collective-permute-done | bytes 524320 | tf_op jit(solution)/shard_map/ppermute | solution.py:39
  384.3 2.1 fusion.10
  386.5 2.3 fusion.15
  388.8 4.5 %fusion.4 = f32[8,256,128]{2,0,1:T(8,128)S(1)} fusion(s32[64]{0:T(128)S(1)} %eq.52, bf16[8,8,256,128]{3,2,1,0:T(8,128)(2,1)} %bitcast.48), kind=kOutput, calls=%fused_computation.15 | convolution fusion | flops 33554944 | bytes 5243136 | tf_op jit(solution)/shard_map/dot_general | solution.py:369
  393.3 4.5 %fusion.1 = f32[8,256,128]{2,0,1:T(8,128)S(1)} fusion(s32[64]{0:T(128)S(1)} %eq.52, bf16[8,8,256,128]{3,2,1,0:T(8,128)(2,1)} %bitcast.51), kind=kOutput, calls=%fused_computation.12 | convolution fusion | flops 33554944 | bytes 5243136 | tf_op jit(solution)/shard_map/dot_general | solution.py:374
  397.8 2.0 fusion.17
  400.4 2.1 copy.134
  402.5 4.8 %all-to-all-start.5 = ((bf16[2,1024,256]{2,0,1:T(2,128)(2,1)}), bf16[2,1024,256]{2,0,1:T(2,128)(2,1)S(1)}, u32[]{:S(2)}, u32[]{:S(2)}) async-start(bf16[2,1024,256]{2,0,1:T(2,128)(2,1)} %copy.134), calls=%async_computation.5 | async-start | bytes 2097152 | tf_op jit(solution)/shard_map/all_to_all | solution.py:391
  407.3 1.9 constant_dynamic-slice_fusion.1
  409.2 1.9 constant_dynamic-slice_fusion
  411.0 11.5 %all-to-all-done.5 = bf16[2,1024,256]{2,0,1:T(2,128)(2,1)S(1)} async-done(((bf16[2,1024,256]{2,0,1:T(2,128)(2,1)}), bf16[2,1024,256]{2,0,1:T(2,128)(2,1)S(1)}, u32[]{:S(2)}, u32[]{:S(2)}) %all-to-all-start.5) | async-done | bytes 1048608 | tf_op jit(solution)/shard_map/all_to_all | solution.py:391
  (82 shorter events, 12.6 us)
Async XLA Ops:
  7.2 7.7 %copy-start = (s32[8]{0:T(128)S(1)}, s32[8]{0:T(128)}, u32[]{:S(2)}) copy-start(s32[8]{0:T(128)} %count_ref.1) | copy-start | bytes 100
  7.2 7.7 %copy-start.5 = (s32[8,4]{0,1:T(4,128)S(1)}, s32[8,4]{0,1:T(4,128)}, u32[]{:S(2)}) copy-start(s32[8,4]{0,1:T(4,128)} %param.18) | copy-start | bytes 388
  7.2 7.9 %copy-start.4 = (s32[8,4]{0,1:T(4,128)S(1)}, s32[8,4]{0,1:T(4,128)}, u32[]{:S(2)}) copy-start(s32[8,4]{0,1:T(4,128)} %param.17) | copy-start | bytes 388
  10.6 30.8 %all-to-all-start = ((bf16[2,256,1024]{1,0,2:T(2,128)(2,1)}), bf16[2,256,1024]{1,0,2:T(2,128)(2,1)S(1)}, u32[]{:S(2)}, u32[]{:S(2)}) async-start(bf16[2,256,1024]{1,0,2:T(2,128)(2,1)} %copy.115), calls=%async_computation | async-start | bytes 2097152 | tf_op jit(solution)/shard_map/all_to_all | solution.py:270
  53.6 57.1 %all-to-all-start.2 = ((bf16[32,2,128,256]{3,2,1,0:T(8,128)(2,1)}), bf16[32,2,128,256]{3,2,1,0:T(8,128)(2,1)}, u32[]{:S(2)}, u32[]{:S(2)}) async-start(bf16[32,2,128,256]{3,2,1,0:T(8,128)(2,1)} %get-tuple-element.72), calls=%async_computation.2 | async-start | bytes 8388608 | tf_op jit(solution)/shard_map/all_to_all | solution.py:320
  59.2 113.5 %all-gather.7.cloned.1.call-start = ((), (), s32[]{:S(2)}) async-start(), calls=%async_computation.6 | async-start | bytes 2621440 | tf_op jit(solution)/shard_map/all_gather | solution.py:276
  110.6 8.3 %copy-start.2 = (s32[4,8,16]{2,1,0:T(8,128)S(1)}, s32[4,8,16]{2,1,0:T(8,128)}, u32[]{:S(2)}) copy-start(s32[4,8,16]{2,1,0:T(8,128)} %param.21) | copy-start | bytes 6148
  110.6 10.7 %copy-start.3 = (s32[8,11]{1,0:T(8,128)S(1)}, s32[8,11]{1,0:T(8,128)}, u32[]{:S(2)}) copy-start(s32[8,11]{1,0:T(8,128)} %param.19) | copy-start | bytes 1060
  110.6 69.2 %all-to-all-start.1 = ((bf16[32,2,128,256]{3,2,1,0:T(8,128)(2,1)}), bf16[32,2,128,256]{3,2,1,0:T(8,128)(2,1)}, u32[]{:S(2)}, u32[]{:S(2)}) async-start(bf16[32,2,128,256]{3,2,1,0:T(8,128)(2,1)} %get-tuple-element.73), calls=%async_computation.1 | async-start | bytes 8388608 | tf_op jit(solution)/shard_map/all_to_all | solution.py:313
  118.1 55.7 %all-gather.9.cloned.1.call-start = ((), (), s32[]{:S(2)}) async-start(), calls=%async_computation.7 | async-start | bytes 2621440 | tf_op jit(solution)/shard_map/all_gather | solution.py:276
  119.5 52.7 %collective-permute-start = (bf16[4,2,128,256]{3,2,0,1:T(8,128)(2,1)S(1)}, bf16[4,2,128,256]{3,2,0,1:T(8,128)(2,1)S(1)}, u32[]{:S(2)}, u32[]{:S(2)}) collective-permute-start(bf16[4,2,128,256]{3,2,0,1:T(8,128)(2,1)S(1)} %get-tuple-element.66), channel_id=1, source_target_pairs={{0,4},{4,8},{8,12},{12,16},{16,20},{20,24},{24,28},{28,32},{32,36}... | collective-permute-start | bytes 1572872 | tf_op jit(solution)/shard_map/ppermute | solution.py:28
  119.7 52.5 %collective-permute-start.1 = (bf16[4,2,128,256]{3,2,0,1:T(8,128)(2,1)S(1)}, bf16[4,2,128,256]{3,2,0,1:T(8,128)(2,1)S(1)}, u32[]{:S(2)}, u32[]{:S(2)}) collective-permute-start(bf16[4,2,128,256]{3,2,0,1:T(8,128)(2,1)S(1)} %get-tuple-element.67), channel_id=1, source_target_pairs={{4,0},{8,4},{12,8},{16,12},{20,16},{24,20},{28,24},{32,28},{36,32}... | collective-permute-start | bytes 1572872 | tf_op jit(solution)/shard_map/ppermute | solution.py:31
  262.7 60.1 %all-to-all-start.3 = ((bf16[32,2,256,128]{3,2,1,0:T(8,128)(2,1)}), bf16[32,2,256,128]{3,2,1,0:T(8,128)(2,1)}, u32[]{:S(2)}, u32[]{:S(2)}) async-start(bf16[32,2,256,128]{3,2,1,0:T(8,128)(2,1)} %bitcast.120), calls=%async_computation.3 | async-start | bytes 8388608 | tf_op jit(solution)/shard_map/all_to_all | solution.py:363
  271.4 135.9 %all-gather.11.cloned.1.call-start = ((), (), s32[]{:S(2)}) async-start(), calls=%async_computation.8 | async-start | bytes 2621440 | tf_op jit(solution)/shard_map/all_gather | solution.py:396
  322.8 70.5 %all-to-all-start.4 = ((bf16[32,2,256,128]{3,2,1,0:T(8,128)(2,1)}), bf16[32,2,256,128]{3,2,1,0:T(8,128)(2,1)}, u32[]{:S(2)}, u32[]{:S(2)}) async-start(bf16[32,2,256,128]{3,2,1,0:T(8,128)(2,1)} %bitcast.119), calls=%async_computation.4 | async-start | bytes 8388608 | tf_op jit(solution)/shard_map/all_to_all | solution.py:364
  330.1 79.0 %all-gather.13.cloned.1.call-start = ((), (), s32[]{:S(2)}) async-start(), calls=%async_computation.9 | async-start | bytes 2621440 | tf_op jit(solution)/shard_map/all_gather | solution.py:396
  333.6 50.7 %collective-permute-start.2 = (bf16[4,2,256,128]{3,2,0,1:T(8,128)(2,1)}, bf16[4,2,256,128]{3,2,0,1:T(8,128)(2,1)}, u32[]{:S(2)}, u32[]{:S(2)}) collective-permute-start(bf16[4,2,256,128]{3,2,0,1:T(8,128)(2,1)} %get-tuple-element.61), channel_id=1, source_target_pairs={{124,0},{0,4},{4,8},{8,12},{12,16},{16,20},{20,24},{24,28},{28,32}... | collective-permute-start | bytes 1572872 | tf_op jit(solution)/shard_map/ppermute | solution.py:39
  333.7 52.8 %collective-permute-start.3 = (bf16[4,2,256,128]{3,2,0,1:T(8,128)(2,1)S(1)}, bf16[4,2,256,128]{3,2,0,1:T(8,128)(2,1)S(1)}, u32[]{:S(2)}, u32[]{:S(2)}) collective-permute-start(bf16[4,2,256,128]{3,2,0,1:T(8,128)(2,1)S(1)} %get-tuple-element.60), channel_id=1, source_target_pairs={{4,0},{8,4},{12,8},{16,12},{20,16},{24,20},{28,24},{32,28},{36,32}... | collective-permute-start | bytes 1572872 | tf_op jit(solution)/shard_map/ppermute | solution.py:39
  335.5 48.8 %copy-start.1 = (f32[16,256,128]{2,1,0:T(8,128)S(1)}, f32[16,256,128]{2,1,0:T(8,128)}, u32[]{:S(2)}) copy-start(f32[16,256,128]{2,1,0:T(8,128)} %get-tuple-element.37) | copy-start | bytes 6291460
  402.5 20.1 %all-to-all-start.5 = ((bf16[2,1024,256]{2,0,1:T(2,128)(2,1)}), bf16[2,1024,256]{2,0,1:T(2,128)(2,1)S(1)}, u32[]{:S(2)}, u32[]{:S(2)}) async-start(bf16[2,1024,256]{2,0,1:T(2,128)(2,1)} %copy.134), calls=%async_computation.5 | async-start | bytes 2097152 | tf_op jit(solution)/shard_map/all_to_all | solution.py:391
Sparse Core Ops, SparseCore 0:
  61.7 32.3 all-gather.6
  120.6 32.4 all-gather.8
  274.5 35.5 all-gather.10
  332.9 35.6 all-gather.12

commit v11 on v9

--- a/solution.py
+++ b/solution.py
@@ -303,17 +303,25 @@
     chosen = jnp.clip(wanted_flat, 0, QB_DEV - 1)
     asked_mask = (wanted_flat >= 0)[:, None, None]
     zero_block = jnp.zeros((), jnp.bfloat16)
+    selection = (
+        wanted_flat[:, None] == jnp.arange(QB_DEV, dtype=jnp.int32)[None, :]
+    ).astype(jnp.bfloat16)
+
+    def asked_of(blocks):
+        return jnp.dot(
+            selection, blocks.reshape(QB_DEV, -1), preferred_element_type=jnp.float32
+        ).astype(jnp.bfloat16)
     reply_shape = (peer_count, capacity, BS, local_width)
     far_key, far_value = (
         lax.all_to_all(
-            jnp.where(asked_mask, key_blocks[chosen], zero_block).reshape(reply_shape),
+            asked_of(key_blocks).reshape(reply_shape),
             "blk",
             split_axis=0,
             concat_axis=0,
             tiled=True,
         ),
         lax.all_to_all(
-            jnp.where(asked_mask, value_blocks[chosen], zero_block).reshape(reply_shape),
+            asked_of(value_blocks).reshape(reply_shape),
             "blk",
             split_axis=0,
             concat_axis=0,

time: 425 us -> 425 us (level)
  blocking collectives: 142 us -> 83.9 us
  waiting for transfers between devices: 112 us -> 162 us
  starting transfers between devices: 27.1 us -> 37.2 us
    all_to_all x1 -> x0, blocking collectives: 57.9 us -> none  [on_device(): lax.all_to_all(jnp.where(asked_mask, value_blocks[chosen], zero_block).re...]
    all_to_all x1 -> x2, waiting for transfers between devices: 0.01 us -> 46.8 us  [the longest x1 46.8 us: on_device(): lax.all_to_all(asked_of(key_blocks).reshape(reply_shape), 'blk', split_ax...]
    all_to_all x1 -> x2, starting transfers between devices: 6.04 us -> 16 us  [the longest x1 8.53 us: on_device(): lax.all_to_all(asked_of(key_blocks).reshape(reply_shape), 'blk', split_ax...]
    unnamed x27, local copies, waits for them, and re-layouts: 4.72 us -> 10.8 us
    gather x2 -> x0, local copies, waits for them, and re-layouts: 5.66 us -> none  [the longest x1 2.91 us: on_device(): key_blocks[chosen]]
    select_n x2 -> x0, other arithmetic: 5.22 us -> none  [the longest x1 5.21 us: on_device(): jnp.where(asked_mask, value_blocks[chosen], zero_block).reshape(reply_shape)]
  transfers between devices with their start and end apart: 9 -> 10, of which waited for: 4 -> 5; matrix products, arithmetic and copies ran while one was open for 8% -> 9% of each run, Pallas kernels for 0% -> 0%
where the time goes in v11:
time: 425 us; the launch traced here: 424 us
  waiting for transfers between devices  162 us (38%)
  blocking collectives  83.9 us (20%)
  Pallas kernels  78.1 us (18%)
  starting transfers between devices  37.2 us (9%)
  local copies, waits for them, and re-layouts  28.3 us (7%)
  other arithmetic  24 us (6%)
  matrix products  9.39 us (2%)
    pallas_call x1, Pallas kernels, block_attention(): pl.pallas_call(kernel, grid_spec=grid_spec, out_shape=[jax.ShapeDtypeStru...  78.1 us
    all_to_all x1, blocking collectives, on_device(): lax.all_to_all(fk.reshape(column_shape), 'blk', split_axis=0, concat_axis...  58.4 us
    ppermute x1, waiting for transfers between devices, padded(): lax.ppermute(lax.slice_in_dim(block, block.shape[dim] - width, None, axis...  51.3 us
    all_to_all x1, waiting for transfers between devices, on_device(): lax.all_to_all(asked_of(key_blocks).reshape(reply_shape), 'blk', split_ax...  46.8 us
    ppermute x2, waiting for transfers between devices, shifted(): return lax.ppermute(block, axis, route)  46.5 us
    all_gather x1, blocking collectives, on_device(): lax.all_gather(jnp.stack([flat_device, asked_block.reshape(-1)]), 'blk',...  25.5 us
    all_to_all x2, waiting for transfers between devices, to_rows(): lax.all_to_all(jnp.stack(arrays), 'head', split_axis=1, concat_axis=2, ti...  17.3 us
    unnamed x27, local copies, waits for them, and re-layouts  10.8 us
  transfers between devices with their start and end apart: 10, of which 5 were waited for; matrix products, arithmetic and copies ran while one was open for 9% of the time, Pallas kernels for 0%

profile of v11, /device:TPU:8, one launch (start us, length us, event | category | flops | bytes accessed | tf_op | source)
XLA Modules:
  0.0 423.7 jit_solution(315803065490150393)
XLA Ops:
  0.6 1.8 pad_maximum_fusion.3
  2.4 2.6 copy.87
  5.1 4.4 %all-to-all-start = ((bf16[4,256,1024]{1,0,2:T(4,128)(2,1)}), bf16[4,256,1024]{1,0,2:T(4,128)(2,1)S(1)}, u32[]{:S(2)}, u32[]{:S(2)}) async-start(bf16[4,256,1024]{1,0,2:T(4,128)(2,1)} %copy.87), calls=%async_computation | async-start | bytes 4194304 | tf_op jit(solution)/shard_map/all_to_all | solution.py:270
  9.8 25.5 %all-gather.1 = s32[32,2,32]{2,1,0:T(2,128)S(1)} all-gather(s32[1,2,32]{2,1,0:T(2,128)S(1)} %add_bitcast_fusion), channel_id=2, replica_groups=mesh['blk'=32,'head'=4] {'blk'}, dimensions={0}, use_global_device_ids=true | all-gather | bytes 8448 | tf_op jit(solution)/shard_map/all_gather | solution.py:286
  35.9 2.6 copy.88
  38.5 2.6 fusion.31
  42.7 3.0 copy.113
  45.7 8.5 %all-to-all-start.1 = ((bf16[32,2,128,256]{3,2,1,0:T(8,128)(2,1)}), bf16[32,2,128,256]{3,2,1,0:T(8,128)(2,1)}, u32[]{:S(2)}, u32[]{:S(2)}) async-start(bf16[32,2,128,256]{3,2,1,0:T(8,128)(2,1)} %bitcast.134), calls=%async_computation.1 | async-start | bytes 8388608 | tf_op jit(solution)/shard_map/all_to_all | solution.py:316
  55.8 3.1 copy.114
  58.8 46.8 %all-to-all-done.1 = bf16[32,2,128,256]{3,2,1,0:T(8,128)(2,1)} async-done(((bf16[32,2,128,256]{3,2,1,0:T(8,128)(2,1)}), bf16[32,2,128,256]{3,2,1,0:T(8,128)(2,1)}, u32[]{:S(2)}, u32[]{:S(2)}) %all-to-all-start.1) | async-done | bytes 4194336 | tf_op jit(solution)/shard_map/all_to_all | solution.py:316
  105.7 7.4 %all-to-all-start.2 = ((bf16[32,2,128,256]{3,2,1,0:T(8,128)(2,1)}), bf16[32,2,128,256]{3,2,1,0:T(8,128)(2,1)}, u32[]{:S(2)}, u32[]{:S(2)}) async-start(bf16[32,2,128,256]{3,2,1,0:T(8,128)(2,1)} %bitcast.133), calls=%async_computation.2 | async-start | bytes 8388608 | tf_op jit(solution)/shard_map/all_to_all | solution.py:323
  114.0 1.6 collective-permute-start.1
  115.9 51.3 %collective-permute-done = bf16[4,2,128,256]{3,2,0,1:T(8,128)(2,1)S(1)} collective-permute-done((bf16[4,2,128,256]{3,2,0,1:T(8,128)(2,1)S(1)}, bf16[4,2,128,256]{3,2,0,1:T(8,128)(2,1)S(1)}, u32[]{:S(2)}, u32[]{:S(2)}) %collective-permute-start) | collective-permute-done | bytes 524320 | tf_op jit(solution)/shard_map/ppermute | solution.py:28
  169.6 5.0 %pad_maximum_fusion.1 = bf16[80,128,256]{2,1,0:T(8,128)(2,1)} fusion(bf16[64,128,256]{2,1,0:T(8,128)(2,1)} %bitcast.16, bf16[16,128,256]{2,1,0:T(8,128)(2,1)S(1)} %get-tuple-element.59), kind=kLoop, calls=%fused_computation.7 | loop fusion | flops 2621440 | bytes 10485760 | tf_op jit(solution)/shard_map/concatenate | solution.py:333
  174.6 5.1 %pad_maximum_fusion.2 = bf16[80,128,256]{2,1,0:T(8,128)(2,1)} fusion(bf16[64,128,256]{2,1,0:T(8,128)(2,1)} %bitcast.19, bf16[16,128,256]{2,1,0:T(8,128)(2,1)S(1)} %get-tuple-element.58), kind=kLoop, calls=%fused_computation.8 | loop fusion | flops 2621440 | bytes 10485760 | tf_op jit(solution)/shard_map/concatenate | solution.py:336
  179.7 78.1 %shard_map.120 = (bf16[1024,256]{1,0:T(8,128)(2,1)S(1)}, bf16[1024,256]{1,0:T(8,128)(2,1)S(1)}, f32[16,256,128]{2,1,0:T(8,128)S(1)}, f32[16,256,128]{2,1,0:T(8,1...) custom-call(s32[128]{0:T(128)S(1)} %reshape.177.rows_ref, s32[8]{0:T(128)S(1)} %copy-done.2, ...), custom_call_target="tpu_custom_call" | custom-call | flops 12884901888 | bytes 33554432 | tf_op jit(solution)/shard_map/pallas_call | solution.py:232
  257.8 58.4 %all_to_all.65 = bf16[32,2,256,128]{3,2,1,0:T(8,128)(2,1)} all-to-all(bf16[32,2,256,128]{3,2,1,0:T(8,128)(2,1)} %bitcast.148), channel_id=1, replica_groups=mesh['blk'=32,'head'=4] {'blk'}, dimensions={0} | all-to-all | bytes 8388608 | tf_op jit(solution)/shard_map/all_to_all | solution.py:366
  316.3 5.9 %all-to-all-start.5 = ((bf16[32,2,256,128]{3,2,1,0:T(8,128)(2,1)}), bf16[32,2,256,128]{3,2,1,0:T(8,128)(2,1)}, u32[]{:S(2)}, u32[]{:S(2)}) async-start(bf16[32,2,256,128]{3,2,1,0:T(8,128)(2,1)} %bitcast.146), calls=%async_computation.5 | async-start | bytes 8388608 | tf_op jit(solution)/shard_map/all_to_all | solution.py:367
  322.2 2.0 fusion
  324.4 1.6 collective-permute-start.3
  326.1 2.1 copy.94
  328.2 1.6 fusion.7
  329.8 46.5 %collective-permute-done.2 = bf16[4,2,256,128]{3,2,0,1:T(8,128)(2,1)S(1)} collective-permute-done((bf16[4,2,256,128]{3,2,0,1:T(8,128)(2,1)S(1)}, bf16[4,2,256,128]{3,2,0,1:T(8,128)(2,1)S(1)}, u32[]{:S(2)}, u32[]{:S(2)}) %collective-permute-start.2) | collective-permute-done | bytes 524320 | tf_op jit(solution)/shard_map/ppermute | solution.py:39
  377.4 2.8 fusion.15
  380.2 2.3 fusion.4
  382.6 3.5 all-to-all-start.3
  386.1 4.5 %fusion.1 = f32[8,256,128]{2,0,1:T(8,128)S(1)} fusion(s32[64]{0:T(128)S(1)} %eq.64, bf16[8,8,256,128]{3,2,1,0:T(8,128)(2,1)} %bitcast.68), kind=kOutput, calls=%fused_computation.12 | convolution fusion | flops 33554944 | bytes 5243136 | tf_op jit(solution)/shard_map/dot_general | solution.py:377
  390.6 2.0 fusion.17
  393.2 2.1 copy.103
  395.3 6.9 %all-to-all-done.3 = bf16[2,1024,256]{2,0,1:T(2,128)(2,1)S(1)} async-done(((bf16[2,1024,256]{2,0,1:T(2,128)(2,1)}), bf16[2,1024,256]{2,0,1:T(2,128)(2,1)S(1)}, u32[]{:S(2)}, u32[]{:S(2)}) %all-to-all-start.3) | async-done | bytes 1048608 | tf_op jit(solution)/shard_map/all_to_all | solution.py:394
  402.2 3.8 all-to-all-start.6
  410.7 10.4 %all-to-all-done.6 = bf16[2,1024,256]{2,0,1:T(2,128)(2,1)S(1)} async-done(((bf16[2,1024,256]{2,0,1:T(2,128)(2,1)}), bf16[2,1024,256]{2,0,1:T(2,128)(2,1)S(1)}, u32[]{:S(2)}, u32[]{:S(2)}) %all-to-all-start.6) | async-done | bytes 1048608 | tf_op jit(solution)/shard_map/all_to_all | solution.py:394
  (77 shorter events, 16.8 us)
Async XLA Ops:
  5.1 4.4 %copy-start.2 = (s32[8]{0:T(128)S(1)}, s32[8]{0:T(128)}, u32[]{:S(2)}) copy-start(s32[8]{0:T(128)} %count_ref.1) | copy-start | bytes 100
  5.1 4.4 %copy-start.9 = (s32[8,4]{0,1:T(4,128)S(1)}, s32[8,4]{0,1:T(4,128)}, u32[]{:S(2)}) copy-start(s32[8,4]{0,1:T(4,128)} %param.18) | copy-start | bytes 388
  5.1 4.6 %copy-start.8 = (s32[8,4]{0,1:T(4,128)S(1)}, s32[8,4]{0,1:T(4,128)}, u32[]{:S(2)}) copy-start(s32[8,4]{0,1:T(4,128)} %param.17) | copy-start | bytes 388
  5.1 30.8 %all-to-all-start = ((bf16[4,256,1024]{1,0,2:T(4,128)(2,1)}), bf16[4,256,1024]{1,0,2:T(4,128)(2,1)S(1)}, u32[]{:S(2)}, u32[]{:S(2)}) async-start(bf16[4,256,1024]{1,0,2:T(4,128)(2,1)} %copy.87), calls=%async_computation | async-start | bytes 4194304 | tf_op jit(solution)/shard_map/all_to_all | solution.py:270
  45.7 60.0 %all-to-all-start.1 = ((bf16[32,2,128,256]{3,2,1,0:T(8,128)(2,1)}), bf16[32,2,128,256]{3,2,1,0:T(8,128)(2,1)}, u32[]{:S(2)}, u32[]{:S(2)}) async-start(bf16[32,2,128,256]{3,2,1,0:T(8,128)(2,1)} %bitcast.134), calls=%async_computation.1 | async-start | bytes 8388608 | tf_op jit(solution)/shard_map/all_to_all | solution.py:316
  105.7 7.5 %copy-start.6 = (s32[4,8,16]{2,1,0:T(8,128)S(1)}, s32[4,8,16]{2,1,0:T(8,128)}, u32[]{:S(2)}) copy-start(s32[4,8,16]{2,1,0:T(8,128)} %param.21) | copy-start | bytes 6148
  105.7 68.9 %all-to-all-start.2 = ((bf16[32,2,128,256]{3,2,1,0:T(8,128)(2,1)}), bf16[32,2,128,256]{3,2,1,0:T(8,128)(2,1)}, u32[]{:S(2)}, u32[]{:S(2)}) async-start(bf16[32,2,128,256]{3,2,1,0:T(8,128)(2,1)} %bitcast.133), calls=%async_computation.2 | async-start | bytes 8388608 | tf_op jit(solution)/shard_map/all_to_all | solution.py:323
  113.1 2.5 copy-start.7
  113.8 53.4 %collective-permute-start = (bf16[4,2,128,256]{3,2,0,1:T(8,128)(2,1)S(1)}, bf16[4,2,128,256]{3,2,0,1:T(8,128)(2,1)S(1)}, u32[]{:S(2)}, u32[]{:S(2)}) collective-permute-start(bf16[4,2,128,256]{3,2,0,1:T(8,128)(2,1)S(1)} %get-tuple-element.68), channel_id=1, source_target_pairs={{0,4},{4,8},{8,12},{12,16},{16,20},{20,24},{24,28},{28,32},{32,36}... | collective-permute-start | bytes 1572872 | tf_op jit(solution)/shard_map/ppermute | solution.py:28
  114.0 54.0 %collective-permute-start.1 = (bf16[4,2,128,256]{3,2,0,1:T(8,128)(2,1)S(1)}, bf16[4,2,128,256]{3,2,0,1:T(8,128)(2,1)}, u32[]{:S(2)}, u32[]{:S(2)}) collective-permute-start(bf16[4,2,128,256]{3,2,0,1:T(8,128)(2,1)S(1)} %get-tuple-element.69), channel_id=1, source_target_pairs={{4,0},{8,4},{12,8},{16,12},{20,16},{24,20},{28,24},{32,28},{36,32}... | collective-permute-start | bytes 1572872 | tf_op jit(solution)/shard_map/ppermute | solution.py:31
  167.2 0.8 copy-start.5
  174.6 5.1 %copy-start = (bf16[1,4,256,256]{3,2,1,0:T(8,128)(2,1)S(1)}, bf16[1,4,256,256]{3,2,1,0:T(8,128)(2,1)}, u32[]{:S(2)}) copy-start(bf16[1,4,256,256]{3,2,1,0:T(8,128)(2,1)} %get-tuple-element.62) | copy-start | bytes 1572868
  174.6 5.1 %copy-start.1 = (bf16[1,4,256,256]{3,2,1,0:T(8,128)(2,1)S(1)}, bf16[1,4,256,256]{3,2,1,0:T(8,128)(2,1)}, u32[]{:S(2)}) copy-start(bf16[1,4,256,256]{3,2,1,0:T(8,128)(2,1)} %get-tuple-element.63) | copy-start | bytes 1572868
  316.3 66.3 %all-to-all-start.5 = ((bf16[32,2,256,128]{3,2,1,0:T(8,128)(2,1)}), bf16[32,2,256,128]{3,2,1,0:T(8,128)(2,1)}, u32[]{:S(2)}, u32[]{:S(2)}) async-start(bf16[32,2,256,128]{3,2,1,0:T(8,128)(2,1)} %bitcast.146), calls=%async_computation.5 | async-start | bytes 8388608 | tf_op jit(solution)/shard_map/all_to_all | solution.py:367
  324.2 52.0 %collective-permute-start.2 = (bf16[4,2,256,128]{3,2,0,1:T(8,128)(2,1)S(1)}, bf16[4,2,256,128]{3,2,0,1:T(8,128)(2,1)S(1)}, u32[]{:S(2)}, u32[]{:S(2)}) collective-permute-start(bf16[4,2,256,128]{3,2,0,1:T(8,128)(2,1)S(1)} %get-tuple-element.57), channel_id=1, source_target_pairs={{124,0},{0,4},{4,8},{8,12},{12,16},{16,20},{20,24},{24,28},{28,32}... | collective-permute-start | bytes 1572872 | tf_op jit(solution)/shard_map/ppermute | solution.py:39
  324.4 53.0 %collective-permute-start.3 = (bf16[4,2,256,128]{3,2,0,1:T(8,128)(2,1)S(1)}, bf16[4,2,256,128]{3,2,0,1:T(8,128)(2,1)S(1)}, u32[]{:S(2)}, u32[]{:S(2)}) collective-permute-start(bf16[4,2,256,128]{3,2,0,1:T(8,128)(2,1)S(1)} %get-tuple-element.56), channel_id=1, source_target_pairs={{4,0},{8,4},{12,8},{16,12},{20,16},{24,20},{28,24},{32,28},{36,32}... | collective-permute-start | bytes 1572872 | tf_op jit(solution)/shard_map/ppermute | solution.py:39
  326.0 2.2 copy-start.3
  376.3 4.0 copy-start.4
  382.6 19.7 %all-to-all-start.3 = ((bf16[2,1024,256]{2,0,1:T(2,128)(2,1)}), bf16[2,1024,256]{2,0,1:T(2,128)(2,1)S(1)}, u32[]{:S(2)}, u32[]{:S(2)}) async-start(bf16[2,1024,256]{2,0,1:T(2,128)(2,1)} %copy.94), calls=%async_computation.3 | async-start | bytes 2097152 | tf_op jit(solution)/shard_map/all_to_all | solution.py:394
  402.2 18.8 %all-to-all-start.6 = ((bf16[2,1024,256]{2,0,1:T(2,128)(2,1)}), bf16[2,1024,256]{2,0,1:T(2,128)(2,1)S(1)}, u32[]{:S(2)}, u32[]{:S(2)}) async-start(bf16[2,1024,256]{2,0,1:T(2,128)(2,1)} %copy.103), calls=%async_computation.6 | async-start | bytes 2097152 | tf_op jit(solution)/shard_map/all_to_all | solution.py:394

commit v12 on v11

--- a/solution.py
+++ b/solution.py
@@ -68,7 +68,7 @@
 
 
 def attention_kernel(
-    rows_ref, count_ref, seed_ref, q_ref, g_ref, kt_ref, vt_ref,
+    rows_ref, count_ref, seed_ref, q_ref, g_ref, kt_ref, vt_ref, kf_ref, vf_ref,
     att_ref, qg_ref, nk_ref, nv_ref, fk_ref, fv_ref,
     s_scr, keep_scr, drop_scr,
     *, scale, near_count, slot_count, blocks, head_size,
@@ -102,10 +102,14 @@
         return pl.multiple_of(rows_ref[base + j] * BS, BS)
 
     def keys(j):
-        return kt_ref[pl.ds(start_of(j), BS), :]
+        if j <= L:
+            return kt_ref[pl.ds(start_of(j), BS), :]
+        return kf_ref[pl.ds(pl.multiple_of(start_of(j) - near_count * BS, BS), BS), :]
 
     def values(j):
-        return vt_ref[pl.ds(start_of(j), BS), :]
+        if j <= L:
+            return vt_ref[pl.ds(start_of(j), BS), :]
+        return vf_ref[pl.ds(pl.multiple_of(start_of(j) - near_count * BS, BS), BS), :]
 
     def pick(parts, heads):
         out = parts[-1]
@@ -197,7 +201,7 @@
     qg_ref[...] = (pick(qacc, lane_head) * scale).astype(qg_ref.dtype)
 
 
-def block_attention(rows, counts, seeds, q, g, kt, vt, *, near_count, far_count, scale, head_size):
+def block_attention(rows, counts, seeds, q, g, kt, vt, kf, vf, *, near_count, far_count, scale, head_size):
     row_count, local_width = q.shape
     width = 2 * head_size
     groups = local_width // width
@@ -209,12 +213,13 @@
     )
     q_spec = pl.BlockSpec((BS, width), lambda p, c, *_: (c, p))
     table_spec = pl.BlockSpec((kt.shape[0], width), lambda p, c, *_: (0, p))
+    far_table_spec = pl.BlockSpec((kf.shape[0], width), lambda p, c, *_: (0, p))
     near_spec = pl.BlockSpec((near_count, width, BS), lambda p, c, *_: (0, p, 0))
     far_spec = pl.BlockSpec((far_count, width, BS), lambda p, c, *_: (0, p, 0))
     grid_spec = pltpu.PrefetchScalarGridSpec(
         num_scalar_prefetch=3,
         grid=(groups, blocks),
-        in_specs=[q_spec, q_spec, table_spec, table_spec],
+        in_specs=[q_spec, q_spec, table_spec, table_spec, far_table_spec, far_table_spec],
         out_specs=[q_spec, q_spec, near_spec, near_spec, far_spec, far_spec],
         scratch_shapes=[
             pltpu.VMEM((2, slot_count, BS, BS), jnp.float32),
@@ -244,7 +249,7 @@
             dimension_semantics=("arbitrary", "arbitrary"), vmem_limit_bytes=48 * 1024 * 1024
         ),
         cost_estimate=cost,
-    )(rows, counts, seeds, q, g, kt, vt)
+    )(rows, counts, seeds, q, g, kt, vt, kf, vf)
 
 
 def on_device(
@@ -330,12 +335,6 @@
     )
     near_count = QB_DEV + 2 * W
     far_total_count = peer_count * capacity
-    key_table = jnp.concatenate(
-        [widened[:, 0], far_key.reshape(far_total_count, BS, local_width)], axis=0
-    )
-    value_table = jnp.concatenate(
-        [widened[:, 1], far_value.reshape(far_total_count, BS, local_width)], axis=0
-    )
     local_block = jnp.arange(QB_DEV, dtype=jnp.int32)[:, None]
     self_slot = local_block + W
     near_slot = local_block + W + local_offset
@@ -345,7 +344,6 @@
     live_slots = (slot_number <= L) | (slot_number - 1 - L < live_count[:, None])
     slot_rows = table_rows.reshape(-1).astype(jnp.int32)
     seed_flat = drop_seed.reshape(-1).astype(jnp.int32)
-    table_count = key_table.shape[0]
 
     att_out, qg_out, nk, nv, fk, fv = block_attention(
         slot_rows,
@@ -353,8 +351,10 @@
         seed_flat,
         query_local,
         grad_local,
-        key_table.reshape(table_count * BS, local_width),
-        value_table.reshape(table_count * BS, local_width),
+        widened[:, 0].reshape(near_count * BS, local_width),
+        widened[:, 1].reshape(near_count * BS, local_width),
+        far_key.reshape(far_total_count * BS, local_width),
+        far_value.reshape(far_total_count * BS, local_width),
         near_count=near_count,
         far_count=far_total_count,
         scale=score_scale,

time: 425 us -> 415 us (0.976)
  other arithmetic: 24 us -> 12.6 us
    all_to_all x1, waiting for transfers between devices: 0.01 us -> 46.9 us  [on_device(): lax.all_to_all(asked_of(value_blocks).reshape(reply_shape), 'blk', split_...]
    all_to_all x1, waiting for transfers between devices: 46.8 us -> 0.01 us  [on_device(): lax.all_to_all(asked_of(key_blocks).reshape(reply_shape), 'blk', split_ax...]
    concatenate x2 -> x0, other arithmetic: 10.1 us -> none  [the longest x1 5.09 us: on_device(): jnp.concatenate([widened[:, 1], far_value.reshape(far_total_count, BS, lo...]
  transfers between devices with their start and end apart: 10 -> 10, of which waited for: 5 -> 5; matrix products, arithmetic and copies ran while one was open for 9% -> 8% of each run, Pallas kernels for 0% -> 0%
where the time goes in v12:
time: 415 us; the launch traced here: 414 us
  waiting for transfers between devices  162 us (39%)
  blocking collectives  83.9 us (20%)
  Pallas kernels  78.6 us (19%)
  starting transfers between devices  37.3 us (9%)
  local copies, waits for them, and re-layouts  29.5 us (7%)
  other arithmetic  12.6 us (3%)
  matrix products  9.39 us (2%)
    pallas_call x1, Pallas kernels, block_attention(): pl.pallas_call(kernel, grid_spec=grid_spec, out_shape=[jax.ShapeDtypeStru...  78.6 us
    all_to_all x1, blocking collectives, on_device(): lax.all_to_all(fk.reshape(column_shape), 'blk', split_axis=0, concat_axis...  58.4 us
    ppermute x1, waiting for transfers between devices, padded(): lax.ppermute(lax.slice_in_dim(block, block.shape[dim] - width, None, axis...  51.3 us
    all_to_all x1, waiting for transfers between devices, on_device(): lax.all_to_all(asked_of(value_blocks).reshape(reply_shape), 'blk', split_...  46.9 us
    ppermute x2, waiting for transfers between devices, shifted(): return lax.ppermute(block, axis, route)  46.5 us
    all_gather x1, blocking collectives, on_device(): lax.all_gather(jnp.stack([flat_device, asked_block.reshape(-1)]), 'blk',...  25.5 us
    all_to_all x2, waiting for transfers between devices, to_rows(): lax.all_to_all(jnp.stack(arrays), 'head', split_axis=1, concat_axis=2, ti...  17.3 us
    unnamed x27, local copies, waits for them, and re-layouts  12.1 us
  transfers between devices with their start and end apart: 10, of which 5 were waited for; matrix products, arithmetic and copies ran while one was open for 8% of the time, Pallas kernels for 0%

profile of v12, /device:TPU:8, one launch (start us, length us, event | category | flops | bytes accessed | tf_op | source)
XLA Modules:
  0.0 414.3 jit_solution(6925844744166798944)
XLA Ops:
  0.6 1.8 pad_maximum_fusion.1
  2.4 2.6 copy.87
  5.1 4.4 %all-to-all-start = ((bf16[4,256,1024]{1,0,2:T(4,128)(2,1)}), bf16[4,256,1024]{1,0,2:T(4,128)(2,1)S(1)}, u32[]{:S(2)}, u32[]{:S(2)}) async-start(bf16[4,256,1024]{1,0,2:T(4,128)(2,1)} %copy.87), calls=%async_computation | async-start | bytes 4194304 | tf_op jit(solution)/shard_map/all_to_all | solution.py:275
  9.8 25.5 %all-gather.1 = s32[32,2,32]{2,1,0:T(2,128)S(1)} all-gather(s32[1,2,32]{2,1,0:T(2,128)S(1)} %add_bitcast_fusion), channel_id=2, replica_groups=mesh['blk'=32,'head'=4] {'blk'}, dimensions={0}, use_global_device_ids=true | all-gather | bytes 8448 | tf_op jit(solution)/shard_map/all_gather | solution.py:291
  35.9 2.6 copy.88
  38.5 2.6 fusion.32
  41.4 1.3 convolution_convert_fusion
  42.7 3.1 copy.114
  45.8 8.5 %all-to-all-start.2 = ((bf16[32,2,128,256]{3,2,1,0:T(8,128)(2,1)}), bf16[32,2,128,256]{3,2,1,0:T(8,128)(2,1)}, u32[]{:S(2)}, u32[]{:S(2)}) async-start(bf16[32,2,128,256]{3,2,1,0:T(8,128)(2,1)} %bitcast.132), calls=%async_computation.2 | async-start | bytes 8388608 | tf_op jit(solution)/shard_map/all_to_all | solution.py:328
  55.8 3.0 copy.113
  58.9 46.9 %all-to-all-done.2 = bf16[32,2,128,256]{3,2,1,0:T(8,128)(2,1)} async-done(((bf16[32,2,128,256]{3,2,1,0:T(8,128)(2,1)}), bf16[32,2,128,256]{3,2,1,0:T(8,128)(2,1)}, u32[]{:S(2)}, u32[]{:S(2)}) %all-to-all-start.2) | async-done | bytes 4194336 | tf_op jit(solution)/shard_map/all_to_all | solution.py:328
  105.7 7.4 %all-to-all-start.1 = ((bf16[32,2,128,256]{3,2,1,0:T(8,128)(2,1)}), bf16[32,2,128,256]{3,2,1,0:T(8,128)(2,1)}, u32[]{:S(2)}, u32[]{:S(2)}) async-start(bf16[32,2,128,256]{3,2,1,0:T(8,128)(2,1)} %bitcast.131), calls=%async_computation.1 | async-start | bytes 8388608 | tf_op jit(solution)/shard_map/all_to_all | solution.py:321
  114.0 1.6 collective-permute-start.1
  115.9 51.3 %collective-permute-done = bf16[4,2,128,256]{3,2,0,1:T(8,128)(2,1)S(1)} collective-permute-done((bf16[4,2,128,256]{3,2,0,1:T(8,128)(2,1)S(1)}, bf16[4,2,128,256]{3,2,0,1:T(8,128)(2,1)S(1)}, u32[]{:S(2)}, u32[]{:S(2)}) %collective-permute-start) | collective-permute-done | bytes 524320 | tf_op jit(solution)/shard_map/ppermute | solution.py:28
  169.8 78.6 %shard_map.120 = (bf16[1024,256]{1,0:T(8,128)(2,1)S(1)}, bf16[1024,256]{1,0:T(8,128)(2,1)S(1)}, f32[16,256,128]{2,1,0:T(8,128)}, f32[16,256,128]{2,1,0:T(8,128)}...) custom-call(s32[128]{0:T(128)S(1)} %reshape.171.rows_ref, s32[8]{0:T(128)S(1)} %copy-done.2, ...), custom_call_target="tpu_custom_call" | custom-call | flops 12884901888 | bytes 25165824 | tf_op jit(solution)/shard_map/pallas_call | solution.py:237
  248.3 58.4 %all_to_all.65 = bf16[32,2,256,128]{3,2,1,0:T(8,128)(2,1)} all-to-all(bf16[32,2,256,128]{3,2,1,0:T(8,128)(2,1)} %bitcast.144), channel_id=1, replica_groups=mesh['blk'=32,'head'=4] {'blk'}, dimensions={0} | all-to-all | bytes 8388608 | tf_op jit(solution)/shard_map/all_to_all | solution.py:366
  306.8 6.0 %all-to-all-start.5 = ((bf16[32,2,256,128]{3,2,1,0:T(8,128)(2,1)}), bf16[32,2,256,128]{3,2,1,0:T(8,128)(2,1)}, u32[]{:S(2)}, u32[]{:S(2)}) async-start(bf16[32,2,256,128]{3,2,1,0:T(8,128)(2,1)} %bitcast.142), calls=%async_computation.5 | async-start | bytes 8388608 | tf_op jit(solution)/shard_map/all_to_all | solution.py:367
  312.8 2.0 fusion
  315.1 1.6 collective-permute-start.3
  316.8 2.1 copy.94
  318.9 1.5 fusion.7
  320.4 46.5 %collective-permute-done.2 = bf16[4,2,256,128]{3,2,0,1:T(8,128)(2,1)S(1)} collective-permute-done((bf16[4,2,256,128]{3,2,0,1:T(8,128)(2,1)S(1)}, bf16[4,2,256,128]{3,2,0,1:T(8,128)(2,1)S(1)}, u32[]{:S(2)}, u32[]{:S(2)}) %collective-permute-start.2) | collective-permute-done | bytes 524320 | tf_op jit(solution)/shard_map/ppermute | solution.py:39
  368.1 2.8 fusion.15
  370.9 2.3 fusion.4
  373.2 3.7 all-to-all-start.3
  376.9 4.5 %fusion.1 = f32[8,256,128]{2,0,1:T(8,128)S(1)} fusion(s32[64]{0:T(128)S(1)} %eq.64, bf16[8,8,256,128]{3,2,1,0:T(8,128)(2,1)} %bitcast.66), kind=kOutput, calls=%fused_computation.10 | convolution fusion | flops 33554944 | bytes 5243136 | tf_op jit(solution)/shard_map/dot_general | solution.py:377
  381.5 2.0 fusion.17
  384.1 2.1 copy.103
  386.1 6.7 %all-to-all-done.3 = bf16[2,1024,256]{2,0,1:T(2,128)(2,1)S(1)} async-done(((bf16[2,1024,256]{2,0,1:T(2,128)(2,1)}), bf16[2,1024,256]{2,0,1:T(2,128)(2,1)S(1)}, u32[]{:S(2)}, u32[]{:S(2)}) %all-to-all-start.3) | async-done | bytes 1048608 | tf_op jit(solution)/shard_map/all_to_all | solution.py:394
  392.9 3.5 all-to-all-start.6
  396.4 1.5 fusion.34
  401.0 10.6 %all-to-all-done.6 = bf16[2,1024,256]{2,0,1:T(2,128)(2,1)S(1)} async-done(((bf16[2,1024,256]{2,0,1:T(2,128)(2,1)}), bf16[2,1024,256]{2,0,1:T(2,128)(2,1)S(1)}, u32[]{:S(2)}, u32[]{:S(2)}) %all-to-all-start.6) | async-done | bytes 1048608 | tf_op jit(solution)/shard_map/all_to_all | solution.py:394
  (75 shorter events, 14.1 us)
Async XLA Ops:
  5.1 4.4 %copy-start.2 = (s32[8]{0:T(128)S(1)}, s32[8]{0:T(128)}, u32[]{:S(2)}) copy-start(s32[8]{0:T(128)} %count_ref.1) | copy-start | bytes 100
  5.1 4.4 %copy-start.9 = (s32[8,4]{0,1:T(4,128)S(1)}, s32[8,4]{0,1:T(4,128)}, u32[]{:S(2)}) copy-start(s32[8,4]{0,1:T(4,128)} %param.18) | copy-start | bytes 388
  5.1 4.6 %copy-start.8 = (s32[8,4]{0,1:T(4,128)S(1)}, s32[8,4]{0,1:T(4,128)}, u32[]{:S(2)}) copy-start(s32[8,4]{0,1:T(4,128)} %param.17) | copy-start | bytes 388
  5.1 30.8 %all-to-all-start = ((bf16[4,256,1024]{1,0,2:T(4,128)(2,1)}), bf16[4,256,1024]{1,0,2:T(4,128)(2,1)S(1)}, u32[]{:S(2)}, u32[]{:S(2)}) async-start(bf16[4,256,1024]{1,0,2:T(4,128)(2,1)} %copy.87), calls=%async_computation | async-start | bytes 4194304 | tf_op jit(solution)/shard_map/all_to_all | solution.py:275
  45.8 60.0 %all-to-all-start.2 = ((bf16[32,2,128,256]{3,2,1,0:T(8,128)(2,1)}), bf16[32,2,128,256]{3,2,1,0:T(8,128)(2,1)}, u32[]{:S(2)}, u32[]{:S(2)}) async-start(bf16[32,2,128,256]{3,2,1,0:T(8,128)(2,1)} %bitcast.132), calls=%async_computation.2 | async-start | bytes 8388608 | tf_op jit(solution)/shard_map/all_to_all | solution.py:328
  105.7 7.5 %copy-start.6 = (s32[4,8,16]{2,1,0:T(8,128)S(1)}, s32[4,8,16]{2,1,0:T(8,128)}, u32[]{:S(2)}) copy-start(s32[4,8,16]{2,1,0:T(8,128)} %param.21) | copy-start | bytes 6148
  105.7 61.9 %all-to-all-start.1 = ((bf16[32,2,128,256]{3,2,1,0:T(8,128)(2,1)}), bf16[32,2,128,256]{3,2,1,0:T(8,128)(2,1)}, u32[]{:S(2)}, u32[]{:S(2)}) async-start(bf16[32,2,128,256]{3,2,1,0:T(8,128)(2,1)} %bitcast.131), calls=%async_computation.1 | async-start | bytes 8388608 | tf_op jit(solution)/shard_map/all_to_all | solution.py:321
  113.2 2.5 copy-start.7
  113.8 53.4 %collective-permute-start = (bf16[4,2,128,256]{3,2,0,1:T(8,128)(2,1)S(1)}, bf16[4,2,128,256]{3,2,0,1:T(8,128)(2,1)S(1)}, u32[]{:S(2)}, u32[]{:S(2)}) collective-permute-start(bf16[4,2,128,256]{3,2,0,1:T(8,128)(2,1)S(1)} %get-tuple-element.68), channel_id=1, source_target_pairs={{0,4},{4,8},{8,12},{12,16},{16,20},{20,24},{24,28},{28,32},{32,36}... | collective-permute-start | bytes 1572872 | tf_op jit(solution)/shard_map/ppermute | solution.py:28
  114.0 53.2 %collective-permute-start.1 = (bf16[4,2,128,256]{3,2,0,1:T(8,128)(2,1)S(1)}, bf16[4,2,128,256]{3,2,0,1:T(8,128)(2,1)S(1)}, u32[]{:S(2)}, u32[]{:S(2)}) collective-permute-start(bf16[4,2,128,256]{3,2,0,1:T(8,128)(2,1)S(1)} %get-tuple-element.69), channel_id=1, source_target_pairs={{4,0},{8,4},{12,8},{16,12},{20,16},{24,20},{28,24},{32,28},{36,32}... | collective-permute-start | bytes 1572872 | tf_op jit(solution)/shard_map/ppermute | solution.py:31
  167.7 1.0 copy-start
  168.7 1.0 copy-start.1
  306.8 6.1 %copy-start.3 = (f32[16,256,128]{2,1,0:T(8,128)S(1)}, f32[16,256,128]{2,1,0:T(8,128)}, u32[]{:S(2)}) copy-start(f32[16,256,128]{2,1,0:T(8,128)} %get-tuple-element.36) | copy-start | bytes 6291460
  306.8 66.4 %all-to-all-start.5 = ((bf16[32,2,256,128]{3,2,1,0:T(8,128)(2,1)}), bf16[32,2,256,128]{3,2,1,0:T(8,128)(2,1)}, u32[]{:S(2)}, u32[]{:S(2)}) async-start(bf16[32,2,256,128]{3,2,1,0:T(8,128)(2,1)} %bitcast.142), calls=%async_computation.5 | async-start | bytes 8388608 | tf_op jit(solution)/shard_map/all_to_all | solution.py:367
  314.9 52.0 %collective-permute-start.2 = (bf16[4,2,256,128]{3,2,0,1:T(8,128)(2,1)S(1)}, bf16[4,2,256,128]{3,2,0,1:T(8,128)(2,1)S(1)}, u32[]{:S(2)}, u32[]{:S(2)}) collective-permute-start(bf16[4,2,256,128]{3,2,0,1:T(8,128)(2,1)S(1)} %get-tuple-element.57), channel_id=1, source_target_pairs={{124,0},{0,4},{4,8},{8,12},{12,16},{16,20},{20,24},{24,28},{28,32}... | collective-permute-start | bytes 1572872 | tf_op jit(solution)/shard_map/ppermute | solution.py:39
  315.1 53.0 %collective-permute-start.3 = (bf16[4,2,256,128]{3,2,0,1:T(8,128)(2,1)S(1)}, bf16[4,2,256,128]{3,2,0,1:T(8,128)(2,1)S(1)}, u32[]{:S(2)}, u32[]{:S(2)}) collective-permute-start(bf16[4,2,256,128]{3,2,0,1:T(8,128)(2,1)S(1)} %get-tuple-element.56), channel_id=1, source_target_pairs={{4,0},{8,4},{12,8},{16,12},{20,16},{24,20},{28,24},{32,28},{36,32}... | collective-permute-start | bytes 1572872 | tf_op jit(solution)/shard_map/ppermute | solution.py:39
  316.7 2.2 copy-start.4
  366.9 4.0 copy-start.5
  373.2 19.7 %all-to-all-start.3 = ((bf16[2,1024,256]{2,0,1:T(2,128)(2,1)}), bf16[2,1024,256]{2,0,1:T(2,128)(2,1)S(1)}, u32[]{:S(2)}, u32[]{:S(2)}) async-start(bf16[2,1024,256]{2,0,1:T(2,128)(2,1)} %copy.94), calls=%async_computation.3 | async-start | bytes 2097152 | tf_op jit(solution)/shard_map/all_to_all | solution.py:394
  392.9 18.8 %all-to-all-start.6 = ((bf16[2,1024,256]{2,0,1:T(2,128)(2,1)}), bf16[2,1024,256]{2,0,1:T(2,128)(2,1)S(1)}, u32[]{:S(2)}, u32[]{:S(2)}) async-start(bf16[2,1024,256]{2,0,1:T(2,128)(2,1)} %copy.103), calls=%async_computation.6 | async-start | bytes 2097152 | tf_op jit(solution)/shard_map/all_to_all | solution.py:394

commit v13 on v12

--- a/solution.py
+++ b/solution.py
@@ -103,12 +103,12 @@
 
     def keys(j):
         if j <= L:
-            return kt_ref[pl.ds(start_of(j), BS), :]
+            return kt_ref[pl.ds(pl.multiple_of(rows_ref[base + j] * (2 * BS), BS), BS), :]
         return kf_ref[pl.ds(pl.multiple_of(start_of(j) - near_count * BS, BS), BS), :]
 
     def values(j):
         if j <= L:
-            return vt_ref[pl.ds(start_of(j), BS), :]
+            return kt_ref[pl.ds(pl.multiple_of(rows_ref[base + j] * (2 * BS) + BS, BS), BS), :]
         return vf_ref[pl.ds(pl.multiple_of(start_of(j) - near_count * BS, BS), BS), :]
 
     def pick(parts, heads):
@@ -351,8 +351,8 @@
         seed_flat,
         query_local,
         grad_local,
-        widened[:, 0].reshape(near_count * BS, local_width),
-        widened[:, 1].reshape(near_count * BS, local_width),
+        widened.reshape(near_count * 2 * BS, local_width),
+        widened.reshape(near_count * 2 * BS, local_width),
         far_key.reshape(far_total_count * BS, local_width),
         far_value.reshape(far_total_count * BS, local_width),
         near_count=near_count,

time: 415 us -> 416 us (level)
    unnamed x27 -> x25, local copies, waits for them, and re-layouts: 12.1 us -> 12.1 us
where the time goes in v13:
time: 416 us; the launch traced here: 415 us
  waiting for transfers between devices  162 us (39%)
  blocking collectives  83.9 us (20%)
  Pallas kernels  78 us (19%)
  starting transfers between devices  37.2 us (9%)
  local copies, waits for them, and re-layouts  29.3 us (7%)
  other arithmetic  13.9 us (3%)
  matrix products  9.39 us (2%)
    pallas_call x1, Pallas kernels, block_attention(): pl.pallas_call(kernel, grid_spec=grid_spec, out_shape=[jax.ShapeDtypeStru...  78 us
    all_to_all x1, blocking collectives, on_device(): lax.all_to_all(fk.reshape(column_shape), 'blk', split_axis=0, concat_axis...  58.4 us
    ppermute x1, waiting for transfers between devices, padded(): lax.ppermute(lax.slice_in_dim(block, block.shape[dim] - width, None, axis...  51.3 us
    all_to_all x1, waiting for transfers between devices, on_device(): lax.all_to_all(asked_of(value_blocks).reshape(reply_shape), 'blk', split_...  46.8 us
    ppermute x2, waiting for transfers between devices, shifted(): return lax.ppermute(block, axis, route)  46.5 us
    all_gather x1, blocking collectives, on_device(): lax.all_gather(jnp.stack([flat_device, asked_block.reshape(-1)]), 'blk',...  25.5 us
    all_to_all x2, waiting for transfers between devices, to_rows(): lax.all_to_all(jnp.stack(arrays), 'head', split_axis=1, concat_axis=2, ti...  17.4 us
    unnamed x25, local copies, waits for them, and re-layouts  12.1 us
  transfers between devices with their start and end apart: 10, of which 5 were waited for; matrix products, arithmetic and copies ran while one was open for 8% of the time, Pallas kernels for 0%

profile of v13, /device:TPU:8, one launch (start us, length us, event | category | flops | bytes accessed | tf_op | source)
XLA Modules:
  0.0 414.6 jit_solution(4254474767290028880)
XLA Ops:
  0.6 1.8 pad_maximum_fusion.1
  2.4 2.6 copy.87
  5.1 4.4 %all-to-all-start = ((bf16[4,256,1024]{1,0,2:T(4,128)(2,1)}), bf16[4,256,1024]{1,0,2:T(4,128)(2,1)S(1)}, u32[]{:S(2)}, u32[]{:S(2)}) async-start(bf16[4,256,1024]{1,0,2:T(4,128)(2,1)} %copy.87), calls=%async_computation | async-start | bytes 4194304 | tf_op jit(solution)/shard_map/all_to_all | solution.py:275
  9.8 25.5 %all-gather.1 = s32[32,2,32]{2,1,0:T(2,128)S(1)} all-gather(s32[1,2,32]{2,1,0:T(2,128)S(1)} %add_bitcast_fusion), channel_id=2, replica_groups=mesh['blk'=32,'head'=4] {'blk'}, dimensions={0}, use_global_device_ids=true | all-gather | bytes 8448 | tf_op jit(solution)/shard_map/all_gather | solution.py:291
  35.9 2.6 copy.88
  38.5 2.6 fusion.31
  42.7 3.1 copy.114
  45.7 8.5 %all-to-all-start.2 = ((bf16[32,2,128,256]{3,2,1,0:T(8,128)(2,1)}), bf16[32,2,128,256]{3,2,1,0:T(8,128)(2,1)}, u32[]{:S(2)}, u32[]{:S(2)}) async-start(bf16[32,2,128,256]{3,2,1,0:T(8,128)(2,1)} %bitcast.129), calls=%async_computation.2 | async-start | bytes 8388608 | tf_op jit(solution)/shard_map/all_to_all | solution.py:328
  55.8 3.0 copy.113
  58.8 46.8 %all-to-all-done.2 = bf16[32,2,128,256]{3,2,1,0:T(8,128)(2,1)} async-done(((bf16[32,2,128,256]{3,2,1,0:T(8,128)(2,1)}), bf16[32,2,128,256]{3,2,1,0:T(8,128)(2,1)}, u32[]{:S(2)}, u32[]{:S(2)}) %all-to-all-start.2) | async-done | bytes 4194336 | tf_op jit(solution)/shard_map/all_to_all | solution.py:328
  105.7 7.4 %all-to-all-start.1 = ((bf16[32,2,128,256]{3,2,1,0:T(8,128)(2,1)}), bf16[32,2,128,256]{3,2,1,0:T(8,128)(2,1)}, u32[]{:S(2)}, u32[]{:S(2)}) async-start(bf16[32,2,128,256]{3,2,1,0:T(8,128)(2,1)} %bitcast.128), calls=%async_computation.1 | async-start | bytes 8388608 | tf_op jit(solution)/shard_map/all_to_all | solution.py:321
  114.0 1.6 collective-permute-start.1
  115.9 51.3 %collective-permute-done = bf16[4,2,128,256]{3,2,1,0:T(8,128)(2,1)S(1)} collective-permute-done((bf16[4,2,128,256]{3,2,1,0:T(8,128)(2,1)S(1)}, bf16[4,2,128,256]{3,2,1,0:T(8,128)(2,1)S(1)}, u32[]{:S(2)}, u32[]{:S(2)}) %collective-permute-start) | collective-permute-done | bytes 524320 | tf_op jit(solution)/shard_map/ppermute | solution.py:28
  167.2 1.6 pad_maximum_fusion.2
  170.9 78.0 %shard_map.120 = (bf16[1024,256]{1,0:T(8,128)(2,1)S(1)}, bf16[1024,256]{1,0:T(8,128)(2,1)S(1)}, f32[16,256,128]{2,1,0:T(8,128)S(1)}, f32[16,256,128]{2,1,0:T(8,1...) custom-call(s32[128]{0:T(128)S(1)} %reshape.175.rows_ref, s32[8]{0:T(128)S(1)} %copy-done.2, ...), custom_call_target="tpu_custom_call" | custom-call | flops 12884901888 | bytes 27262976 | tf_op jit(solution)/shard_map/pallas_call | solution.py:237
  248.8 58.4 %all_to_all.65 = bf16[32,2,256,128]{3,2,1,0:T(8,128)(2,1)} all-to-all(bf16[32,2,256,128]{3,2,1,0:T(8,128)(2,1)} %bitcast.141), channel_id=1, replica_groups=mesh['blk'=32,'head'=4] {'blk'}, dimensions={0} | all-to-all | bytes 8388608 | tf_op jit(solution)/shard_map/all_to_all | solution.py:366
  307.3 5.9 %all-to-all-start.5 = ((bf16[32,2,256,128]{3,2,1,0:T(8,128)(2,1)}), bf16[32,2,256,128]{3,2,1,0:T(8,128)(2,1)}, u32[]{:S(2)}, u32[]{:S(2)}) async-start(bf16[32,2,256,128]{3,2,1,0:T(8,128)(2,1)} %bitcast.139), calls=%async_computation.5 | async-start | bytes 8388608 | tf_op jit(solution)/shard_map/all_to_all | solution.py:367
  313.2 2.0 fusion
  315.4 1.6 collective-permute-start.3
  317.2 2.1 copy.94
  319.3 1.5 fusion.7
  320.7 46.5 %collective-permute-done.2 = bf16[4,2,256,128]{3,2,0,1:T(8,128)(2,1)S(1)} collective-permute-done((bf16[4,2,256,128]{3,2,0,1:T(8,128)(2,1)S(1)}, bf16[4,2,256,128]{3,2,0,1:T(8,128)(2,1)S(1)}, u32[]{:S(2)}, u32[]{:S(2)}) %collective-permute-start.2) | collective-permute-done | bytes 524320 | tf_op jit(solution)/shard_map/ppermute | solution.py:39
  368.4 2.8 fusion.15
  371.2 2.3 fusion.4
  373.6 3.7 all-to-all-start.3
  377.3 4.5 %fusion.1 = f32[8,256,128]{2,0,1:T(8,128)S(1)} fusion(s32[64]{0:T(128)S(1)} %eq.64, bf16[8,8,256,128]{3,2,1,0:T(8,128)(2,1)} %bitcast.65), kind=kOutput, calls=%fused_computation.10 | convolution fusion | flops 33554944 | bytes 5243136 | tf_op jit(solution)/shard_map/dot_general | solution.py:377
  381.8 2.0 fusion.17
  384.4 2.1 copy.103
  386.4 6.8 %all-to-all-done.3 = bf16[2,1024,256]{2,0,1:T(2,128)(2,1)S(1)} async-done(((bf16[2,1024,256]{2,0,1:T(2,128)(2,1)}), bf16[2,1024,256]{2,0,1:T(2,128)(2,1)S(1)}, u32[]{:S(2)}, u32[]{:S(2)}) %all-to-all-start.3) | async-done | bytes 1048608 | tf_op jit(solution)/shard_map/all_to_all | solution.py:394
  393.2 3.5 all-to-all-start.6
  396.7 1.5 fusion.33
  401.4 10.6 %all-to-all-done.6 = bf16[2,1024,256]{2,0,1:T(2,128)(2,1)S(1)} async-done(((bf16[2,1024,256]{2,0,1:T(2,128)(2,1)}), bf16[2,1024,256]{2,0,1:T(2,128)(2,1)S(1)}, u32[]{:S(2)}, u32[]{:S(2)}) %all-to-all-start.6) | async-done | bytes 1048608 | tf_op jit(solution)/shard_map/all_to_all | solution.py:394
  (72 shorter events, 14.9 us)
Async XLA Ops:
  5.1 4.4 %copy-start.2 = (s32[8]{0:T(128)S(1)}, s32[8]{0:T(128)}, u32[]{:S(2)}) copy-start(s32[8]{0:T(128)} %count_ref.1) | copy-start | bytes 100
  5.1 4.4 %copy-start.8 = (s32[8,4]{0,1:T(4,128)S(1)}, s32[8,4]{0,1:T(4,128)}, u32[]{:S(2)}) copy-start(s32[8,4]{0,1:T(4,128)} %param.18) | copy-start | bytes 388
  5.1 4.6 %copy-start.7 = (s32[8,4]{0,1:T(4,128)S(1)}, s32[8,4]{0,1:T(4,128)}, u32[]{:S(2)}) copy-start(s32[8,4]{0,1:T(4,128)} %param.17) | copy-start | bytes 388
  5.1 30.8 %all-to-all-start = ((bf16[4,256,1024]{1,0,2:T(4,128)(2,1)}), bf16[4,256,1024]{1,0,2:T(4,128)(2,1)S(1)}, u32[]{:S(2)}, u32[]{:S(2)}) async-start(bf16[4,256,1024]{1,0,2:T(4,128)(2,1)} %copy.87), calls=%async_computation | async-start | bytes 4194304 | tf_op jit(solution)/shard_map/all_to_all | solution.py:275
  45.7 60.0 %all-to-all-start.2 = ((bf16[32,2,128,256]{3,2,1,0:T(8,128)(2,1)}), bf16[32,2,128,256]{3,2,1,0:T(8,128)(2,1)}, u32[]{:S(2)}, u32[]{:S(2)}) async-start(bf16[32,2,128,256]{3,2,1,0:T(8,128)(2,1)} %bitcast.129), calls=%async_computation.2 | async-start | bytes 8388608 | tf_op jit(solution)/shard_map/all_to_all | solution.py:328
  105.7 7.5 %copy-start.5 = (s32[4,8,16]{2,1,0:T(8,128)S(1)}, s32[4,8,16]{2,1,0:T(8,128)}, u32[]{:S(2)}) copy-start(s32[4,8,16]{2,1,0:T(8,128)} %param.21) | copy-start | bytes 6148
  105.7 63.1 %all-to-all-start.1 = ((bf16[32,2,128,256]{3,2,1,0:T(8,128)(2,1)}), bf16[32,2,128,256]{3,2,1,0:T(8,128)(2,1)}, u32[]{:S(2)}, u32[]{:S(2)}) async-start(bf16[32,2,128,256]{3,2,1,0:T(8,128)(2,1)} %bitcast.128), calls=%async_computation.1 | async-start | bytes 8388608 | tf_op jit(solution)/shard_map/all_to_all | solution.py:321
  113.1 2.5 copy-start.6
  113.8 53.4 %collective-permute-start = (bf16[4,2,128,256]{3,2,1,0:T(8,128)(2,1)S(1)}, bf16[4,2,128,256]{3,2,1,0:T(8,128)(2,1)S(1)}, u32[]{:S(2)}, u32[]{:S(2)}) collective-permute-start(bf16[4,2,128,256]{3,2,1,0:T(8,128)(2,1)S(1)} %get-tuple-element.66), channel_id=1, source_target_pairs={{0,4},{4,8},{8,12},{12,16},{16,20},{20,24},{24,28},{28,32},{32,36}... | collective-permute-start | bytes 1572872 | tf_op jit(solution)/shard_map/ppermute | solution.py:28
  114.0 53.2 %collective-permute-start.1 = (bf16[4,2,128,256]{3,2,1,0:T(8,128)(2,1)S(1)}, bf16[4,2,128,256]{3,2,1,0:T(8,128)(2,1)S(1)}, u32[]{:S(2)}, u32[]{:S(2)}) collective-permute-start(bf16[4,2,128,256]{3,2,1,0:T(8,128)(2,1)S(1)} %get-tuple-element.67), channel_id=1, source_target_pairs={{4,0},{8,4},{12,8},{16,12},{20,16},{24,20},{28,24},{32,28},{36,32}... | collective-permute-start | bytes 1572872 | tf_op jit(solution)/shard_map/ppermute | solution.py:31
  168.8 1.0 copy-start
  169.8 1.0 copy-start.1
  307.3 66.3 %all-to-all-start.5 = ((bf16[32,2,256,128]{3,2,1,0:T(8,128)(2,1)}), bf16[32,2,256,128]{3,2,1,0:T(8,128)(2,1)}, u32[]{:S(2)}, u32[]{:S(2)}) async-start(bf16[32,2,256,128]{3,2,1,0:T(8,128)(2,1)} %bitcast.139), calls=%async_computation.5 | async-start | bytes 8388608 | tf_op jit(solution)/shard_map/all_to_all | solution.py:367
  315.2 52.0 %collective-permute-start.2 = (bf16[4,2,256,128]{3,2,0,1:T(8,128)(2,1)S(1)}, bf16[4,2,256,128]{3,2,0,1:T(8,128)(2,1)S(1)}, u32[]{:S(2)}, u32[]{:S(2)}) collective-permute-start(bf16[4,2,256,128]{3,2,0,1:T(8,128)(2,1)S(1)} %get-tuple-element.57), channel_id=1, source_target_pairs={{124,0},{0,4},{4,8},{8,12},{12,16},{16,20},{20,24},{24,28},{28,32}... | collective-permute-start | bytes 1572872 | tf_op jit(solution)/shard_map/ppermute | solution.py:39
  315.4 53.0 %collective-permute-start.3 = (bf16[4,2,256,128]{3,2,0,1:T(8,128)(2,1)S(1)}, bf16[4,2,256,128]{3,2,0,1:T(8,128)(2,1)S(1)}, u32[]{:S(2)}, u32[]{:S(2)}) collective-permute-start(bf16[4,2,256,128]{3,2,0,1:T(8,128)(2,1)S(1)} %get-tuple-element.56), channel_id=1, source_target_pairs={{4,0},{8,4},{12,8},{16,12},{20,16},{24,20},{28,24},{32,28},{36,32}... | collective-permute-start | bytes 1572872 | tf_op jit(solution)/shard_map/ppermute | solution.py:39
  317.1 2.2 copy-start.3
  367.3 4.0 copy-start.4
  373.6 19.7 %all-to-all-start.3 = ((bf16[2,1024,256]{2,0,1:T(2,128)(2,1)}), bf16[2,1024,256]{2,0,1:T(2,128)(2,1)S(1)}, u32[]{:S(2)}, u32[]{:S(2)}) async-start(bf16[2,1024,256]{2,0,1:T(2,128)(2,1)} %copy.94), calls=%async_computation.3 | async-start | bytes 2097152 | tf_op jit(solution)/shard_map/all_to_all | solution.py:394
  393.2 18.8 %all-to-all-start.6 = ((bf16[2,1024,256]{2,0,1:T(2,128)(2,1)}), bf16[2,1024,256]{2,0,1:T(2,128)(2,1)S(1)}, u32[]{:S(2)}, u32[]{:S(2)}) async-start(bf16[2,1024,256]{2,0,1:T(2,128)(2,1)} %copy.103), calls=%async_computation.6 | async-start | bytes 2097152 | tf_op jit(solution)/shard_map/all_to_all | solution.py:394

commit v14 on v12

--- a/solution.py
+++ b/solution.py
@@ -69,7 +69,7 @@
 
 def attention_kernel(
     rows_ref, count_ref, seed_ref, q_ref, g_ref, kt_ref, vt_ref, kf_ref, vf_ref,
-    att_ref, qg_ref, nk_ref, nv_ref, fk_ref, fv_ref,
+    pair_out_ref, nk_ref, nv_ref, fk_ref, fv_ref,
     s_scr, keep_scr, drop_scr,
     *, scale, near_count, slot_count, blocks, head_size,
 ):
@@ -166,7 +166,7 @@
         )
     acc = [acc_both[a * BS : (a + 1) * BS] for a in range(pair)]
     attended = pick(acc, lane_head)
-    att_ref[...] = attended.astype(att_ref.dtype)
+    pair_out_ref[0] = attended.astype(pair_out_ref.dtype)
     spread = g.astype(f32) * attended
     delta = [
         jnp.sum(jnp.where(lane_head == a, spread, 0.0), axis=1, keepdims=True) for a in range(pair)
@@ -198,7 +198,7 @@
             fk_ref[at - near_count] = kp.astype(fk_ref.dtype)
             fv_ref[at - near_count] = vp.astype(fv_ref.dtype)
     qacc = [qacc_both[a * BS : (a + 1) * BS] for a in range(pair)]
-    qg_ref[...] = (pick(qacc, lane_head) * scale).astype(qg_ref.dtype)
+    pair_out_ref[1] = (pick(qacc, lane_head) * scale).astype(pair_out_ref.dtype)
 
 
 def block_attention(rows, counts, seeds, q, g, kt, vt, kf, vf, *, near_count, far_count, scale, head_size):
@@ -212,6 +212,7 @@
         blocks=blocks, head_size=head_size,
     )
     q_spec = pl.BlockSpec((BS, width), lambda p, c, *_: (c, p))
+    pair_spec = pl.BlockSpec((2, BS, width), lambda p, c, *_: (0, c, p))
     table_spec = pl.BlockSpec((kt.shape[0], width), lambda p, c, *_: (0, p))
     far_table_spec = pl.BlockSpec((kf.shape[0], width), lambda p, c, *_: (0, p))
     near_spec = pl.BlockSpec((near_count, width, BS), lambda p, c, *_: (0, p, 0))
@@ -220,7 +221,7 @@
         num_scalar_prefetch=3,
         grid=(groups, blocks),
         in_specs=[q_spec, q_spec, table_spec, table_spec, far_table_spec, far_table_spec],
-        out_specs=[q_spec, q_spec, near_spec, near_spec, far_spec, far_spec],
+        out_specs=[pair_spec, near_spec, near_spec, far_spec, far_spec],
         scratch_shapes=[
             pltpu.VMEM((2, slot_count, BS, BS), jnp.float32),
             pltpu.VMEM((2, slot_count, BS, BS), jnp.float32),
@@ -238,8 +239,7 @@
         kernel,
         grid_spec=grid_spec,
         out_shape=[
-            jax.ShapeDtypeStruct(q.shape, jnp.bfloat16),
-            jax.ShapeDtypeStruct(q.shape, jnp.bfloat16),
+            jax.ShapeDtypeStruct((2,) + q.shape, jnp.bfloat16),
             jax.ShapeDtypeStruct((near_count, local_width, BS), jnp.float32),
             jax.ShapeDtypeStruct((near_count, local_width, BS), jnp.float32),
             jax.ShapeDtypeStruct((far_count, local_width, BS), jnp.bfloat16),
@@ -345,7 +345,7 @@
     slot_rows = table_rows.reshape(-1).astype(jnp.int32)
     seed_flat = drop_seed.reshape(-1).astype(jnp.int32)
 
-    att_out, qg_out, nk, nv, fk, fv = block_attention(
+    pair_out, nk, nv, fk, fv = block_attention(
         slot_rows,
         live_count.astype(jnp.int32),
         seed_flat,
@@ -360,7 +360,6 @@
         scale=score_scale,
         head_size=head_size,
     )
-    outputs = (att_out, qg_out)
     column_shape = (peer_count, capacity, local_width, BS)
     back_key, back_value = (
         lax.all_to_all(fk.reshape(column_shape), "blk", split_axis=0, concat_axis=0, tiled=True),
@@ -393,10 +392,8 @@
     def to_rows(arrays):
         return lax.all_to_all(jnp.stack(arrays), "head", split_axis=1, concat_axis=2, tiled=True)
 
-    attended, query_grad = to_rows([
-        outputs[0].reshape(block_rows, local_width),
-        outputs[1].reshape(block_rows, local_width),
-    ])
+    pair_back = lax.all_to_all(pair_out, "head", split_axis=1, concat_axis=2, tiled=True)
+    attended, query_grad = pair_back[0], pair_back[1]
     key_grad, value_grad = to_rows([
         key_grad.reshape(block_rows, local_width),
         value_grad.reshape(block_rows, local_width),

time: 415 us -> 415 us (level)
    all_to_all x0 -> x1, waiting for transfers between devices: none -> 6.72 us  [on_device(): lax.all_to_all(pair_out, 'head', split_axis=1, concat_axis=2, tiled=True)]
    all_to_all x2 -> x1, waiting for transfers between devices: 17.3 us -> 10.6 us  [to_rows(): lax.all_to_all(jnp.stack(arrays), 'head', split_axis=1, concat_axis=2, ti...]
where the time goes in v14:
time: 415 us; the launch traced here: 414 us
  waiting for transfers between devices  162 us (39%)
  blocking collectives  83.9 us (20%)
  Pallas kernels  78.4 us (19%)
  starting transfers between devices  37.3 us (9%)
  local copies, waits for them, and re-layouts  29.5 us (7%)
  other arithmetic  12.5 us (3%)
  matrix products  9.39 us (2%)
    pallas_call x1, Pallas kernels, block_attention(): pl.pallas_call(kernel, grid_spec=grid_spec, out_shape=[jax.ShapeDtypeStru...  78.4 us
    all_to_all x1, blocking collectives, on_device(): lax.all_to_all(fk.reshape(column_shape), 'blk', split_axis=0, concat_axis...  58.4 us
    ppermute x1, waiting for transfers between devices, padded(): lax.ppermute(lax.slice_in_dim(block, block.shape[dim] - width, None, axis...  51.3 us
    all_to_all x1, waiting for transfers between devices, on_device(): lax.all_to_all(asked_of(value_blocks).reshape(reply_shape), 'blk', split_...  46.9 us
    ppermute x2, waiting for transfers between devices, shifted(): return lax.ppermute(block, axis, route)  46.6 us
    all_gather x1, blocking collectives, on_device(): lax.all_gather(jnp.stack([flat_device, asked_block.reshape(-1)]), 'blk',...  25.5 us
    unnamed x27, local copies, waits for them, and re-layouts  12.1 us
    all_to_all x1, waiting for transfers between devices, to_rows(): lax.all_to_all(jnp.stack(arrays), 'head', split_axis=1, concat_axis=2, ti...  10.6 us
  transfers between devices with their start and end apart: 10, of which 5 were waited for; matrix products, arithmetic and copies ran while one was open for 8% of the time, Pallas kernels for 0%

profile of v14, /device:TPU:8, one launch (start us, length us, event | category | flops | bytes accessed | tf_op | source)
XLA Modules:
  0.0 414.1 jit_solution(4497883973364099060)
XLA Ops:
  0.6 1.8 pad_maximum_fusion.1
  2.4 2.6 copy.87
  5.1 4.4 %all-to-all-start = ((bf16[4,256,1024]{1,0,2:T(4,128)(2,1)}), bf16[4,256,1024]{1,0,2:T(4,128)(2,1)S(1)}, u32[]{:S(2)}, u32[]{:S(2)}) async-start(bf16[4,256,1024]{1,0,2:T(4,128)(2,1)} %copy.87), calls=%async_computation | async-start | bytes 4194304 | tf_op jit(solution)/shard_map/all_to_all | solution.py:275
  9.8 25.5 %all-gather.1 = s32[32,2,32]{2,1,0:T(2,128)S(1)} all-gather(s32[1,2,32]{2,1,0:T(2,128)S(1)} %add_bitcast_fusion), channel_id=2, replica_groups=mesh['blk'=32,'head'=4] {'blk'}, dimensions={0}, use_global_device_ids=true | all-gather | bytes 8448 | tf_op jit(solution)/shard_map/all_gather | solution.py:291
  35.9 2.6 copy.88
  38.5 2.6 fusion.32
  41.4 1.3 convolution_convert_fusion
  42.7 3.1 copy.114
  45.8 8.5 %all-to-all-start.2 = ((bf16[32,2,128,256]{3,2,1,0:T(8,128)(2,1)}), bf16[32,2,128,256]{3,2,1,0:T(8,128)(2,1)}, u32[]{:S(2)}, u32[]{:S(2)}) async-start(bf16[32,2,128,256]{3,2,1,0:T(8,128)(2,1)} %bitcast.128), calls=%async_computation.2 | async-start | bytes 8388608 | tf_op jit(solution)/shard_map/all_to_all | solution.py:328
  55.8 3.0 copy.113
  58.9 46.9 %all-to-all-done.2 = bf16[32,2,128,256]{3,2,1,0:T(8,128)(2,1)} async-done(((bf16[32,2,128,256]{3,2,1,0:T(8,128)(2,1)}), bf16[32,2,128,256]{3,2,1,0:T(8,128)(2,1)}, u32[]{:S(2)}, u32[]{:S(2)}) %all-to-all-start.2) | async-done | bytes 4194336 | tf_op jit(solution)/shard_map/all_to_all | solution.py:328
  105.7 7.4 %all-to-all-start.1 = ((bf16[32,2,128,256]{3,2,1,0:T(8,128)(2,1)}), bf16[32,2,128,256]{3,2,1,0:T(8,128)(2,1)}, u32[]{:S(2)}, u32[]{:S(2)}) async-start(bf16[32,2,128,256]{3,2,1,0:T(8,128)(2,1)} %bitcast.127), calls=%async_computation.1 | async-start | bytes 8388608 | tf_op jit(solution)/shard_map/all_to_all | solution.py:321
  114.0 1.6 collective-permute-start.1
  115.9 51.3 %collective-permute-done = bf16[4,2,128,256]{3,2,0,1:T(8,128)(2,1)S(1)} collective-permute-done((bf16[4,2,128,256]{3,2,0,1:T(8,128)(2,1)S(1)}, bf16[4,2,128,256]{3,2,0,1:T(8,128)(2,1)S(1)}, u32[]{:S(2)}, u32[]{:S(2)}) %collective-permute-start) | collective-permute-done | bytes 524320 | tf_op jit(solution)/shard_map/ppermute | solution.py:28
  169.8 78.4 %shard_map.120 = (bf16[2,1024,256]{2,1,0:T(8,128)(2,1)S(1)}, f32[16,256,128]{2,1,0:T(8,128)}, f32[16,256,128]{2,1,0:T(8,128)}, bf16[64,256,128]{2,1,0:T(8,128)(2,1)}, bf16[64,256,128]{2,1,0:T(8,128)(2,1)}) custom-call(s32[128]{0:T(128)S(1)} %reshape.171.rows_ref, s32[8]{0:T(128)S(1)} %copy-done.2, s32[512]{0:T(512)S(1)} %reshape.172.seed_ref, ...), custom_call_target="tpu_custom_call" | custom-call | flops 12884901888 | bytes 25165824 | tf_op jit(solution)/shard_map/pallas_call | solution.py:238
  248.1 58.4 %all_to_all.65 = bf16[32,2,256,128]{3,2,1,0:T(8,128)(2,1)} all-to-all(bf16[32,2,256,128]{3,2,1,0:T(8,128)(2,1)} %bitcast.140), channel_id=1, replica_groups=mesh['blk'=32,'head'=4] {'blk'}, dimensions={0} | all-to-all | bytes 8388608 | tf_op jit(solution)/shard_map/all_to_all | solution.py:365
  306.5 6.0 %all-to-all-start.5 = ((bf16[32,2,256,128]{3,2,1,0:T(8,128)(2,1)}), bf16[32,2,256,128]{3,2,1,0:T(8,128)(2,1)}, u32[]{:S(2)}, u32[]{:S(2)}) async-start(bf16[32,2,256,128]{3,2,1,0:T(8,128)(2,1)} %bitcast.138), calls=%async_computation.5 | async-start | bytes 8388608 | tf_op jit(solution)/shard_map/all_to_all | solution.py:366
  312.6 2.0 fusion
  314.9 1.6 collective-permute-start.3
  316.5 2.1 copy.94
  318.5 1.5 fusion.7
  320.1 46.6 %collective-permute-done.2 = bf16[4,2,256,128]{3,2,0,1:T(8,128)(2,1)S(1)} collective-permute-done((bf16[4,2,256,128]{3,2,0,1:T(8,128)(2,1)S(1)}, bf16[4,2,256,128]{3,2,0,1:T(8,128)(2,1)S(1)}, u32[]{:S(2)}, u32[]{:S(2)}) %collective-permute-start.2) | collective-permute-done | bytes 524320 | tf_op jit(solution)/shard_map/ppermute | solution.py:39
  367.8 2.8 fusion.15
  370.6 2.3 fusion.4
  373.0 3.7 all-to-all-start.3
  376.7 4.5 %fusion.1 = f32[8,256,128]{2,0,1:T(8,128)S(1)} fusion(s32[64]{0:T(128)S(1)} %eq.64, bf16[8,8,256,128]{3,2,1,0:T(8,128)(2,1)} %bitcast.64), kind=kOutput, calls=%fused_computation.10 | convolution fusion | flops 33554944 | bytes 5243136 | tf_op jit(solution)/shard_map/dot_general | solution.py:376
  381.2 2.0 fusion.17
  383.8 2.1 copy.103
  385.9 6.7 %all-to-all-done.3 = bf16[2,1024,256]{2,0,1:T(2,128)(2,1)S(1)} async-done(((bf16[2,1024,256]{2,0,1:T(2,128)(2,1)}), bf16[2,1024,256]{2,0,1:T(2,128)(2,1)S(1)}, u32[]{:S(2)}, u32[]{:S(2)}) %all-to-all-start.3) | async-done | bytes 1048608 | tf_op jit(solution)/shard_map/all_to_all | solution.py:395
  392.6 3.5 all-to-all-start.6
  396.1 1.5 fusion.34
  400.8 10.6 %all-to-all-done.6 = bf16[2,1024,256]{2,0,1:T(2,128)(2,1)S(1)} async-done(((bf16[2,1024,256]{2,0,1:T(2,128)(2,1)}), bf16[2,1024,256]{2,0,1:T(2,128)(2,1)S(1)}, u32[]{:S(2)}, u32[]{:S(2)}) %all-to-all-start.6) | async-done | bytes 1048608 | tf_op jit(solution)/shard_map/all_to_all | solution.py:393
  (74 shorter events, 14.0 us)
Async XLA Ops:
  5.1 4.4 %copy-start.2 = (s32[8]{0:T(128)S(1)}, s32[8]{0:T(128)}, u32[]{:S(2)}) copy-start(s32[8]{0:T(128)} %count_ref.1) | copy-start | bytes 100
  5.1 4.4 %copy-start.9 = (s32[8,4]{0,1:T(4,128)S(1)}, s32[8,4]{0,1:T(4,128)}, u32[]{:S(2)}) copy-start(s32[8,4]{0,1:T(4,128)} %param.18) | copy-start | bytes 388
  5.1 4.6 %copy-start.8 = (s32[8,4]{0,1:T(4,128)S(1)}, s32[8,4]{0,1:T(4,128)}, u32[]{:S(2)}) copy-start(s32[8,4]{0,1:T(4,128)} %param.17) | copy-start | bytes 388
  5.1 30.8 %all-to-all-start = ((bf16[4,256,1024]{1,0,2:T(4,128)(2,1)}), bf16[4,256,1024]{1,0,2:T(4,128)(2,1)S(1)}, u32[]{:S(2)}, u32[]{:S(2)}) async-start(bf16[4,256,1024]{1,0,2:T(4,128)(2,1)} %copy.87), calls=%async_computation | async-start | bytes 4194304 | tf_op jit(solution)/shard_map/all_to_all | solution.py:275
  45.8 60.0 %all-to-all-start.2 = ((bf16[32,2,128,256]{3,2,1,0:T(8,128)(2,1)}), bf16[32,2,128,256]{3,2,1,0:T(8,128)(2,1)}, u32[]{:S(2)}, u32[]{:S(2)}) async-start(bf16[32,2,128,256]{3,2,1,0:T(8,128)(2,1)} %bitcast.128), calls=%async_computation.2 | async-start | bytes 8388608 | tf_op jit(solution)/shard_map/all_to_all | solution.py:328
  105.7 7.5 %copy-start.6 = (s32[4,8,16]{2,1,0:T(8,128)S(1)}, s32[4,8,16]{2,1,0:T(8,128)}, u32[]{:S(2)}) copy-start(s32[4,8,16]{2,1,0:T(8,128)} %param.21) | copy-start | bytes 6148
  105.7 61.9 %all-to-all-start.1 = ((bf16[32,2,128,256]{3,2,1,0:T(8,128)(2,1)}), bf16[32,2,128,256]{3,2,1,0:T(8,128)(2,1)}, u32[]{:S(2)}, u32[]{:S(2)}) async-start(bf16[32,2,128,256]{3,2,1,0:T(8,128)(2,1)} %bitcast.127), calls=%async_computation.1 | async-start | bytes 8388608 | tf_op jit(solution)/shard_map/all_to_all | solution.py:321
  113.2 2.5 copy-start.7
  113.8 53.4 %collective-permute-start = (bf16[4,2,128,256]{3,2,0,1:T(8,128)(2,1)S(1)}, bf16[4,2,128,256]{3,2,0,1:T(8,128)(2,1)S(1)}, u32[]{:S(2)}, u32[]{:S(2)}) collective-permute-start(bf16[4,2,128,256]{3,2,0,1:T(8,128)(2,1)S(1)} %get-tuple-element.66), channel_id=1, source_target_pairs={{0,4},{4,8},{8,12},{12,16},{16,20},{20,24},{24,28},{28,32},{32,36}... | collective-permute-start | bytes 1572872 | tf_op jit(solution)/shard_map/ppermute | solution.py:28
  114.0 53.2 %collective-permute-start.1 = (bf16[4,2,128,256]{3,2,0,1:T(8,128)(2,1)S(1)}, bf16[4,2,128,256]{3,2,0,1:T(8,128)(2,1)S(1)}, u32[]{:S(2)}, u32[]{:S(2)}) collective-permute-start(bf16[4,2,128,256]{3,2,0,1:T(8,128)(2,1)S(1)} %get-tuple-element.67), channel_id=1, source_target_pairs={{4,0},{8,4},{12,8},{16,12},{20,16},{24,20},{28,24},{32,28},{36,32}... | collective-permute-start | bytes 1572872 | tf_op jit(solution)/shard_map/ppermute | solution.py:31
  167.7 1.0 copy-start
  168.7 1.0 copy-start.1
  306.5 6.1 %copy-start.3 = (f32[16,256,128]{2,1,0:T(8,128)S(1)}, f32[16,256,128]{2,1,0:T(8,128)}, u32[]{:S(2)}) copy-start(f32[16,256,128]{2,1,0:T(8,128)} %get-tuple-element.34) | copy-start | bytes 6291460
  306.5 66.4 %all-to-all-start.5 = ((bf16[32,2,256,128]{3,2,1,0:T(8,128)(2,1)}), bf16[32,2,256,128]{3,2,1,0:T(8,128)(2,1)}, u32[]{:S(2)}, u32[]{:S(2)}) async-start(bf16[32,2,256,128]{3,2,1,0:T(8,128)(2,1)} %bitcast.138), calls=%async_computation.5 | async-start | bytes 8388608 | tf_op jit(solution)/shard_map/all_to_all | solution.py:366
  314.6 4.0 copy-start.4
  314.7 52.0 %collective-permute-start.2 = (bf16[4,2,256,128]{3,2,0,1:T(8,128)(2,1)S(1)}, bf16[4,2,256,128]{3,2,0,1:T(8,128)(2,1)S(1)}, u32[]{:S(2)}, u32[]{:S(2)}) collective-permute-start(bf16[4,2,256,128]{3,2,0,1:T(8,128)(2,1)S(1)} %get-tuple-element.55), channel_id=1, source_target_pairs={{124,0},{0,4},{4,8},{8,12},{12,16},{16,20},{20,24},{24,28},{28,32}... | collective-permute-start | bytes 1572872 | tf_op jit(solution)/shard_map/ppermute | solution.py:39
  314.9 53.0 %collective-permute-start.3 = (bf16[4,2,256,128]{3,2,0,1:T(8,128)(2,1)S(1)}, bf16[4,2,256,128]{3,2,0,1:T(8,128)(2,1)S(1)}, u32[]{:S(2)}, u32[]{:S(2)}) collective-permute-start(bf16[4,2,256,128]{3,2,0,1:T(8,128)(2,1)S(1)} %get-tuple-element.54), channel_id=1, source_target_pairs={{4,0},{8,4},{12,8},{16,12},{20,16},{24,20},{28,24},{32,28},{36,32}... | collective-permute-start | bytes 1572872 | tf_op jit(solution)/shard_map/ppermute | solution.py:39
  366.7 4.0 copy-start.5
  373.0 19.7 %all-to-all-start.3 = ((bf16[2,1024,256]{2,0,1:T(2,128)(2,1)}), bf16[2,1024,256]{2,0,1:T(2,128)(2,1)S(1)}, u32[]{:S(2)}, u32[]{:S(2)}) async-start(bf16[2,1024,256]{2,0,1:T(2,128)(2,1)} %copy.94), calls=%async_computation.3 | async-start | bytes 2097152 | tf_op jit(solution)/shard_map/all_to_all | solution.py:395
  392.6 18.8 %all-to-all-start.6 = ((bf16[2,1024,256]{2,0,1:T(2,128)(2,1)}), bf16[2,1024,256]{2,0,1:T(2,128)(2,1)S(1)}, u32[]{:S(2)}, u32[]{:S(2)}) async-start(bf16[2,1024,256]{2,0,1:T(2,128)(2,1)} %copy.103), calls=%async_computation.6 | async-start | bytes 2097152 | tf_op jit(solution)/shard_map/all_to_all | solution.py:393
